TPU v7x, 128 devices: a whole 4x4x4 slice. The times are simulated.
128 devices in a mesh: wave: 8 (over z, x_hi), angle: 16 (over x_lo, y, core).
Axes of the slice: x: 4 (x_hi: 2, x_lo: 2; x = x_hi * 2 + x_lo), y: 4, z: 4, core: 2. Of those that a mesh axis runs over, the one named last changes fastest.
Arguments:
- hologram_real: bfloat16 [32, 16, 512, 512], P('wave', 'angle'), may hold values from -6 to 6
- hologram_imaginary: bfloat16 [32, 16, 512, 512], P('wave', 'angle'), may hold values from -6 to 6
- pair_slot: int32 [2, 32], P(None, 'wave'), may hold values from 0 to 3
- kernel_real: bfloat16 [32, 2, 16, 128], replicated, may hold values from -0.1875 to 0.1875
- kernel_imaginary: bfloat16 [32, 2, 16, 128], replicated, may hold values from -0.1875 to 0.1875
Outputs:
- volume_real: float32 [512, 512, 128], P('angle', 'wave')
- volume_imaginary: float32 [512, 512, 128], P('angle', 'wave')
Inputs may be any that keep to these rules, and one draw needn't show every extreme that they name: pair_slot[s, w] is a slot of the wavelength group whose index differs from w's group in bit s; every group has 4 wavelengths.
All inputs are finite; a program needn't handle non-finite values.
Results may differ from a plain program's by a relative error of at most 0.0067.
Values may be sent and summed in bfloat16 or wider, within the bound.
No kernel may reach another device: no remote copies, remote signals or barrier semaphores. Data moves between devices by JAX's collectives and lax.ppermute only.
A program may use at most 128 MiB of HBM per device.

v0:
```python
import math

import jax
import jax.numpy as jnp
from jax import lax
from jax.sharding import PartitionSpec as P


def from_partner(block, axis, bit):
    count = lax.axis_size(axis)
    route = []
    for low in range(count):
        high = low | 1 << bit
        if high != low and high < count:
            route += [(low, high), (high, low)]
    return lax.ppermute(block, axis, route)


def dft_tables(length):
    counter = jnp.arange(length, dtype=jnp.int32)
    product = counter[:, None] * counter[None, :] % length
    phase = product.astype(jnp.float32) * (2.0 * math.pi / length)
    factor = 1.0 / math.sqrt(length)
    return (
        (jnp.cos(phase) * factor).astype(jnp.bfloat16),
        (-jnp.sin(phase) * factor).astype(jnp.bfloat16),
    )


def spectrum(field_real, field_imag, row_tables, col_tables):
    fp = jnp.float32
    half_real = (
        jnp.einsum("mrc,ck->mrk", field_real, col_tables[0], preferred_element_type=fp)
        - jnp.einsum("mrc,ck->mrk", field_imag, col_tables[1], preferred_element_type=fp)
    ).astype(jnp.bfloat16)
    half_imag = (
        jnp.einsum("mrc,ck->mrk", field_real, col_tables[1], preferred_element_type=fp)
        + jnp.einsum("mrc,ck->mrk", field_imag, col_tables[0], preferred_element_type=fp)
    ).astype(jnp.bfloat16)
    out_real = (
        jnp.einsum("rq,mqk->mrk", row_tables[0], half_real, preferred_element_type=fp)
        - jnp.einsum("rq,mqk->mrk", row_tables[1], half_imag, preferred_element_type=fp)
    ).astype(jnp.bfloat16)
    out_imag = (
        jnp.einsum("rq,mqk->mrk", row_tables[0], half_imag, preferred_element_type=fp)
        + jnp.einsum("rq,mqk->mrk", row_tables[1], half_real, preferred_element_type=fp)
    ).astype(jnp.bfloat16)
    return (out_real, out_imag)


def backproject(spec_real, spec_imag, weight_real, weight_imag):
    fp = jnp.float32
    part_real = jnp.einsum(
        "mrk,mz->rkz", spec_real, weight_real, preferred_element_type=fp
    ) - jnp.einsum("mrk,mz->rkz", spec_imag, weight_imag, preferred_element_type=fp)
    part_imag = jnp.einsum(
        "mrk,mz->rkz", spec_real, weight_imag, preferred_element_type=fp
    ) + jnp.einsum("mrk,mz->rkz", spec_imag, weight_real, preferred_element_type=fp)
    return (part_real, part_imag)


def shards(hologram_real, hologram_imaginary, pair_slot, kernel_real, kernel_imaginary):
    wave_devices = lax.axis_size("wave")
    angle_devices = lax.axis_size("angle")
    local_waves, local_angles, row_count, col_count = hologram_real.shape
    section_count = pair_slot.shape[0]
    depth_count = kernel_real.shape[3]
    row_tables = dft_tables(row_count)
    col_tables = dft_tables(col_count)
    own_real = hologram_real.astype(jnp.float32)
    own_imag = hologram_imaginary.astype(jnp.float32)
    synth_reals = []
    synth_imags = []
    for section_number in range(section_count):
        got_real, got_imag = from_partner(
            (hologram_real, hologram_imaginary), "wave", section_number
        )
        other_real = jnp.take(got_real, pair_slot[section_number], axis=0).astype(jnp.float32)
        other_imag = jnp.take(got_imag, pair_slot[section_number], axis=0).astype(jnp.float32)
        synth_reals.append((own_real * other_real + own_imag * other_imag).astype(jnp.bfloat16))
        synth_imags.append((own_imag * other_real - own_real * other_imag).astype(jnp.bfloat16))
    field_real = jnp.stack(synth_reals, axis=1).reshape(-1, row_count, col_count)
    field_imag = jnp.stack(synth_imags, axis=1).reshape(-1, row_count, col_count)
    spec_real, spec_imag = spectrum(field_real, field_imag, row_tables, col_tables)
    moved_real, moved_imag = (
        lax.all_to_all(spec_real, "angle", split_axis=1, concat_axis=0, tiled=True),
        lax.all_to_all(spec_imag, "angle", split_axis=1, concat_axis=0, tiled=True),
    )

    def all_weights(kernel_part):
        block = kernel_part.reshape(
            wave_devices, local_waves, section_count, angle_devices, local_angles, depth_count
        )
        return jnp.transpose(block, (0, 3, 1, 2, 4, 5)).reshape(-1, depth_count)

    column_real, column_imag = (
        lax.all_to_all(moved_real, "wave", split_axis=2, concat_axis=0, tiled=True),
        lax.all_to_all(moved_imag, "wave", split_axis=2, concat_axis=0, tiled=True),
    )
    volume_real, volume_imag = backproject(
        column_real, column_imag, all_weights(kernel_real), all_weights(kernel_imaginary)
    )
    return (volume_real, volume_imag)


def solution(mesh):
    return jax.shard_map(
        shards,
        mesh=mesh,
        in_specs=(
            P("wave", "angle", None, None),
            P("wave", "angle", None, None),
            P(None, "wave"),
            P(),
            P(),
        ),
        out_specs=(P("angle", "wave", None), P("angle", "wave", None)),
        check_vma=False,
    )
```

profile of v0, /device:TPU:24, one launch (start us, length us, event | category | flops | bytes accessed | tf_op | source)
XLA Modules:
  0.0 453.2 jit_solution(16638440102249064862)
XLA Ops:
  0.6 2.0 collective-permute-start.2
  2.6 0.1 collective-permute-start.3
  2.7 3.0 collective-permute-start
  5.8 0.5 collective-permute-start.1
  6.3 0.8 compare_and_fusion.1
  7.0 42.4 %collective-permute-done.2 = bf16[4,1,512,512]{3,2,1,0:T(8,128)(2,1)S(1)} collective-permute-done((bf16[4,1,512,512]{3,2,1,0:T(8,128)(2,1)}, bf16[4,1,512,512]{3,2,1,0:T(8,128)(2,1)S(1)}, u32[]{:S(2)}, u32[]{:S(2)}) %collective-permute-start.2) | collective-permute-done | bytes 2097184 | tf_op jit(solution)/shard_map/ppermute | solution.py:16
  49.4 1.3 copy-done.11
  50.8 2.3 gather_fusion.2
  53.0 40.5 %collective-permute-done.3 = bf16[4,1,512,512]{3,2,1,0:T(8,128)(2,1)} collective-permute-done((bf16[4,1,512,512]{3,2,1,0:T(8,128)(2,1)}, bf16[4,1,512,512]{3,2,1,0:T(8,128)(2,1)}, u32[]{:S(2)}, u32[]{:S(2)}) %collective-permute-start.3) | collective-permute-done | bytes 2097184 | tf_op jit(solution)/shard_map/ppermute | solution.py:16
  93.5 3.6 gather_fusion.3
  97.1 0.0 collective-permute-done
  97.1 3.7 gather_fusion
  100.8 0.0 collective-permute-done.1
  100.8 3.6 gather_fusion.1
  104.4 0.0 copy-start.9
  104.4 5.9 %fusion.14 = bf16[4,1,1,512,512]{4,3,0,2,1:T(8,128)(2,1)} fusion(bf16[4,1,512,512]{3,2,1,0:T(8,128)(2,1)} %param.8, bf16[4,1,512,512]{3,2,1,0:T(8,128)(2,1)} %param.7, bf16[4,512,512]{2,1,0:T(8,128)(2,1)S(1)} %gather_fusion.2, pred[4]{0:T(512)(128)(4,1)S(1)} %get-tuple-element.10, bf16[4,512,512]{2,1,0:T(8,128)(2,1)} %gather_fusion.3), kind=kLoop, calls=%fused_computation.33 | loop fusion | flops 10485760 | bytes 10485764 | tf_op jit(solution)/shard_map/stack | solution.py:83
  110.3 0.0 copy-done.5
  110.3 0.0 copy-done.6
  110.3 0.0 copy-done.7
  110.3 0.0 copy-done.8
  110.3 0.8 copy-done.9
  111.1 3.1 fusion.15
  114.2 0.4 pad_maximum_fusion
  114.6 0.3 copy.72
  114.9 10.7 %fusion.26 = f32[8,512,512]{2,1,0:T(8,128)S(1)} fusion(bf16[8,512,512]{2,1,0:T(8,128)(2,1)S(1)} %bitcast.155), kind=kOutput, calls=%fused_computation.54 | convolution fusion | flops 2151940096 | bytes 12582912 | tf_op jit(solution)/shard_map/mrc,ck->mrk/dot_general | solution.py:37
  125.6 0.0 copy-start.10
  125.6 10.7 %fusion.34 = f32[8,512,512]{2,1,0:T(8,128)S(1)} fusion(bf16[8,512,512]{2,1,0:T(8,128)(2,1)S(1)} %bitcast.156), kind=kOutput, calls=%fused_computation.57 | convolution fusion | flops 2151677952 | bytes 12582912 | tf_op jit(solution)/shard_map/mrc,ck->mrk/dot_general | solution.py:33
  136.3 0.0 copy-done.10
  136.3 0.4 pad_maximum_fusion.1
  136.7 0.3 copy.76
  136.9 8.8 %add_convert_fusion.1 = bf16[8,512,512]{2,1,0:T(8,128)(2,1)S(1)} fusion(f32[8,512,512]{2,1,0:T(8,128)S(1)} %fusion.26, bf16[8,512,512]{2,1,0:T(8,128)(2,1)S(1)} %bitcast.157), kind=kOutput, calls=%fused_computation.6 | convolution fusion | flops 2155872256 | bytes 16777216 | tf_op jit(solution)/shard_map/mrc,ck->mrk/dot_general | solution.py:38
  145.8 0.0 copy-start
  145.8 9.1 %subtract_convert_fusion.1 = bf16[8,512,512]{2,1,0:T(8,128)(2,1)S(1)} fusion(f32[8,512,512]{2,1,0:T(8,128)S(1)} %fusion.34, bf16[8,512,512]{2,1,0:T(8,128)(2,1)S(1)} %bitcast.158), kind=kOutput, calls=%fused_computation.7 | convolution fusion | flops 2156134400 | bytes 16777216 | tf_op jit(solution)/shard_map/mrc,ck->mrk/dot_general | solution.py:34
  154.9 12.6 %fusion.32 = f32[8,512,512]{2,1,0:T(8,128)S(1)} fusion(bf16[8,512,512]{2,1,0:T(8,128)(2,1)S(1)} %subtract_convert_fusion.1), kind=kOutput, calls=%fused_computation.56 | convolution fusion | flops 2151677952 | bytes 12582912 | tf_op jit(solution)/shard_map/rq,mqk->mrk/dot_general | solution.py:41
  167.5 0.0 copy-done
  167.5 7.8 %fusion.10 = bf16[8,512,512]{1,2,0:T(8,128)(2,1)} fusion(f32[8,512,512]{2,1,0:T(8,128)S(1)} %fusion.32, bf16[8,512,512]{2,1,0:T(8,128)(2,1)S(1)} %add_convert_fusion.1), kind=kOutput, calls=%fused_computation.27 | convolution fusion | flops 2156134400 | bytes 16777216 | tf_op jit(solution)/shard_map/rq,mqk->mrk/dot_general | solution.py:42
  175.2 8.0 %copy.79 = bf16[8,512,512]{2,0,1:T(8,128)(2,1)} copy(bf16[8,512,512]{1,2,0:T(8,128)(2,1)} %fusion.10) | data formatting | bytes 8388608 | tf_op jit(solution)/shard_map/convert_element_type | solution.py:43
  183.3 6.2 %all-to-all-start = ((bf16[8,512,512]{2,0,1:T(8,128)(2,1)}), bf16[8,512,512]{2,0,1:T(8,128)(2,1)}, u32[]{:S(2)}, u32[]{:S(2)}) async-start(bf16[8,512,512]{2,0,1:T(8,128)(2,1)} %copy.79), calls=%async_computation | async-start | bytes 8388608 | tf_op jit(solution)/shard_map/all_to_all | solution.py:86
  189.5 0.0 copy-start.2
  189.5 7.6 %fusion.29 = f32[8,512,512]{2,1,0:T(8,128)S(1)} fusion(bf16[8,512,512]{2,1,0:T(8,128)(2,1)} %copy-done), kind=kOutput, calls=%fused_computation.55 | convolution fusion | flops 2151677952 | bytes 12582912 | tf_op jit(solution)/shard_map/rq,mqk->mrk/dot_general | solution.py:45
  197.2 7.7 %fusion.11 = bf16[8,512,512]{1,2,0:T(8,128)(2,1)} fusion(f32[8,512,512]{2,1,0:T(8,128)S(1)} %fusion.29, bf16[8,512,512]{2,1,0:T(8,128)(2,1)S(1)} %copy-done.2), kind=kOutput, calls=%fused_computation.28 | convolution fusion | flops 2156134400 | bytes 16777216 | tf_op jit(solution)/shard_map/rq,mqk->mrk/dot_general | solution.py:46
  204.9 8.0 %copy.88 = bf16[8,512,512]{2,0,1:T(8,128)(2,1)} copy(bf16[8,512,512]{1,2,0:T(8,128)(2,1)} %fusion.11) | data formatting | bytes 8388608 | tf_op jit(solution)/shard_map/convert_element_type | solution.py:47
  213.0 37.9 %all-to-all-done = bf16[8,512,512]{2,0,1:T(8,128)(2,1)} async-done(((bf16[8,512,512]{2,0,1:T(8,128)(2,1)}), bf16[8,512,512]{2,0,1:T(8,128)(2,1)}, u32[]{:S(2)}, u32[]{:S(2)}) %all-to-all-start) | async-done | bytes 4194336 | tf_op jit(solution)/shard_map/all_to_all | solution.py:86
  250.9 5.6 %all-to-all-start.2 = ((bf16[8,512,512]{2,0,1:T(8,128)(2,1)}), bf16[8,512,512]{2,0,1:T(8,128)(2,1)}, u32[]{:S(2)}, u32[]{:S(2)}) async-start(bf16[8,512,512]{2,0,1:T(8,128)(2,1)} %copy.88), calls=%async_computation.2 | async-start | bytes 8388608 | tf_op jit(solution)/shard_map/all_to_all | solution.py:87
  256.5 6.0 %copy.81 = bf16[16,8,32,512]{3,2,1,0:T(8,128)(2,1)} copy(bf16[16,8,32,512]{3,1,2,0:T(8,128)(2,1)} %bitcast.27) | data formatting | bytes 8388608 | tf_op jit(solution)/shard_map/all_to_all | solution.py:86
  262.5 9.1 %copy.82 = bf16[128,32,512]{0,1,2:T(8,128)(2,1)} copy(bf16[128,32,512]{2,1,0:T(8,128)(2,1)} %bitcast.159) | data formatting | bytes 8388608 | tf_op jit(solution)/shard_map/all_to_all | solution.py:86
  271.6 46.4 %all-to-all-done.2 = bf16[8,512,512]{2,0,1:T(8,128)(2,1)} async-done(((bf16[8,512,512]{2,0,1:T(8,128)(2,1)}), bf16[8,512,512]{2,0,1:T(8,128)(2,1)}, u32[]{:S(2)}, u32[]{:S(2)}) %all-to-all-start.2) | async-done | bytes 4194336 | tf_op jit(solution)/shard_map/all_to_all | solution.py:87
  318.0 7.3 %all-to-all-start.1 = ((bf16[128,32,512]{0,1,2:T(8,128)(2,1)}), bf16[128,32,512]{0,1,2:T(8,128)(2,1)}, u32[]{:S(2)}, u32[]{:S(2)}) async-start(bf16[128,32,512]{0,1,2:T(8,128)(2,1)} %copy.82), calls=%async_computation.1 | async-start | bytes 8388608 | tf_op jit(solution)/shard_map/all_to_all | solution.py:97
  325.3 5.9 %copy.90 = bf16[16,8,32,512]{3,2,1,0:T(8,128)(2,1)} copy(bf16[16,8,32,512]{3,1,2,0:T(8,128)(2,1)} %bitcast.39) | data formatting | bytes 8388608 | tf_op jit(solution)/shard_map/all_to_all | solution.py:87
  331.2 9.1 %copy.91 = bf16[128,32,512]{0,1,2:T(8,128)(2,1)} copy(bf16[128,32,512]{2,1,0:T(8,128)(2,1)} %bitcast.160) | data formatting | bytes 8388608 | tf_op jit(solution)/shard_map/all_to_all | solution.py:87
  340.3 36.5 %all-to-all-done.1 = bf16[128,32,512]{0,1,2:T(8,128)(2,1)} async-done(((bf16[128,32,512]{0,1,2:T(8,128)(2,1)}), bf16[128,32,512]{0,1,2:T(8,128)(2,1)}, u32[]{:S(2)}, u32[]{:S(2)}) %all-to-all-start.1) | async-done | bytes 4194336 | tf_op jit(solution)/shard_map/all_to_all | solution.py:97
  376.8 4.6 %all-to-all-start.3 = ((bf16[128,32,512]{0,1,2:T(8,128)(2,1)}), bf16[128,32,512]{0,1,2:T(8,128)(2,1)}, u32[]{:S(2)}, u32[]{:S(2)}) async-start(bf16[128,32,512]{0,1,2:T(8,128)(2,1)} %copy.91), calls=%async_computation.3 | async-start | bytes 8388608 | tf_op jit(solution)/shard_map/all_to_all | solution.py:98
  381.5 0.2 copy.85
  381.7 0.2 copy.94
  381.9 6.8 %copy.84 = bf16[8,128,32,64]{1,0,3,2:T(8,128)(2,1)} copy(bf16[8,128,32,64]{1,2,3,0:T(8,128)(2,1)} %bitcast.31) | data formatting | bytes 8388608 | tf_op jit(solution)/shard_map/all_to_all | solution.py:97
  388.7 7.4 %all_to_all.59 = bf16[1024,32,64]{0,2,1:T(8,128)(2,1)} reshape(bf16[8,128,32,64]{1,0,3,2:T(8,128)(2,1)} %copy.84) | data formatting | bytes 8388608 | tf_op jit(solution)/shard_map/all_to_all | solution.py:97
  396.1 3.6 fusion.77
  399.7 0.0 copy-done.4
  399.7 1.3 fusion.76
  401.0 31.0 %all-to-all-done.3 = bf16[128,32,512]{0,1,2:T(8,128)(2,1)} async-done(((bf16[128,32,512]{0,1,2:T(8,128)(2,1)}), bf16[128,32,512]{0,1,2:T(8,128)(2,1)}, u32[]{:S(2)}, u32[]{:S(2)}) %all-to-all-start.3) | async-done | bytes 4194336 | tf_op jit(solution)/shard_map/all_to_all | solution.py:98
  432.0 6.8 %copy.93 = bf16[8,128,32,64]{1,0,3,2:T(8,128)(2,1)} copy(bf16[8,128,32,64]{1,2,3,0:T(8,128)(2,1)} %bitcast.43) | data formatting | bytes 8388608 | tf_op jit(solution)/shard_map/all_to_all | solution.py:98
  438.8 7.4 %all_to_all.67 = bf16[1024,32,64]{0,2,1:T(8,128)(2,1)} reshape(bf16[8,128,32,64]{1,0,3,2:T(8,128)(2,1)} %copy.93) | data formatting | bytes 8388608 | tf_op jit(solution)/shard_map/all_to_all | solution.py:98
  446.2 4.6 %convolution_add_fusion = f32[32,64,128]{2,1,0:T(8,128)} fusion(f32[32,64,128]{2,1,0:T(8,128)S(1)} %fusion.77, bf16[1024,32,64]{0,2,1:T(8,128)(2,1)} %all_to_all.67, bf16[1024,128,1]{1,0,2:T(8,128)(2,1)S(1)} %bitcast.164), kind=kOutput, calls=%fused_computation.42 | convolution fusion | flops 537133056 | bytes 6553600 | tf_op jit(solution)/shard_map/mrk,mz->rkz/dot_general | solution.py:58
  450.8 2.3 convolution_subtract_fusion
  (16 shorter events, 0.0 us)
Async XLA Ops:
  0.6 48.8 %collective-permute-start.2 = (bf16[4,1,512,512]{3,2,1,0:T(8,128)(2,1)}, bf16[4,1,512,512]{3,2,1,0:T(8,128)(2,1)S(1)}, u32[]{:S(2)}, u32[]{:S(2)}) collective-permute-start(bf16[4,1,512,512]{3,2,1,0:T(8,128)(2,1)} %param.7), channel_id=1, source_target_pairs={{0,32},{32,0},{16,48},{48,16},{64,96},{96,64},{80,112},{112,80},{1... | collective-permute-start | bytes 6291464 | tf_op jit(solution)/shard_map/ppermute | solution.py:16
  2.6 90.9 %collective-permute-start.3 = (bf16[4,1,512,512]{3,2,1,0:T(8,128)(2,1)}, bf16[4,1,512,512]{3,2,1,0:T(8,128)(2,1)}, u32[]{:S(2)}, u32[]{:S(2)}) collective-permute-start(bf16[4,1,512,512]{3,2,1,0:T(8,128)(2,1)} %param.8), channel_id=1, source_target_pairs={{0,32},{32,0},{16,48},{48,16},{64,96},{96,64},{80,112},{112,80},{1... | collective-permute-start | bytes 6291464 | tf_op jit(solution)/shard_map/ppermute | solution.py:16
  2.7 94.4 %collective-permute-start = (bf16[4,1,512,512]{3,2,1,0:T(8,128)(2,1)}, bf16[4,1,512,512]{3,2,1,0:T(8,128)(2,1)}, u32[]{:S(2)}, u32[]{:S(2)}) collective-permute-start(bf16[4,1,512,512]{3,2,1,0:T(8,128)(2,1)} %param.7), channel_id=1, source_target_pairs={{0,16},{16,0},{32,48},{48,32},{64,80},{80,64},{96,112},{112,96},{1... | collective-permute-start | bytes 6291464 | tf_op jit(solution)/shard_map/ppermute | solution.py:16
  5.8 95.1 %collective-permute-start.1 = (bf16[4,1,512,512]{3,2,1,0:T(8,128)(2,1)}, bf16[4,1,512,512]{3,2,1,0:T(8,128)(2,1)}, u32[]{:S(2)}, u32[]{:S(2)}) collective-permute-start(bf16[4,1,512,512]{3,2,1,0:T(8,128)(2,1)} %param.8), channel_id=1, source_target_pairs={{0,16},{16,0},{32,48},{48,32},{64,80},{80,64},{96,112},{112,96},{1... | collective-permute-start | bytes 6291464 | tf_op jit(solution)/shard_map/ppermute | solution.py:16
  49.4 1.4 copy-start.11
  104.4 5.9 %copy-start.5 = (bf16[4,512,512]{2,1,0:T(8,128)(2,1)S(1)}, bf16[4,512,512]{2,1,0:T(8,128)(2,1)}, u32[]{:S(2)}) copy-start(bf16[4,512,512]{2,1,0:T(8,128)(2,1)} %gather_fusion.3) | copy-start | bytes 6291460
  104.4 5.9 %copy-start.6 = (bf16[4,512,512]{2,1,0:T(8,128)(2,1)S(1)}, bf16[4,512,512]{2,1,0:T(8,128)(2,1)}, u32[]{:S(2)}) copy-start(bf16[4,512,512]{2,1,0:T(8,128)(2,1)} %gather_fusion) | copy-start | bytes 6291460
  104.4 5.9 %copy-start.7 = (bf16[4,512,512]{2,1,0:T(8,128)(2,1)S(1)}, bf16[4,512,512]{2,1,0:T(8,128)(2,1)}, u32[]{:S(2)}) copy-start(bf16[4,512,512]{2,1,0:T(8,128)(2,1)} %gather_fusion.1) | copy-start | bytes 6291460
  104.4 5.9 %copy-start.8 = (bf16[4,1,512,512]{3,2,1,0:T(8,128)(2,1)S(1)}, bf16[4,1,512,512]{3,2,1,0:T(8,128)(2,1)}, u32[]{:S(2)}) copy-start(bf16[4,1,512,512]{3,2,1,0:T(8,128)(2,1)} %param.8) | copy-start | bytes 6291460
  104.4 6.7 %copy-start.9 = (bf16[4,1,512,512]{3,2,1,0:T(8,128)(2,1)S(1)}, bf16[4,1,512,512]{3,2,1,0:T(8,128)(2,1)}, u32[]{:S(2)}) copy-start(bf16[4,1,512,512]{3,2,1,0:T(8,128)(2,1)} %param.7) | copy-start | bytes 6291460
  125.6 10.7 %copy-start.10 = (bf16[4,1,1,512,512]{4,3,0,2,1:T(8,128)(2,1)S(1)}, bf16[4,1,1,512,512]{4,3,0,2,1:T(8,128)(2,1)}, u32[]{:S(2)}) copy-start(bf16[4,1,1,512,512]{4,3,0,2,1:T(8,128)(2,1)} %fusion.14) | copy-start | bytes 6291460
  145.8 21.7 %copy-start = (bf16[8,512,512]{2,1,0:T(8,128)(2,1)}, bf16[8,512,512]{2,1,0:T(8,128)(2,1)S(1)}, u32[]{:S(2)}) copy-start(bf16[8,512,512]{2,1,0:T(8,128)(2,1)S(1)} %add_convert_fusion.1) | copy-start | bytes 12582916
  154.9 12.6 %copy-start.1 = (bf16[8,512,512]{2,1,0:T(8,128)(2,1)}, bf16[8,512,512]{2,1,0:T(8,128)(2,1)S(1)}, u32[]{:S(2)}) copy-start(bf16[8,512,512]{2,1,0:T(8,128)(2,1)S(1)} %subtract_convert_fusion.1) | copy-start | bytes 12582916
  183.3 67.6 %all-to-all-start = ((bf16[8,512,512]{2,0,1:T(8,128)(2,1)}), bf16[8,512,512]{2,0,1:T(8,128)(2,1)}, u32[]{:S(2)}, u32[]{:S(2)}) async-start(bf16[8,512,512]{2,0,1:T(8,128)(2,1)} %copy.79), calls=%async_computation | async-start | bytes 8388608 | tf_op jit(solution)/shard_map/all_to_all | solution.py:86
  189.5 7.7 %copy-start.2 = (bf16[8,512,512]{2,1,0:T(8,128)(2,1)S(1)}, bf16[8,512,512]{2,1,0:T(8,128)(2,1)}, u32[]{:S(2)}) copy-start(bf16[8,512,512]{2,1,0:T(8,128)(2,1)} %copy-done.1) | copy-start | bytes 12582916
  250.9 67.1 %all-to-all-start.2 = ((bf16[8,512,512]{2,0,1:T(8,128)(2,1)}), bf16[8,512,512]{2,0,1:T(8,128)(2,1)}, u32[]{:S(2)}, u32[]{:S(2)}) async-start(bf16[8,512,512]{2,0,1:T(8,128)(2,1)} %copy.88), calls=%async_computation.2 | async-start | bytes 8388608 | tf_op jit(solution)/shard_map/all_to_all | solution.py:87
  318.0 58.8 %all-to-all-start.1 = ((bf16[128,32,512]{0,1,2:T(8,128)(2,1)}), bf16[128,32,512]{0,1,2:T(8,128)(2,1)}, u32[]{:S(2)}, u32[]{:S(2)}) async-start(bf16[128,32,512]{0,1,2:T(8,128)(2,1)} %copy.82), calls=%async_computation.1 | async-start | bytes 8388608 | tf_op jit(solution)/shard_map/all_to_all | solution.py:97
  340.3 41.2 %copy-start.12 = (bf16[32,2,16,128]{3,2,1,0:T(8,128)(2,1)S(1)}, bf16[32,2,16,128]{3,2,1,0:T(8,128)(2,1)}, u32[]{:S(2)}) copy-start(bf16[32,2,16,128]{3,2,1,0:T(8,128)(2,1)} %param.10) | copy-start | bytes 786436
  340.3 41.4 %copy-start.13 = (bf16[32,2,16,128]{3,2,1,0:T(8,128)(2,1)S(1)}, bf16[32,2,16,128]{3,2,1,0:T(8,128)(2,1)}, u32[]{:S(2)}) copy-start(bf16[32,2,16,128]{3,2,1,0:T(8,128)(2,1)} %param.11) | copy-start | bytes 786436
  376.8 55.2 %all-to-all-start.3 = ((bf16[128,32,512]{0,1,2:T(8,128)(2,1)}), bf16[128,32,512]{0,1,2:T(8,128)(2,1)}, u32[]{:S(2)}, u32[]{:S(2)}) async-start(bf16[128,32,512]{0,1,2:T(8,128)(2,1)} %copy.91), calls=%async_computation.3 | async-start | bytes 8388608 | tf_op jit(solution)/shard_map/all_to_all | solution.py:98
  396.1 3.6 copy-start.4
  446.2 4.6 %copy-start.3 = (bf16[1024,32,64]{0,2,1:T(8,128)(2,1)S(1)}, bf16[1024,32,64]{0,2,1:T(8,128)(2,1)}, u32[]{:S(2)}) copy-start(bf16[1024,32,64]{0,2,1:T(8,128)(2,1)} %all_to_all.67) | copy-start | bytes 12582916
where the time goes:
time: 458 us; the launch traced here: 453 us
  waiting for transfers between devices  235 us (51%)
  local copies, waits for them, and re-layouts  90.8 us (20%)
  matrix products  86.7 us (19%)
  starting transfers between devices  29.4 us (6%)
  other arithmetic  10.5 us (2%)
    ppermute x4, waiting for transfers between devices, from_partner(): return lax.ppermute(block, axis, route)  82.9 us
    all_to_all x1, waiting for transfers between devices, shards(): lax.all_to_all(spec_imag, 'angle', split_axis=1, concat_axis=0, tiled=True)  46.4 us
    all_to_all x1, waiting for transfers between devices, shards(): lax.all_to_all(spec_real, 'angle', split_axis=1, concat_axis=0, tiled=True)  37.9 us
    all_to_all x1, waiting for transfers between devices, shards(): lax.all_to_all(moved_real, 'wave', split_axis=2, concat_axis=0, tiled=True)  36.5 us
    all_to_all x1, waiting for transfers between devices, shards(): lax.all_to_all(moved_imag, 'wave', split_axis=2, concat_axis=0, tiled=True)  31 us
    all_to_all x2, local copies, waits for them, and re-layouts, shards(): lax.all_to_all(spec_real, 'angle', split_axis=1, concat_axis=0, tiled=True)  15.1 us
    all_to_all x2, local copies, waits for them, and re-layouts, shards(): lax.all_to_all(spec_imag, 'angle', split_axis=1, concat_axis=0, tiled=True)  15 us
    all_to_all x2, local copies, waits for them, and re-layouts, shards(): lax.all_to_all(moved_imag, 'wave', split_axis=2, concat_axis=0, tiled=True)  14.2 us
  transfers between devices with their start and end apart: 8, of which 6 were waited for; matrix products, arithmetic and copies ran while one was open for 17% of the time, Pallas kernels for 0%

commit v1 on v0

v1 whole, which is shorter than its diff:
```python
import math

import jax
import jax.numpy as jnp
from jax import lax
from jax.sharding import PartitionSpec as P


def from_partner(block, axis, bit):
    count = lax.axis_size(axis)
    route = []
    for low in range(count):
        high = low | 1 << bit
        if high != low and high < count:
            route += [(low, high), (high, low)]
    return lax.ppermute(block, axis, route)


def dft_tables(length):
    counter = jnp.arange(length, dtype=jnp.int32)
    product = counter[:, None] * counter[None, :] % length
    phase = product.astype(jnp.float32) * (2.0 * math.pi / length)
    factor = 1.0 / math.sqrt(length)
    return (
        (jnp.cos(phase) * factor).astype(jnp.bfloat16),
        (-jnp.sin(phase) * factor).astype(jnp.bfloat16),
    )


def complex_block(table_real, table_imag):
    top = jnp.stack([table_real, table_imag], axis=1)
    bottom = jnp.stack([-table_imag, table_real], axis=1)
    return jnp.stack([top, bottom], axis=0)


def shards(hologram_real, hologram_imaginary, pair_slot, kernel_real, kernel_imaginary):
    fp = jnp.float32
    wave_devices = lax.axis_size("wave")
    angle_devices = lax.axis_size("angle")
    local_waves, local_angles, row_count, col_count = hologram_real.shape
    section_count = pair_slot.shape[0]
    depth_count = kernel_real.shape[3]
    row_real, row_imag = dft_tables(row_count)
    col_real, col_imag = dft_tables(col_count)
    own_real = hologram_real[:, 0].astype(fp)
    own_imag = hologram_imaginary[:, 0].astype(fp)
    synth = []
    for section_number in range(section_count):
        got_real, got_imag = from_partner(
            (hologram_real, hologram_imaginary), "wave", section_number
        )
        other_real = jnp.take(got_real[:, 0], pair_slot[section_number], axis=0).astype(fp)
        other_imag = jnp.take(got_imag[:, 0], pair_slot[section_number], axis=0).astype(fp)
        synth_real = (own_real * other_real + own_imag * other_imag).astype(jnp.bfloat16)
        synth_imag = (own_imag * other_real - own_real * other_imag).astype(jnp.bfloat16)
        synth.append(jnp.stack([synth_real, synth_imag], axis=2))
    field = jnp.stack(synth, axis=1).reshape(-1, row_count, 2, col_count)
    col_block = complex_block(col_real, col_imag)
    half = jnp.einsum(
        "mqpc,pcdk->mqdk", field, col_block, preferred_element_type=fp
    ).astype(jnp.bfloat16)
    row_block = jnp.transpose(complex_block(row_real, row_imag), (2, 3, 0, 1))
    spec = jnp.einsum(
        "erdq,mqdk->rmek", row_block, half, preferred_element_type=fp
    ).astype(jnp.bfloat16)
    field_count = spec.shape[1]
    rows_per = row_count // angle_devices
    cols_per = col_count // wave_devices
    send = spec.reshape(angle_devices, rows_per, field_count, 2, wave_devices, cols_per)
    send = jnp.transpose(send, (4, 0, 1, 2, 3, 5)).reshape(
        wave_devices * angle_devices, rows_per, field_count, 2, cols_per
    )
    got = lax.all_to_all(send, ("wave", "angle"), 0, 0, tiled=True)

    def all_weights(kernel_part):
        block = kernel_part.reshape(
            wave_devices, local_waves, section_count, angle_devices, depth_count
        )
        return jnp.transpose(block, (0, 3, 1, 2, 4)).reshape(
            wave_devices * angle_devices, local_waves * section_count, depth_count
        )

    weight = complex_block(all_weights(kernel_real), all_weights(kernel_imaginary))
    volume = jnp.einsum("srmck,csdmz->rkdz", got, weight, preferred_element_type=fp)
    return (volume[:, :, 0, :], volume[:, :, 1, :])


def solution(mesh):
    return jax.shard_map(
        shards,
        mesh=mesh,
        in_specs=(
            P("wave", "angle", None, None),
            P("wave", "angle", None, None),
            P(None, "wave"),
            P(),
            P(),
        ),
        out_specs=(P("angle", "wave", None), P("angle", "wave", None)),
        check_vma=False,
    )
```

time: 458 us -> 392 us (0.86)
  the two profiles are of different devices: /device:TPU:24 before, /device:TPU:15 now
where the time goes in v1:
time: 392 us; the launch traced here: 385 us
  waiting for transfers between devices  172 us (44%)
  local copies, waits for them, and re-layouts  131 us (33%)
  matrix products  42.8 us (11%)
  other arithmetic  21.2 us (5%)
  starting transfers between devices  16.4 us (4%)
    all_to_all x1, waiting for transfers between devices, shards(): got = lax.all_to_all(send, ('wave', 'angle'), 0, 0, tiled=True)  98.7 us
    ppermute x4, waiting for transfers between devices, from_partner(): return lax.ppermute(block, axis, route)  73.5 us
    unnamed x10, local copies, waits for them, and re-layouts  56.2 us
    dot_general x1, matrix products, shards(): jnp.einsum('erdq,mqdk->rmek', row_block, half, preferred_element_type=fp)  22.2 us
    reshape x1, local copies, waits for them, and re-layouts, shards(): spec.reshape(angle_devices, rows_per, field_count, 2, wave_devices, cols_...  21.2 us
    dot_general x1, matrix products, shards(): jnp.einsum('srmck,csdmz->rkdz', got, weight, preferred_element_type=fp)  20.6 us
    transpose x1, local copies, waits for them, and re-layouts, shards(): jnp.transpose(send, (4, 0, 1, 2, 3, 5))  15.1 us
    convert_element_type x1, local copies, waits for them, and re-layouts, shards(): spec = jnp.einsum('erdq,mqdk->rmek', row_block, half, preferred_element_t...  14.9 us
  transfers between devices with their start and end apart: 5, of which 3 were waited for; matrix products, arithmetic and copies ran while one was open for 5% of the time, Pallas kernels for 0%

profile of v1, /device:TPU:15, one launch (start us, length us, event | category | flops | bytes accessed | tf_op | source)
XLA Modules:
  0.0 384.9 jit_solution(12440900041964245359)
XLA Ops:
  0.6 1.7 collective-permute-start.2
  2.3 0.1 collective-permute-start.3
  2.4 1.1 collective-permute-start.1
  3.6 1.8 collective-permute-start
  5.4 0.8 compare_and_fusion.1
  6.2 4.0 %fusion.32 = bf16[512,1,512]{2,0,1:T(8,128)(2,1)S(1)} fusion(), kind=kLoop, calls=%fused_computation.61 | loop fusion | flops 5242880 | bytes 524288 | tf_op jit(solution)/shard_map/neg | solution.py:32
  10.2 4.4 %multiply_convert_fusion = (bf16[512,1,512]{2,0,1:T(8,128)(2,1)S(1)}, bf16[512,1,512]{2,0,1:T(8,128)(2,1)S(1)}) fusion(), kind=kLoop, calls=%fused_computation.54 | loop fusion | flops 4980736 | bytes 1048576 | tf_op jit(solution)/shard_map/convert_element_type | solution.py:26
  14.6 1.2 maximum_bitcast_fusion.2
  15.7 32.2 %collective-permute-done.2 = bf16[4,1,512,512]{3,2,1,0:T(8,128)(2,1)S(1)} collective-permute-done((bf16[4,1,512,512]{3,2,1,0:T(8,128)(2,1)}, bf16[4,1,512,512]{3,2,1,0:T(8,128)(2,1)S(1)}, u32[]{:S(2)}, u32[]{:S(2)}) %collective-permute-start.2) | collective-permute-done | bytes 2097184 | tf_op jit(solution)/shard_map/ppermute | solution.py:16
  47.9 0.0 copy-start
  47.9 1.4 copy-done
  49.3 2.3 gather_fusion.2
  51.5 41.3 %collective-permute-done.3 = bf16[4,1,512,512]{3,2,1,0:T(8,128)(2,1)} collective-permute-done((bf16[4,1,512,512]{3,2,1,0:T(8,128)(2,1)}, bf16[4,1,512,512]{3,2,1,0:T(8,128)(2,1)}, u32[]{:S(2)}, u32[]{:S(2)}) %collective-permute-start.3) | collective-permute-done | bytes 2097184 | tf_op jit(solution)/shard_map/ppermute | solution.py:16
  92.8 3.6 gather_fusion.3
  96.5 0.0 collective-permute-done.1
  96.5 3.6 gather_fusion.1
  100.1 0.0 collective-permute-done
  100.1 3.6 gather_fusion
  103.7 6.0 %fusion.17 = (bf16[4,512,1,512]{3,1,0,2:T(8,128)(2,1)S(1)}, bf16[4,512,1,512]{3,1,0,2:T(8,128)(2,1)S(1)}, bf16[4,512,1,512]{3,1,2,0:T(8,128)(2,1)S(1)}, bf16[4,512,1,512]{3,1,2,0:T(8,128)(2,1)S(1)}) fusion(bf16[4,1,512,512]{3,2,1,0:T(8,128)(2,1)} %param.8, bf16[4,1,512,512]{3,2,1,0:T(8,128)(2,1)} %param.7, bf16[4,512,512]{2,1,0:T(8,128)(2,1)} %gather_fusion, ...), kind=kLoop, calls=%fused_computation.32 | loop fusion | flops 27262976 | bytes 20971528 | tf_op jit(solution)/shard_map/stack | solution.py:56
  109.7 0.4 maximum_bitcast_fusion.1
  110.1 0.0 copy-start.1
  110.1 3.6 pad_maximum_fusion
  113.7 0.0 copy-done.1
  113.7 22.2 %fusion.3 = bf16[512,8,2,512]{0,3,2,1:T(8,128)(2,1)} fusion(bf16[8,512,2,512,1]{3,1,2,4,0:T(8,128)(2,1)} %bitcast.122, bf16[1,512,2,512]{3,1,0,2:T(8,128)(2,1)S(1)} %copy-done.1, bf16[1,512,2,512]{3,1,0,2:T(8,128)(2,1)S(1)} %get-tuple-element.15), kind=kOutput, calls=%fused_computation.18 | convolution fusion | flops 17196646400 | bytes 18874368 | tf_op jit(solution)/shard_map/erdq,mqdk->rmek/dot_general | solution.py:63
  135.9 14.9 %copy.31 = bf16[512,8,2,512]{3,1,2,0:T(8,128)(2,1)} copy(bf16[512,8,2,512]{0,3,2,1:T(8,128)(2,1)} %fusion.3) | data formatting | bytes 16777216 | tf_op jit(solution)/shard_map/convert_element_type | solution.py:65
  150.8 21.2 %reshape.130 = bf16[16,32,8,2,8,64]{5,4,2,3,1,0:T(8,128)(2,1)} reshape(bf16[512,8,2,512]{3,1,2,0:T(8,128)(2,1)} %copy.31) | data formatting | bytes 16777216 | tf_op jit(solution)/shard_map/reshape | solution.py:69
  172.0 15.1 %copy.32 = bf16[8,16,32,8,2,64]{5,3,4,2,1,0:T(8,128)(2,1)} copy(bf16[8,16,32,8,2,64]{5,0,3,4,2,1:T(8,128)(2,1)} %bitcast.120) | data formatting | bytes 16777216 | tf_op jit(solution)/shard_map/transpose | solution.py:70
  187.1 27.2 %reshape.189 = bf16[128,2,16384]{2,1,0:T(2,128)(2,1)} reshape(bf16[128,32,2,8,64]{4,3,2,1,0:T(8,128)(2,1)} %bitcast.121) | data formatting | bytes 16777216
  214.3 0.0 copy-start.2
  214.3 0.0 copy-start.3
  214.3 11.6 %all-to-all-start = ((bf16[128,2,16384]{2,1,0:T(2,128)(2,1)}), bf16[128,2,16384]{2,1,0:T(2,128)(2,1)}, u32[]{:S(2)}, u32[]{:S(2)}) async-start(bf16[128,2,16384]{2,1,0:T(2,128)(2,1)} %reshape.189), calls=%async_computation | async-start | bytes 16777216 | tf_op jit(solution)/shard_map/all_to_all | solution.py:73
  225.9 0.0 copy-done.2
  226.0 0.1 neg.40
  226.0 0.0 copy-done.3
  226.1 0.9 maximum_bitcast_fusion.6
  226.9 98.7 %all-to-all-done = bf16[128,2,16384]{2,1,0:T(2,128)(2,1)} async-done(((bf16[128,2,16384]{2,1,0:T(2,128)(2,1)}), bf16[128,2,16384]{2,1,0:T(2,128)(2,1)}, u32[]{:S(2)}, u32[]{:S(2)}) %all-to-all-start) | async-done | bytes 8388640 | tf_op jit(solution)/shard_map/all_to_all | solution.py:73
  325.6 27.7 %reshape.190 = bf16[128,32,2,8,64]{4,3,2,1,0:T(8,128)(2,1)} reshape(bf16[128,2,16384]{2,1,0:T(2,128)(2,1)} %all-to-all-done) | data formatting | bytes 16777216
  353.3 9.2 %bitcast_bitcast_fusion = bf16[128,32,8,2,64,1]{4,2,3,1,0,5:T(8,128)(2,1)S(1)} fusion(bf16[128,32,2,8,64]{4,3,2,1,0:T(8,128)(2,1)} %reshape.190), kind=kLoop, calls=%fused_computation.70 | loop fusion | bytes 16777216 | tf_op jit(solution)/shard_map/all_to_all | solution.py:73
  362.4 20.6 %fusion.21 = f32[32,64,2,128]{3,1,2,0:T(8,128)S(1)} fusion(bf16[128,32,8,2,64,1]{4,2,3,1,0,5:T(8,128)(2,1)S(1)} %bitcast_bitcast_fusion, bf16[1,128,2,8,128]{4,1,3,0,2:T(8,128)(2,1)} %get-tuple-element.18, bf16[1,128,2,8,128]{4,1,3,0,2:T(8,128)(2,1)S(1)} %get-tuple-element.17), kind=kOutput, calls=%fused_computation.40 | convolution fusion | flops 2149580800 | bytes 11534336 | tf_op jit(solution)/shard_map/srmck,csdmz->rkdz/dot_general | solution.py:84
  383.0 1.5 slice_bitcast_fusion
  (3 shorter events, 0.0 us)
Async XLA Ops:
  0.6 47.3 %collective-permute-start.2 = (bf16[4,1,512,512]{3,2,1,0:T(8,128)(2,1)}, bf16[4,1,512,512]{3,2,1,0:T(8,128)(2,1)S(1)}, u32[]{:S(2)}, u32[]{:S(2)}) collective-permute-start(bf16[4,1,512,512]{3,2,1,0:T(8,128)(2,1)} %param.7), channel_id=1, source_target_pairs={{0,32},{32,0},{16,48},{48,16},{64,96},{96,64},{80,112},{112,80},{1... | collective-permute-start | bytes 6291464 | tf_op jit(solution)/shard_map/ppermute | solution.py:16
  2.3 90.5 %collective-permute-start.3 = (bf16[4,1,512,512]{3,2,1,0:T(8,128)(2,1)}, bf16[4,1,512,512]{3,2,1,0:T(8,128)(2,1)}, u32[]{:S(2)}, u32[]{:S(2)}) collective-permute-start(bf16[4,1,512,512]{3,2,1,0:T(8,128)(2,1)} %param.8), channel_id=1, source_target_pairs={{0,32},{32,0},{16,48},{48,16},{64,96},{96,64},{80,112},{112,80},{1... | collective-permute-start | bytes 6291464 | tf_op jit(solution)/shard_map/ppermute | solution.py:16
  2.4 94.0 %collective-permute-start.1 = (bf16[4,1,512,512]{3,2,1,0:T(8,128)(2,1)}, bf16[4,1,512,512]{3,2,1,0:T(8,128)(2,1)}, u32[]{:S(2)}, u32[]{:S(2)}) collective-permute-start(bf16[4,1,512,512]{3,2,1,0:T(8,128)(2,1)} %param.8), channel_id=1, source_target_pairs={{0,16},{16,0},{32,48},{48,32},{64,80},{80,64},{96,112},{112,96},{1... | collective-permute-start | bytes 6291464 | tf_op jit(solution)/shard_map/ppermute | solution.py:16
  3.6 96.5 %collective-permute-start = (bf16[4,1,512,512]{3,2,1,0:T(8,128)(2,1)}, bf16[4,1,512,512]{3,2,1,0:T(8,128)(2,1)}, u32[]{:S(2)}, u32[]{:S(2)}) collective-permute-start(bf16[4,1,512,512]{3,2,1,0:T(8,128)(2,1)} %param.7), channel_id=1, source_target_pairs={{0,16},{16,0},{32,48},{48,32},{64,80},{80,64},{96,112},{112,96},{1... | collective-permute-start | bytes 6291464 | tf_op jit(solution)/shard_map/ppermute | solution.py:16
  47.9 1.4 copy-start
  110.1 3.6 copy-start.1
  214.3 11.6 %copy-start.2 = (bf16[32,2,16,128]{3,2,1,0:T(8,128)(2,1)S(1)}, bf16[32,2,16,128]{3,2,1,0:T(8,128)(2,1)}, u32[]{:S(2)}) copy-start(bf16[32,2,16,128]{3,2,1,0:T(8,128)(2,1)} %param.11) | copy-start | bytes 786436
  214.3 11.7 %copy-start.3 = (bf16[32,2,16,128]{3,2,1,0:T(8,128)(2,1)S(1)}, bf16[32,2,16,128]{3,2,1,0:T(8,128)(2,1)}, u32[]{:S(2)}) copy-start(bf16[32,2,16,128]{3,2,1,0:T(8,128)(2,1)} %param.10) | copy-start | bytes 786436
  214.3 111.3 %all-to-all-start = ((bf16[128,2,16384]{2,1,0:T(2,128)(2,1)}), bf16[128,2,16384]{2,1,0:T(2,128)(2,1)}, u32[]{:S(2)}, u32[]{:S(2)}) async-start(bf16[128,2,16384]{2,1,0:T(2,128)(2,1)} %reshape.189), calls=%async_computation | async-start | bytes 16777216 | tf_op jit(solution)/shard_map/all_to_all | solution.py:73

commit v2 on v1

v2 whole, which is shorter than its diff:
```python
import functools
import math

import jax
import jax.numpy as jnp
from jax import lax
from jax.experimental import pallas as pl
from jax.experimental.pallas import tpu as pltpu
from jax.sharding import PartitionSpec as P


def from_partner(block, axis, bit):
    count = lax.axis_size(axis)
    route = []
    for low in range(count):
        high = low | 1 << bit
        if high != low and high < count:
            route += [(low, high), (high, low)]
    return lax.ppermute(block, axis, route)


def dft_tables(length):
    counter = jnp.arange(length, dtype=jnp.int32)
    product = counter[:, None] * counter[None, :] % length
    phase = product.astype(jnp.float32) * (2.0 * math.pi / length)
    factor = 1.0 / math.sqrt(length)
    return (
        (jnp.cos(phase) * factor).astype(jnp.bfloat16),
        (-jnp.sin(phase) * factor).astype(jnp.bfloat16),
    )


def column_tables(table_real, table_imag, blocks):
    rows = table_real.shape[0]
    er = table_real.reshape(rows, blocks, 1, -1)
    ei = table_imag.reshape(rows, blocks, 1, -1)

    def join(top, bottom):
        upper = jnp.concatenate(top, axis=2).reshape(rows, -1)
        lower = jnp.concatenate(bottom, axis=2).reshape(rows, -1)
        return jnp.concatenate([upper, lower], axis=0)

    first = join([er, ei], [-ei, er])
    second = join([-ei, er], [-er, -ei])
    return first, second


def spectrum_kernel(
    slot_ref, own_re, own_im, far_re, far_im, col_a, col_b, row_re, row_im, *rest
):
    out_ref = rest[-1]
    fp = jnp.float32
    bf = jnp.bfloat16
    a_re = own_re[0, 0].astype(fp)
    a_im = own_im[0, 0].astype(fp)
    b_re = far_re[0, 0].astype(fp)
    b_im = far_im[0, 0].astype(fp)
    z_re = (a_re * b_re + a_im * b_im).astype(bf)
    z_im = (a_im * b_re - a_re * b_im).astype(bf)
    n = z_re.shape[1]
    y_a = (
        jnp.dot(z_re, col_a[:n, :], preferred_element_type=fp)
        + jnp.dot(z_im, col_a[n:, :], preferred_element_type=fp)
    ).astype(bf)
    y_b = (
        jnp.dot(z_re, col_b[:n, :], preferred_element_type=fp)
        + jnp.dot(z_im, col_b[n:, :], preferred_element_type=fp)
    ).astype(bf)
    spec = (
        jnp.dot(row_re[...], y_a, preferred_element_type=fp)
        + jnp.dot(row_im[...], y_b, preferred_element_type=fp)
    ).astype(bf)
    blocks, groups, _, rows_per, lanes = out_ref.shape
    for block in range(blocks):
        out_ref[block, :, 0, :, :] = spec[:, block * lanes : (block + 1) * lanes].reshape(
            groups, rows_per, lanes
        )


def spectra(slots, own_re, own_im, far_re, far_im, col_a, col_b, row_re, row_im, blocks, groups, after):
    waves, _, rows, cols = own_re.shape
    lanes = 2 * cols // blocks
    rows_per = rows // groups
    field = pl.BlockSpec((1, 1, rows, cols), lambda i, sl: (i, 0, 0, 0))
    partner = pl.BlockSpec((1, 1, rows, cols), lambda i, sl: (sl[i], 0, 0, 0))
    whole_col = pl.BlockSpec((2 * cols, 2 * cols), lambda i, sl: (0, 0))
    whole_row = pl.BlockSpec((rows, rows), lambda i, sl: (0, 0))
    flops = waves * (2 * 2 * rows * (2 * cols) * (2 * cols) + 2 * 2 * rows * rows * (2 * cols))
    return pl.pallas_call(
        spectrum_kernel,
        out_shape=jax.ShapeDtypeStruct((blocks, groups, waves, rows_per, lanes), jnp.bfloat16),
        grid_spec=pltpu.PrefetchScalarGridSpec(
            num_scalar_prefetch=1,
            grid=(waves,),
            in_specs=[field, field, partner, partner, whole_col, whole_col, whole_row, whole_row]
            + [pl.BlockSpec(memory_space=pl.ANY)] * len(after),
            out_specs=pl.BlockSpec(
                (blocks, groups, 1, rows_per, lanes), lambda i, sl: (0, 0, i, 0, 0)
            ),
        ),
        compiler_params=pltpu.CompilerParams(vmem_limit_bytes=60 * 1024 * 1024),
        cost_estimate=pl.CostEstimate(
            flops=flops, transcendentals=0, bytes_accessed=waves * rows * cols * 12 + 12 * cols * cols
        ),
    )(slots, own_re, own_im, far_re, far_im, col_a, col_b, row_re, row_im, *after)


def shards(hologram_real, hologram_imaginary, pair_slot, kernel_real, kernel_imaginary):
    fp = jnp.float32
    wave_devices = lax.axis_size("wave")
    angle_devices = lax.axis_size("angle")
    local_waves, local_angles, row_count, col_count = hologram_real.shape
    section_count = pair_slot.shape[0]
    depth_count = kernel_real.shape[3]
    row_real, row_imag = dft_tables(row_count)
    col_real, col_imag = dft_tables(col_count)
    col_a, col_b = column_tables(col_real, col_imag, wave_devices)

    def all_weights(kernel_part):
        block = kernel_part.reshape(
            wave_devices, local_waves, section_count, angle_devices, depth_count
        )
        return jnp.transpose(block, (2, 0, 3, 1, 4)).reshape(
            section_count, wave_devices * angle_devices, local_waves, depth_count
        )

    k_re = all_weights(kernel_real)
    k_im = all_weights(kernel_imaginary)
    volume = None
    received = [
        from_partner((hologram_real, hologram_imaginary), "wave", section_number)
        for section_number in range(section_count)
    ]
    for section_number in range(section_count):
        got_real, got_imag = received[section_number]
        after = [a for other, got in enumerate(received) if other != section_number for a in got]
        send = spectra(
            pair_slot[section_number],
            hologram_real,
            hologram_imaginary,
            got_real,
            got_imag,
            col_a,
            col_b,
            row_real,
            row_imag,
            wave_devices,
            angle_devices,
            after,
        )
        send = send.reshape(wave_devices * angle_devices, *send.shape[2:])
        got = lax.all_to_all(send, ("wave", "angle"), 0, 0, tiled=True)
        kr = k_re[section_number]
        ki = k_im[section_number]
        w_first = jnp.stack([kr, ki], axis=2).reshape(kr.shape[0], kr.shape[1], -1)
        w_second = jnp.stack([-ki, kr], axis=2).reshape(kr.shape[0], kr.shape[1], -1)
        t_first = jnp.einsum("swrn,swx->rnx", got, w_first, preferred_element_type=fp)
        t_second = jnp.einsum("swrn,swx->rnx", got, w_second, preferred_element_type=fp)
        half = got.shape[3] // 2
        part = t_first[:, :half] + t_second[:, half:]
        volume = part if volume is None else volume + part
    volume = volume.reshape(volume.shape[0], volume.shape[1], 2, depth_count)
    return (volume[:, :, 0, :], volume[:, :, 1, :])


def solution(mesh):
    return jax.shard_map(
        shards,
        mesh=mesh,
        in_specs=(
            P("wave", "angle", None, None),
            P("wave", "angle", None, None),
            P(None, "wave"),
            P(),
            P(),
        ),
        out_specs=(P("angle", "wave", None), P("angle", "wave", None)),
        check_vma=False,
    )
```

time: 392 us -> 271 us (0.69)
  the two profiles are of different devices: /device:TPU:15 before, /device:TPU:24 now
where the time goes in v2:
time: 271 us; the launch traced here: 267 us
  waiting for transfers between devices  121 us (45%)
  local copies, waits for them, and re-layouts  48.5 us (18%)
  Pallas kernels  38 us (14%)
  starting transfers between devices  23.8 us (9%)
  other arithmetic  21 us (8%)
  matrix products  13.6 us (5%)
    ppermute x4, waiting for transfers between devices, from_partner(): return lax.ppermute(block, axis, route)  66.2 us
    all_to_all x2, waiting for transfers between devices, shards(): got = lax.all_to_all(send, ('wave', 'angle'), 0, 0, tiled=True)  54.5 us
    pallas_call x2, Pallas kernels, spectra(): pl.pallas_call(spectrum_kernel, out_shape=jax.ShapeDtypeStruct((blocks, g...  38 us
    all_to_all x2, starting transfers between devices, shards(): got = lax.all_to_all(send, ('wave', 'angle'), 0, 0, tiled=True)  18.2 us
    reshape x2, local copies, waits for them, and re-layouts, shards(): send = send.reshape(wave_devices * angle_devices, *send.shape[2:])  16.8 us
    all_to_all x2, local copies, waits for them, and re-layouts, shards(): got = lax.all_to_all(send, ('wave', 'angle'), 0, 0, tiled=True)  16 us
    convert_element_type x2, other arithmetic, dft_tables(): (-jnp.sin(phase) * factor).astype(jnp.bfloat16)  10.2 us
    dot_general x2, matrix products, shards(): jnp.einsum('swrn,swx->rnx', got, w_second, preferred_element_type=fp)  9.12 us
  transfers between devices with their start and end apart: 6, of which 6 were waited for; matrix products, arithmetic and copies ran while one was open for 19% of the time, Pallas kernels for 7%

profile of v2, /device:TPU:24, one launch (start us, length us, event | category | flops | bytes accessed | tf_op | source)
XLA Modules:
  0.0 266.6 jit_solution(4028229499059161125)
XLA Ops:
  0.6 2.0 collective-permute-start.2
  2.6 3.0 %collective-permute-start = (bf16[4,1,512,512]{3,2,1,0:T(8,128)(2,1)}, bf16[4,1,512,512]{3,2,1,0:T(8,128)(2,1)}, u32[]{:S(2)}, u32[]{:S(2)}) collective-permute-start(bf16[4,1,512,512]{3,2,1,0:T(8,128)(2,1)} %own_re.3), channel_id=1, source_target_pairs={{0,16},{16,0},{32,48},{48,32},{64,80},{80,64},{96,112},{112,96},{1... | collective-permute-start | bytes 6291464 | tf_op jit(solution)/shard_map/ppermute | solution.py:19
  5.7 0.1 collective-permute-start.3
  5.8 0.5 collective-permute-start.1
  6.3 4.9 %multiply_convert_fusion.2 = (bf16[512,8,1,64]{0,3,2,1:T(8,128)(2,1)S(1)}, bf16[512,8,1,64]{0,3,2,1:T(8,128)(2,1)S(1)}) fusion(s32[8,64]{1,0:T(8,128)S(1)} %multiply_add_fusion), kind=kLoop, calls=%fused_computation.28 | loop fusion | flops 4980736 | bytes 1050624 | tf_op jit(solution)/shard_map/convert_element_type | solution.py:29
  11.2 4.9 %fusion.13 = (bf16[512,8,1,64]{0,3,2,1:T(8,128)(2,1)S(1)}, bf16[512,8,1,64]{0,3,2,1:T(8,128)(2,1)S(1)}) fusion(s32[8,64]{1,0:T(8,128)S(1)} %multiply_add_fusion), kind=kLoop, calls=%fused_computation.38 | loop fusion | flops 6553600 | bytes 1050624 | tf_op jit(solution)/shard_map/neg | solution.py:44
  16.1 1.2 pad_maximum_fusion.4
  17.3 0.5 copy.46
  17.8 1.5 copy.44
  19.3 1.3 copy.43
  20.6 0.0 copy-start.6
  20.6 5.3 %multiply_convert_fusion = (bf16[512,512]{1,0:T(8,128)(2,1)}, bf16[512,512]{1,0:T(8,128)(2,1)}) fusion(), kind=kLoop, calls=%fused_computation.24 | loop fusion | flops 4980736 | bytes 1048576 | tf_op jit(solution)/shard_map/convert_element_type | solution.py:29
  25.9 3.7 %pad_maximum_fusion.1 = (bf16[1024,1024]{1,0:T(8,128)(2,1)}, bf16[1024,1024]{1,0:T(8,128)(2,1)}) fusion(bf16[512,1024]{1,0:T(8,128)(2,1)S(1)} %copy.46, bf16[512,1024]{1,0:T(8,128)(2,1)S(1)} %copy.44, bf16[512,1024]{1,0:T(8,128)(2,1)} %copy.43), kind=kLoop, calls=%fused_computation.8 | loop fusion | flops 8388608 | bytes 7340032 | tf_op jit(solution)/shard_map/concatenate | solution.py:41
  29.7 0.0 copy-done.6
  29.7 0.6 slice_bitcast_fusion.1
  30.3 19.2 %collective-permute-done.2.rest_0_.far_re = bf16[4,1,512,512]{3,2,1,0:T(8,128)(2,1)} collective-permute-done((bf16[4,1,512,512]{3,2,1,0:T(8,128)(2,1)}, bf16[4,1,512,512]{3,2,1,0:T(8,128)(2,1)}, u32[]{:S(2)}, u32[]{:S(2)}) %collective-permute-start.2) | collective-permute-done | bytes 2097184 | tf_op jit(solution)/shard_map/ppermute | solution.py:19
  49.5 3.5 %collective-permute-done.far_re.rest_0_ = bf16[4,1,512,512]{3,2,1,0:T(8,128)(2,1)} collective-permute-done((bf16[4,1,512,512]{3,2,1,0:T(8,128)(2,1)}, bf16[4,1,512,512]{3,2,1,0:T(8,128)(2,1)}, u32[]{:S(2)}, u32[]{:S(2)}) %collective-permute-start) | collective-permute-done | bytes 2097184 | tf_op jit(solution)/shard_map/ppermute | solution.py:19
  53.0 40.5 %collective-permute-done.3.rest_1_.far_im = bf16[4,1,512,512]{3,2,1,0:T(8,128)(2,1)} collective-permute-done((bf16[4,1,512,512]{3,2,1,0:T(8,128)(2,1)}, bf16[4,1,512,512]{3,2,1,0:T(8,128)(2,1)}, u32[]{:S(2)}, u32[]{:S(2)}) %collective-permute-start.3) | collective-permute-done | bytes 2097184 | tf_op jit(solution)/shard_map/ppermute | solution.py:19
  93.5 3.0 %collective-permute-done.1.far_im.rest_1_ = bf16[4,1,512,512]{3,2,1,0:T(8,128)(2,1)} collective-permute-done((bf16[4,1,512,512]{3,2,1,0:T(8,128)(2,1)}, bf16[4,1,512,512]{3,2,1,0:T(8,128)(2,1)}, u32[]{:S(2)}, u32[]{:S(2)}) %collective-permute-start.1) | collective-permute-done | bytes 2097184 | tf_op jit(solution)/shard_map/ppermute | solution.py:19
  96.5 19.0 %shard_map.68 = bf16[8,16,4,32,128]{4,3,2,1,0:T(8,128)(2,1)} custom-call(s32[4]{0:T(128)} %get-tuple-element.21.slot_ref, bf16[4,1,512,512]{3,2,1,0:T(8,128)(2,1)} %own_re.3, bf16[4,1,512,512]{3,2,1,0:T(8,128)(2,1)} %own_im.3, bf16[4,1,512,512]{3,2,1,0:T(8,128)(2,1)} %collective-permute-done.far_re.rest_0_, ...), custom_call_target="tpu_custom_call" | custom-call | flops 12884901888 | bytes 15728640 | tf_op jit(solution)/shard_map/pallas_call | solution.py:89
  115.5 8.4 %copy.47 = bf16[128,4,32,128]{3,1,2,0:T(4,128)(2,1)} copy(bf16[128,4,32,128]{3,2,1,0:T(8,128)(2,1)} %bitcast.59) | data formatting | bytes 8388608 | tf_op jit(solution)/shard_map/reshape | solution.py:151
  123.9 10.3 %all-to-all-start = ((bf16[128,4,32,128]{3,1,2,0:T(4,128)(2,1)}), bf16[128,4,32,128]{3,1,2,0:T(4,128)(2,1)}, u32[]{:S(2)}, u32[]{:S(2)}) async-start(bf16[128,4,32,128]{3,1,2,0:T(4,128)(2,1)} %copy.47), calls=%async_computation | async-start | bytes 8388608 | tf_op jit(solution)/shard_map/all_to_all | solution.py:152
  134.2 19.0 %shard_map.69 = bf16[8,16,4,32,128]{4,3,2,1,0:T(8,128)(2,1)} custom-call(s32[4]{0:T(128)} %get-tuple-element.22.slot_ref, bf16[4,1,512,512]{3,2,1,0:T(8,128)(2,1)} %own_re.3, bf16[4,1,512,512]{3,2,1,0:T(8,128)(2,1)} %own_im.3, bf16[4,1,512,512]{3,2,1,0:T(8,128)(2,1)} %collective-permute-done.2.rest_0_.far_re, ...), custom_call_target="tpu_custom_call" | custom-call | flops 12884901888 | bytes 15728640 | tf_op jit(solution)/shard_map/pallas_call | solution.py:89
  153.2 8.4 %copy.54 = bf16[128,4,32,128]{3,1,2,0:T(4,128)(2,1)} copy(bf16[128,4,32,128]{3,2,1,0:T(8,128)(2,1)} %bitcast.58) | data formatting | bytes 8388608 | tf_op jit(solution)/shard_map/reshape | solution.py:151
  161.6 0.0 copy-start.4
  161.6 0.0 copy-start.5
  161.6 23.0 %all-to-all-done = bf16[128,4,32,128]{3,1,2,0:T(4,128)(2,1)} async-done(((bf16[128,4,32,128]{3,1,2,0:T(4,128)(2,1)}), bf16[128,4,32,128]{3,1,2,0:T(4,128)(2,1)}, u32[]{:S(2)}, u32[]{:S(2)}) %all-to-all-start) | async-done | bytes 4194336 | tf_op jit(solution)/shard_map/all_to_all | solution.py:152
  184.6 7.9 %all-to-all-start.1 = ((bf16[128,4,32,128]{3,1,2,0:T(4,128)(2,1)}), bf16[128,4,32,128]{3,1,2,0:T(4,128)(2,1)}, u32[]{:S(2)}, u32[]{:S(2)}) async-start(bf16[128,4,32,128]{3,1,2,0:T(4,128)(2,1)} %copy.54), calls=%async_computation.1 | async-start | bytes 8388608 | tf_op jit(solution)/shard_map/all_to_all | solution.py:152
  192.5 0.0 copy-done.4
  192.6 0.0 copy-done.5
  192.8 0.3 copy.50
  193.1 0.2 reshape.227
  193.3 0.3 copy.57
  193.6 0.2 reshape.231
  193.8 0.3 copy.59
  194.0 0.2 reshape.233
  194.2 0.3 copy.52
  194.5 0.2 reshape.229
  194.7 8.0 %copy.51 = bf16[128,4,32,128]{0,3,1,2:T(8,128)(2,1)} copy(bf16[128,4,32,128]{3,1,2,0:T(4,128)(2,1)} %all-to-all-done) | data formatting | bytes 8388608 | tf_op jit(solution)/shard_map/all_to_all | solution.py:152
  202.7 0.0 copy-start
  202.7 5.5 %convolution_bitcast_fusion.2 = f32[32,128,256]{2,1,0:T(8,128)} fusion(bf16[128,4,32,128]{0,3,1,2:T(8,128)(2,1)} %copy.51, bf16[128,4,256,1]{2,0,1,3:T(8,128)(2,1)S(1)} %reshape.229), kind=kOutput, calls=%fused_computation.2 | convolution fusion | flops 1073741824 | bytes 8650752 | tf_op jit(solution)/shard_map/swrn,swx->rnx/dot_general | solution.py:158
  208.2 0.0 copy-done
  208.2 3.2 %convolution_bitcast_fusion.3 = f32[32,128,256]{2,1,0:T(8,128)} fusion(bf16[128,4,32,128]{0,3,1,2:T(8,128)(2,1)S(1)} %copy-done, bf16[128,4,256,1]{2,0,1,3:T(8,128)(2,1)S(1)} %reshape.227), kind=kOutput, calls=%fused_computation.3 | convolution fusion | flops 1073741824 | bytes 8650752 | tf_op jit(solution)/shard_map/swrn,swx->rnx/dot_general | solution.py:157
  211.5 31.5 %all-to-all-done.1 = bf16[128,4,32,128]{3,1,2,0:T(4,128)(2,1)} async-done(((bf16[128,4,32,128]{3,1,2,0:T(4,128)(2,1)}), bf16[128,4,32,128]{3,1,2,0:T(4,128)(2,1)}, u32[]{:S(2)}, u32[]{:S(2)}) %all-to-all-start.1) | async-done | bytes 4194336 | tf_op jit(solution)/shard_map/all_to_all | solution.py:152
  242.9 8.0 %copy.58 = bf16[128,4,32,128]{0,3,1,2:T(8,128)(2,1)} copy(bf16[128,4,32,128]{3,1,2,0:T(4,128)(2,1)} %all-to-all-done.1) | data formatting | bytes 8388608 | tf_op jit(solution)/shard_map/all_to_all | solution.py:152
  250.9 0.0 copy-start.1
  250.9 3.6 %convolution_bitcast_fusion = f32[32,128,256]{2,1,0:T(8,128)S(1)} fusion(bf16[128,4,32,128]{0,3,1,2:T(8,128)(2,1)} %copy.58, bf16[128,4,256,1]{2,0,1,3:T(8,128)(2,1)S(1)} %reshape.233), kind=kOutput, calls=%fused_computation | convolution fusion | flops 1073741824 | bytes 8650752 | tf_op jit(solution)/shard_map/swrn,swx->rnx/dot_general | solution.py:158
  254.5 0.0 copy-done.1
  254.5 0.0 copy-start.2
  254.5 0.0 copy-start.3
  254.5 1.2 convolution_bitcast_fusion.1
  255.8 0.9 copy-done.2
  256.7 1.3 copy-done.3
  258.0 0.8 fusion
  258.8 2.1 reshape.226
  260.9 5.7 %fusion.15 = (f32[32,64,1,128]{3,2,1,0:T(1,128)}, f32[32,64,1,128]{3,2,1,0:T(1,128)}) fusion(f32[32,64,2,128]{3,2,1,0:T(2,128)} %reshape.226), kind=kLoop, calls=%fused_computation.45 | loop fusion | bytes 4194304 | tf_op jit(solution)/shard_map/slice | solution.py:163
  (11 shorter events, 0.2 us)
Async XLA Ops:
  0.6 48.9 %collective-permute-start.2 = (bf16[4,1,512,512]{3,2,1,0:T(8,128)(2,1)}, bf16[4,1,512,512]{3,2,1,0:T(8,128)(2,1)}, u32[]{:S(2)}, u32[]{:S(2)}) collective-permute-start(bf16[4,1,512,512]{3,2,1,0:T(8,128)(2,1)} %own_re.3), channel_id=1, source_target_pairs={{0,32},{32,0},{16,48},{48,16},{64,96},{96,64},{80,112},{112,80},{1... | collective-permute-start | bytes 6291464 | tf_op jit(solution)/shard_map/ppermute | solution.py:19
  2.6 50.4 %collective-permute-start = (bf16[4,1,512,512]{3,2,1,0:T(8,128)(2,1)}, bf16[4,1,512,512]{3,2,1,0:T(8,128)(2,1)}, u32[]{:S(2)}, u32[]{:S(2)}) collective-permute-start(bf16[4,1,512,512]{3,2,1,0:T(8,128)(2,1)} %own_re.3), channel_id=1, source_target_pairs={{0,16},{16,0},{32,48},{48,32},{64,80},{80,64},{96,112},{112,96},{1... | collective-permute-start | bytes 6291464 | tf_op jit(solution)/shard_map/ppermute | solution.py:19
  5.7 87.9 %collective-permute-start.3 = (bf16[4,1,512,512]{3,2,1,0:T(8,128)(2,1)}, bf16[4,1,512,512]{3,2,1,0:T(8,128)(2,1)}, u32[]{:S(2)}, u32[]{:S(2)}) collective-permute-start(bf16[4,1,512,512]{3,2,1,0:T(8,128)(2,1)} %own_im.3), channel_id=1, source_target_pairs={{0,32},{32,0},{16,48},{48,16},{64,96},{96,64},{80,112},{112,80},{1... | collective-permute-start | bytes 6291464 | tf_op jit(solution)/shard_map/ppermute | solution.py:19
  5.8 90.7 %collective-permute-start.1 = (bf16[4,1,512,512]{3,2,1,0:T(8,128)(2,1)}, bf16[4,1,512,512]{3,2,1,0:T(8,128)(2,1)}, u32[]{:S(2)}, u32[]{:S(2)}) collective-permute-start(bf16[4,1,512,512]{3,2,1,0:T(8,128)(2,1)} %own_im.3), channel_id=1, source_target_pairs={{0,16},{16,0},{32,48},{48,32},{64,80},{80,64},{96,112},{112,96},{1... | collective-permute-start | bytes 6291464 | tf_op jit(solution)/shard_map/ppermute | solution.py:19
  20.6 9.1 %copy-start.6 = (s32[2,4]{1,0:T(2,128)S(1)}, s32[2,4]{1,0:T(2,128)}, u32[]{:S(2)}) copy-start(s32[2,4]{1,0:T(2,128)} %param.7) | copy-start | bytes 100
  123.9 60.7 %all-to-all-start = ((bf16[128,4,32,128]{3,1,2,0:T(4,128)(2,1)}), bf16[128,4,32,128]{3,1,2,0:T(4,128)(2,1)}, u32[]{:S(2)}, u32[]{:S(2)}) async-start(bf16[128,4,32,128]{3,1,2,0:T(4,128)(2,1)} %copy.47), calls=%async_computation | async-start | bytes 8388608 | tf_op jit(solution)/shard_map/all_to_all | solution.py:152
  161.6 31.0 %copy-start.4 = (bf16[32,2,16,128]{3,2,1,0:T(8,128)(2,1)S(1)}, bf16[32,2,16,128]{3,2,1,0:T(8,128)(2,1)}, u32[]{:S(2)}) copy-start(bf16[32,2,16,128]{3,2,1,0:T(8,128)(2,1)} %param.8) | copy-start | bytes 786436
  161.6 31.0 %copy-start.5 = (bf16[32,2,16,128]{3,2,1,0:T(8,128)(2,1)S(1)}, bf16[32,2,16,128]{3,2,1,0:T(8,128)(2,1)}, u32[]{:S(2)}) copy-start(bf16[32,2,16,128]{3,2,1,0:T(8,128)(2,1)} %param.9) | copy-start | bytes 786436
  184.6 58.3 %all-to-all-start.1 = ((bf16[128,4,32,128]{3,1,2,0:T(4,128)(2,1)}), bf16[128,4,32,128]{3,1,2,0:T(4,128)(2,1)}, u32[]{:S(2)}, u32[]{:S(2)}) async-start(bf16[128,4,32,128]{3,1,2,0:T(4,128)(2,1)} %copy.54), calls=%async_computation.1 | async-start | bytes 8388608 | tf_op jit(solution)/shard_map/all_to_all | solution.py:152
  202.7 5.5 %copy-start = (bf16[128,4,32,128]{0,3,1,2:T(8,128)(2,1)S(1)}, bf16[128,4,32,128]{0,3,1,2:T(8,128)(2,1)}, u32[]{:S(2)}) copy-start(bf16[128,4,32,128]{0,3,1,2:T(8,128)(2,1)} %copy.51) | copy-start | bytes 12582916
  250.9 3.6 %copy-start.1 = (bf16[128,4,32,128]{0,3,1,2:T(8,128)(2,1)S(1)}, bf16[128,4,32,128]{0,3,1,2:T(8,128)(2,1)}, u32[]{:S(2)}) copy-start(bf16[128,4,32,128]{0,3,1,2:T(8,128)(2,1)} %copy.58) | copy-start | bytes 12582916
  254.5 2.2 copy-start.2
  254.5 3.5 %copy-start.3 = (f32[32,128,256]{2,1,0:T(8,128)S(1)}, f32[32,128,256]{2,1,0:T(8,128)}, u32[]{:S(2)}) copy-start(f32[32,128,256]{2,1,0:T(8,128)} %convolution_bitcast_fusion.3) | copy-start | bytes 12582916

commit v3 on v2

--- a/solution.py
+++ b/solution.py
@@ -150,16 +150,16 @@
         )
         send = send.reshape(wave_devices * angle_devices, *send.shape[2:])
         got = lax.all_to_all(send, ("wave", "angle"), 0, 0, tiled=True)
-        kr = k_re[section_number]
-        ki = k_im[section_number]
-        w_first = jnp.stack([kr, ki], axis=2).reshape(kr.shape[0], kr.shape[1], -1)
-        w_second = jnp.stack([-ki, kr], axis=2).reshape(kr.shape[0], kr.shape[1], -1)
-        t_first = jnp.einsum("swrn,swx->rnx", got, w_first, preferred_element_type=fp)
-        t_second = jnp.einsum("swrn,swx->rnx", got, w_second, preferred_element_type=fp)
-        half = got.shape[3] // 2
-        part = t_first[:, :half] + t_second[:, half:]
+        got = got.reshape(-1, *got.shape[2:])
+        kr = k_re[section_number].reshape(-1, depth_count)
+        ki = k_im[section_number].reshape(-1, depth_count)
+        weight = jnp.concatenate([kr, ki, -ki, kr], axis=1).T
+        part = jnp.einsum("yk,krn->yrn", weight, got, preferred_element_type=fp)
         volume = part if volume is None else volume + part
-    volume = volume.reshape(volume.shape[0], volume.shape[1], 2, depth_count)
+    half = volume.shape[2] // 2
+    out_count = volume.shape[0] // 2
+    volume = volume[:out_count, :, :half] + volume[out_count:, :, half:]
+    volume = jnp.transpose(volume.reshape(2, depth_count, *volume.shape[1:]), (2, 3, 0, 1))
     return (volume[:, :, 0, :], volume[:, :, 1, :])
 
 

time: 271 us -> 276 us (1.018)
  local copies, waits for them, and re-layouts: 48.5 us -> 21 us
  waiting for transfers between devices: 121 us -> 140 us
  other arithmetic: 21 us -> 34.5 us
    all_to_all x2, waiting for transfers between devices: 54.5 us -> 73.6 us  [shards(): got = lax.all_to_all(send, ('wave', 'angle'), 0, 0, tiled=True)]
    all_to_all x2 -> x0, local copies, waits for them, and re-layouts: 16 us -> none  [shards(): got = lax.all_to_all(send, ('wave', 'angle'), 0, 0, tiled=True)]
    unnamed x0 -> x2, matrix products: none -> 13.7 us
    dot_general x4 -> x0, matrix products: 13.6 us -> none  [the longest x2 9.12 us: shards(): jnp.einsum('swrn,swx->rnx', got, w_second, preferred_element_type=fp)]
    add x1, other arithmetic: 0.81 us -> 11.8 us  [shards(): volume = part if volume is None else volume + part]
    slice x7 -> x2, local copies, waits for them, and re-layouts: 5.8 us -> 0.21 us  [the longest x1 0.1 us: shards(): kr = k_re[section_number].reshape(-1, depth_count)]
    reshape x7 -> x4, local copies, waits for them, and re-layouts: 19.5 us -> 15.4 us  [the longest x2 15.2 us: shards(): got = got.reshape(-1, *got.shape[2:])]
  transfers between devices with their start and end apart: 6 -> 6, of which waited for: 6 -> 6; matrix products, arithmetic and copies ran while one was open for 19% -> 12% of each run, Pallas kernels for 7% -> 7%
where the time goes in v3:
time: 276 us; the launch traced here: 272 us
  waiting for transfers between devices  140 us (51%)
  Pallas kernels  38.1 us (14%)
  other arithmetic  34.5 us (12%)
  starting transfers between devices  24 us (9%)
  local copies, waits for them, and re-layouts  21 us (8%)
  matrix products  13.7 us (5%)
    all_to_all x2, waiting for transfers between devices, shards(): got = lax.all_to_all(send, ('wave', 'angle'), 0, 0, tiled=True)  73.6 us
    ppermute x4, waiting for transfers between devices, from_partner(): return lax.ppermute(block, axis, route)  66.2 us
    pallas_call x2, Pallas kernels, spectra(): pl.pallas_call(spectrum_kernel, out_shape=jax.ShapeDtypeStruct((blocks, g...  38.1 us
    all_to_all x2, starting transfers between devices, shards(): got = lax.all_to_all(send, ('wave', 'angle'), 0, 0, tiled=True)  18.3 us
    reshape x2, local copies, waits for them, and re-layouts, shards(): got = got.reshape(-1, *got.shape[2:])  15.2 us
    unnamed x2, matrix products  13.7 us
    add x1, other arithmetic, shards(): volume = part if volume is None else volume + part  11.8 us
    convert_element_type x2, other arithmetic, dft_tables(): (-jnp.sin(phase) * factor).astype(jnp.bfloat16)  10.3 us
  transfers between devices with their start and end apart: 6, of which 6 were waited for; matrix products, arithmetic and copies ran while one was open for 12% of the time, Pallas kernels for 7%

profile of v3, /device:TPU:24, one launch (start us, length us, event | category | flops | bytes accessed | tf_op | source)
XLA Modules:
  0.0 271.7 jit_solution(3548856812222584254)
XLA Ops:
  0.6 2.0 collective-permute-start.2
  2.6 3.0 %collective-permute-start = (bf16[4,1,512,512]{3,2,1,0:T(8,128)(2,1)}, bf16[4,1,512,512]{3,2,1,0:T(8,128)(2,1)}, u32[]{:S(2)}, u32[]{:S(2)}) collective-permute-start(bf16[4,1,512,512]{3,2,1,0:T(8,128)(2,1)} %own_re.3), channel_id=1, source_target_pairs={{0,16},{16,0},{32,48},{48,32},{64,80},{80,64},{96,112},{112,96},{1... | collective-permute-start | bytes 6291464 | tf_op jit(solution)/shard_map/ppermute | solution.py:19
  5.7 0.1 collective-permute-start.3
  5.8 0.5 collective-permute-start.1
  6.3 4.9 %multiply_convert_fusion.2 = (bf16[512,8,1,64]{0,3,2,1:T(8,128)(2,1)S(1)}, bf16[512,8,1,64]{0,3,2,1:T(8,128)(2,1)S(1)}) fusion(s32[8,64]{1,0:T(8,128)S(1)} %multiply_add_fusion), kind=kLoop, calls=%fused_computation.26 | loop fusion | flops 4980736 | bytes 1050624 | tf_op jit(solution)/shard_map/convert_element_type | solution.py:29
  11.2 4.9 %fusion.29 = (bf16[512,8,1,64]{0,3,2,1:T(8,128)(2,1)S(1)}, bf16[512,8,1,64]{0,3,2,1:T(8,128)(2,1)S(1)}) fusion(s32[8,64]{1,0:T(8,128)S(1)} %multiply_add_fusion), kind=kLoop, calls=%fused_computation.50 | loop fusion | flops 6553600 | bytes 1050624 | tf_op jit(solution)/shard_map/neg | solution.py:44
  16.1 1.2 pad_maximum_fusion.4
  17.3 0.5 copy.17
  17.8 1.5 copy.15
  19.3 1.3 copy.14
  20.6 0.0 copy-start.3
  20.6 5.3 %multiply_convert_fusion = (bf16[512,512]{1,0:T(8,128)(2,1)}, bf16[512,512]{1,0:T(8,128)(2,1)}) fusion(), kind=kLoop, calls=%fused_computation.22 | loop fusion | flops 4980736 | bytes 1048576 | tf_op jit(solution)/shard_map/convert_element_type | solution.py:29
  26.0 3.7 %pad_maximum_fusion.1 = (bf16[1024,1024]{1,0:T(8,128)(2,1)}, bf16[1024,1024]{1,0:T(8,128)(2,1)}) fusion(bf16[512,1024]{1,0:T(8,128)(2,1)S(1)} %copy.17, bf16[512,1024]{1,0:T(8,128)(2,1)S(1)} %copy.15, bf16[512,1024]{1,0:T(8,128)(2,1)} %copy.14), kind=kLoop, calls=%fused_computation.4 | loop fusion | flops 8388608 | bytes 7340032 | tf_op jit(solution)/shard_map/concatenate | solution.py:41
  29.7 0.0 copy-done.3
  29.7 0.5 slice_bitcast_fusion.2
  30.3 19.3 %collective-permute-done.2.rest_0_.far_re = bf16[4,1,512,512]{3,2,1,0:T(8,128)(2,1)} collective-permute-done((bf16[4,1,512,512]{3,2,1,0:T(8,128)(2,1)}, bf16[4,1,512,512]{3,2,1,0:T(8,128)(2,1)}, u32[]{:S(2)}, u32[]{:S(2)}) %collective-permute-start.2) | collective-permute-done | bytes 2097184 | tf_op jit(solution)/shard_map/ppermute | solution.py:19
  49.5 3.5 %collective-permute-done.far_re.rest_0_ = bf16[4,1,512,512]{3,2,1,0:T(8,128)(2,1)} collective-permute-done((bf16[4,1,512,512]{3,2,1,0:T(8,128)(2,1)}, bf16[4,1,512,512]{3,2,1,0:T(8,128)(2,1)}, u32[]{:S(2)}, u32[]{:S(2)}) %collective-permute-start) | collective-permute-done | bytes 2097184 | tf_op jit(solution)/shard_map/ppermute | solution.py:19
  53.0 40.5 %collective-permute-done.3.rest_1_.far_im = bf16[4,1,512,512]{3,2,1,0:T(8,128)(2,1)} collective-permute-done((bf16[4,1,512,512]{3,2,1,0:T(8,128)(2,1)}, bf16[4,1,512,512]{3,2,1,0:T(8,128)(2,1)}, u32[]{:S(2)}, u32[]{:S(2)}) %collective-permute-start.3) | collective-permute-done | bytes 2097184 | tf_op jit(solution)/shard_map/ppermute | solution.py:19
  93.5 3.0 %collective-permute-done.1.far_im.rest_1_ = bf16[4,1,512,512]{3,2,1,0:T(8,128)(2,1)} collective-permute-done((bf16[4,1,512,512]{3,2,1,0:T(8,128)(2,1)}, bf16[4,1,512,512]{3,2,1,0:T(8,128)(2,1)}, u32[]{:S(2)}, u32[]{:S(2)}) %collective-permute-start.1) | collective-permute-done | bytes 2097184 | tf_op jit(solution)/shard_map/ppermute | solution.py:19
  96.5 19.0 %shard_map.69 = bf16[8,16,4,32,128]{4,3,2,1,0:T(8,128)(2,1)} custom-call(s32[4]{0:T(128)} %get-tuple-element.17.slot_ref, bf16[4,1,512,512]{3,2,1,0:T(8,128)(2,1)} %own_re.3, bf16[4,1,512,512]{3,2,1,0:T(8,128)(2,1)} %own_im.3, bf16[4,1,512,512]{3,2,1,0:T(8,128)(2,1)} %collective-permute-done.2.rest_0_.far_re, ...), custom_call_target="tpu_custom_call" | custom-call | flops 12884901888 | bytes 15728640 | tf_op jit(solution)/shard_map/pallas_call | solution.py:89
  115.5 10.3 %all-to-all-start.1 = ((bf16[128,4,32,128]{3,2,1,0:T(8,128)(2,1)}), bf16[128,4,32,128]{3,2,1,0:T(8,128)(2,1)}, u32[]{:S(2)}, u32[]{:S(2)}) async-start(bf16[128,4,32,128]{3,2,1,0:T(8,128)(2,1)} %bitcast.48), calls=%async_computation.1 | async-start | bytes 8388608 | tf_op jit(solution)/shard_map/all_to_all | solution.py:152
  125.8 19.0 %shard_map.68 = bf16[8,16,4,32,128]{4,3,2,1,0:T(8,128)(2,1)} custom-call(s32[4]{0:T(128)} %get-tuple-element.18.slot_ref, bf16[4,1,512,512]{3,2,1,0:T(8,128)(2,1)} %own_re.3, bf16[4,1,512,512]{3,2,1,0:T(8,128)(2,1)} %own_im.3, bf16[4,1,512,512]{3,2,1,0:T(8,128)(2,1)} %collective-permute-done.far_re.rest_0_, ...), custom_call_target="tpu_custom_call" | custom-call | flops 12884901888 | bytes 15728640 | tf_op jit(solution)/shard_map/pallas_call | solution.py:89
  144.8 31.4 %all-to-all-done.1 = bf16[128,4,32,128]{3,2,1,0:T(8,128)(2,1)} async-done(((bf16[128,4,32,128]{3,2,1,0:T(8,128)(2,1)}), bf16[128,4,32,128]{3,2,1,0:T(8,128)(2,1)}, u32[]{:S(2)}, u32[]{:S(2)}) %all-to-all-start.1) | async-done | bytes 4194336 | tf_op jit(solution)/shard_map/all_to_all | solution.py:152
  176.2 0.0 copy-start.1
  176.2 0.0 copy-start.2
  176.2 8.1 %all-to-all-start = ((bf16[128,4,32,128]{3,2,1,0:T(8,128)(2,1)}), bf16[128,4,32,128]{3,2,1,0:T(8,128)(2,1)}, u32[]{:S(2)}, u32[]{:S(2)}) async-start(bf16[128,4,32,128]{3,2,1,0:T(8,128)(2,1)} %bitcast.47), calls=%async_computation | async-start | bytes 8388608 | tf_op jit(solution)/shard_map/all_to_all | solution.py:152
  184.3 0.0 copy-done.1
  184.3 0.1 copy.26
  184.4 0.0 copy-done.2
  184.4 0.1 copy.25
  184.6 0.1 fusion.33
  184.8 0.1 fusion.34
  184.9 7.6 %copy.19 = bf16[512,32,128]{0,2,1:T(8,128)(2,1)} copy(bf16[512,32,128]{2,1,0:T(8,128)(2,1)} %bitcast.18) | data formatting | bytes 8388608 | tf_op jit(solution)/shard_map/reshape | solution.py:153
  192.5 42.2 %all-to-all-done = bf16[128,4,32,128]{3,2,1,0:T(8,128)(2,1)} async-done(((bf16[128,4,32,128]{3,2,1,0:T(8,128)(2,1)}), bf16[128,4,32,128]{3,2,1,0:T(8,128)(2,1)}, u32[]{:S(2)}, u32[]{:S(2)}) %all-to-all-start) | async-done | bytes 4194336 | tf_op jit(solution)/shard_map/all_to_all | solution.py:152
  234.7 7.6 %copy.18 = bf16[512,32,128]{0,2,1:T(8,128)(2,1)} copy(bf16[512,32,128]{2,1,0:T(8,128)(2,1)} %bitcast.11) | data formatting | bytes 8388608 | tf_op jit(solution)/shard_map/reshape | solution.py:153
  242.2 0.0 copy-start
  242.2 7.9 %fusion.13 = f32[512,4096]{0,1} fusion(bf16[512,4096]{0,1:T(8,128)(2,1)} %bitcast.43, bf16[512,128]{1,0:T(8,128)(2,1)S(1)} %bitcast.56, bf16[512,128]{1,0:T(8,128)(2,1)S(1)} %neg.57, bf16[512,128]{1,0:T(8,128)(2,1)S(1)} %bitcast.52), kind=kOutput, calls=%fused_computation.32 | convolution fusion | flops 2149580800 | bytes 12976128
  250.2 0.0 copy-done
  250.2 5.8 %fusion.21 = f32[512,4096]{0,1} fusion(bf16[512,4096]{0,1:T(8,128)(2,1)S(1)} %bitcast.42, bf16[512,128]{1,0:T(8,128)(2,1)S(1)} %bitcast.55, bf16[512,128]{1,0:T(8,128)(2,1)S(1)} %neg.62, bf16[512,128]{1,0:T(8,128)(2,1)S(1)} %bitcast.50), kind=kOutput, calls=%fused_computation.40 | convolution fusion | flops 2149580800 | bytes 12976128
  255.9 11.8 %add.68 = f32[512,32,128]{0,2,1:T(8,128)} add(f32[512,32,128]{0,2,1:T(8,128)} %bitcast.40, f32[512,32,128]{0,2,1:T(8,128)} %bitcast.41) | non-fusion elementwise | flops 2097152 | bytes 25165824 | tf_op jit(solution)/shard_map/add | solution.py:158
  267.7 2.6 bitcast_bitcast_fusion
  270.3 1.5 slice_bitcast_fusion
  (3 shorter events, 0.1 us)
Async XLA Ops:
  0.6 48.9 %collective-permute-start.2 = (bf16[4,1,512,512]{3,2,1,0:T(8,128)(2,1)}, bf16[4,1,512,512]{3,2,1,0:T(8,128)(2,1)}, u32[]{:S(2)}, u32[]{:S(2)}) collective-permute-start(bf16[4,1,512,512]{3,2,1,0:T(8,128)(2,1)} %own_re.3), channel_id=1, source_target_pairs={{0,32},{32,0},{16,48},{48,16},{64,96},{96,64},{80,112},{112,80},{1... | collective-permute-start | bytes 6291464 | tf_op jit(solution)/shard_map/ppermute | solution.py:19
  2.6 50.4 %collective-permute-start = (bf16[4,1,512,512]{3,2,1,0:T(8,128)(2,1)}, bf16[4,1,512,512]{3,2,1,0:T(8,128)(2,1)}, u32[]{:S(2)}, u32[]{:S(2)}) collective-permute-start(bf16[4,1,512,512]{3,2,1,0:T(8,128)(2,1)} %own_re.3), channel_id=1, source_target_pairs={{0,16},{16,0},{32,48},{48,32},{64,80},{80,64},{96,112},{112,96},{1... | collective-permute-start | bytes 6291464 | tf_op jit(solution)/shard_map/ppermute | solution.py:19
  5.7 87.9 %collective-permute-start.3 = (bf16[4,1,512,512]{3,2,1,0:T(8,128)(2,1)}, bf16[4,1,512,512]{3,2,1,0:T(8,128)(2,1)}, u32[]{:S(2)}, u32[]{:S(2)}) collective-permute-start(bf16[4,1,512,512]{3,2,1,0:T(8,128)(2,1)} %own_im.3), channel_id=1, source_target_pairs={{0,32},{32,0},{16,48},{48,16},{64,96},{96,64},{80,112},{112,80},{1... | collective-permute-start | bytes 6291464 | tf_op jit(solution)/shard_map/ppermute | solution.py:19
  5.8 90.7 %collective-permute-start.1 = (bf16[4,1,512,512]{3,2,1,0:T(8,128)(2,1)}, bf16[4,1,512,512]{3,2,1,0:T(8,128)(2,1)}, u32[]{:S(2)}, u32[]{:S(2)}) collective-permute-start(bf16[4,1,512,512]{3,2,1,0:T(8,128)(2,1)} %own_im.3), channel_id=1, source_target_pairs={{0,16},{16,0},{32,48},{48,32},{64,80},{80,64},{96,112},{112,96},{1... | collective-permute-start | bytes 6291464 | tf_op jit(solution)/shard_map/ppermute | solution.py:19
  20.6 9.1 %copy-start.3 = (s32[2,4]{1,0:T(2,128)S(1)}, s32[2,4]{1,0:T(2,128)}, u32[]{:S(2)}) copy-start(s32[2,4]{1,0:T(2,128)} %param.7) | copy-start | bytes 100
  115.5 60.7 %all-to-all-start.1 = ((bf16[128,4,32,128]{3,2,1,0:T(8,128)(2,1)}), bf16[128,4,32,128]{3,2,1,0:T(8,128)(2,1)}, u32[]{:S(2)}, u32[]{:S(2)}) async-start(bf16[128,4,32,128]{3,2,1,0:T(8,128)(2,1)} %bitcast.48), calls=%async_computation.1 | async-start | bytes 8388608 | tf_op jit(solution)/shard_map/all_to_all | solution.py:152
  176.2 8.1 %copy-start.1 = (bf16[32,2,16,128]{3,2,1,0:T(8,128)(2,1)S(1)}, bf16[32,2,16,128]{3,2,1,0:T(8,128)(2,1)}, u32[]{:S(2)}) copy-start(bf16[32,2,16,128]{3,2,1,0:T(8,128)(2,1)} %param.8) | copy-start | bytes 786436
  176.2 8.2 %copy-start.2 = (bf16[32,2,16,128]{3,2,1,0:T(8,128)(2,1)S(1)}, bf16[32,2,16,128]{3,2,1,0:T(8,128)(2,1)}, u32[]{:S(2)}) copy-start(bf16[32,2,16,128]{3,2,1,0:T(8,128)(2,1)} %param.9) | copy-start | bytes 786436
  176.2 58.5 %all-to-all-start = ((bf16[128,4,32,128]{3,2,1,0:T(8,128)(2,1)}), bf16[128,4,32,128]{3,2,1,0:T(8,128)(2,1)}, u32[]{:S(2)}, u32[]{:S(2)}) async-start(bf16[128,4,32,128]{3,2,1,0:T(8,128)(2,1)} %bitcast.47), calls=%async_computation | async-start | bytes 8388608 | tf_op jit(solution)/shard_map/all_to_all | solution.py:152
  242.2 7.9 %copy-start = (bf16[512,32,128]{0,2,1:T(8,128)(2,1)S(1)}, bf16[512,32,128]{0,2,1:T(8,128)(2,1)}, u32[]{:S(2)}) copy-start(bf16[512,32,128]{0,2,1:T(8,128)(2,1)} %copy.19) | copy-start | bytes 12582916

commit v4 on v2

--- a/solution.py
+++ b/solution.py
@@ -40,13 +40,11 @@
         lower = jnp.concatenate(bottom, axis=2).reshape(rows, -1)
         return jnp.concatenate([upper, lower], axis=0)
 
-    first = join([er, ei], [-ei, er])
-    second = join([-ei, er], [-er, -ei])
-    return first, second
+    return join([er, ei], [-ei, er])
 
 
 def spectrum_kernel(
-    slot_ref, own_re, own_im, far_re, far_im, col_a, col_b, row_re, row_im, *rest
+    slot_ref, own_re, own_im, far_re, far_im, col_a, row_re, row_im, *rest
 ):
     out_ref = rest[-1]
     fp = jnp.float32
@@ -58,26 +56,23 @@
     z_re = (a_re * b_re + a_im * b_im).astype(bf)
     z_im = (a_im * b_re - a_re * b_im).astype(bf)
     n = z_re.shape[1]
-    y_a = (
+    y = (
         jnp.dot(z_re, col_a[:n, :], preferred_element_type=fp)
         + jnp.dot(z_im, col_a[n:, :], preferred_element_type=fp)
     ).astype(bf)
-    y_b = (
-        jnp.dot(z_re, col_b[:n, :], preferred_element_type=fp)
-        + jnp.dot(z_im, col_b[n:, :], preferred_element_type=fp)
-    ).astype(bf)
-    spec = (
-        jnp.dot(row_re[...], y_a, preferred_element_type=fp)
-        + jnp.dot(row_im[...], y_b, preferred_element_type=fp)
-    ).astype(bf)
+    first = jnp.dot(row_re[...], y, preferred_element_type=fp)
+    second = jnp.dot(row_im[...], y, preferred_element_type=fp)
     blocks, groups, _, rows_per, lanes = out_ref.shape
+    lane = lax.broadcasted_iota(jnp.int32, (first.shape[0], lanes), 1)
     for block in range(blocks):
-        out_ref[block, :, 0, :, :] = spec[:, block * lanes : (block + 1) * lanes].reshape(
-            groups, rows_per, lanes
-        )
+        cut = slice(block * lanes, (block + 1) * lanes)
+        swapped = pltpu.roll(second[:, cut], lanes // 2, 1)
+        swapped = jnp.where(lane < lanes // 2, -swapped, swapped)
+        spec = (first[:, cut] + swapped).astype(bf)
+        out_ref[block, :, 0, :, :] = spec.reshape(groups, rows_per, lanes)
 
 
-def spectra(slots, own_re, own_im, far_re, far_im, col_a, col_b, row_re, row_im, blocks, groups, after):
+def spectra(slots, own_re, own_im, far_re, far_im, col_a, row_re, row_im, blocks, groups, after):
     waves, _, rows, cols = own_re.shape
     lanes = 2 * cols // blocks
     rows_per = rows // groups
@@ -85,14 +80,14 @@
     partner = pl.BlockSpec((1, 1, rows, cols), lambda i, sl: (sl[i], 0, 0, 0))
     whole_col = pl.BlockSpec((2 * cols, 2 * cols), lambda i, sl: (0, 0))
     whole_row = pl.BlockSpec((rows, rows), lambda i, sl: (0, 0))
-    flops = waves * (2 * 2 * rows * (2 * cols) * (2 * cols) + 2 * 2 * rows * rows * (2 * cols))
+    flops = waves * (2 * rows * (2 * cols) * (2 * cols) + 2 * 2 * rows * rows * (2 * cols))
     return pl.pallas_call(
         spectrum_kernel,
         out_shape=jax.ShapeDtypeStruct((blocks, groups, waves, rows_per, lanes), jnp.bfloat16),
         grid_spec=pltpu.PrefetchScalarGridSpec(
             num_scalar_prefetch=1,
             grid=(waves,),
-            in_specs=[field, field, partner, partner, whole_col, whole_col, whole_row, whole_row]
+            in_specs=[field, field, partner, partner, whole_col, whole_row, whole_row]
             + [pl.BlockSpec(memory_space=pl.ANY)] * len(after),
             out_specs=pl.BlockSpec(
                 (blocks, groups, 1, rows_per, lanes), lambda i, sl: (0, 0, i, 0, 0)
@@ -102,7 +97,7 @@
         cost_estimate=pl.CostEstimate(
             flops=flops, transcendentals=0, bytes_accessed=waves * rows * cols * 12 + 12 * cols * cols
         ),
-    )(slots, own_re, own_im, far_re, far_im, col_a, col_b, row_re, row_im, *after)
+    )(slots, own_re, own_im, far_re, far_im, col_a, row_re, row_im, *after)
 
 
 def shards(hologram_real, hologram_imaginary, pair_slot, kernel_real, kernel_imaginary):
@@ -114,7 +109,7 @@
     depth_count = kernel_real.shape[3]
     row_real, row_imag = dft_tables(row_count)
     col_real, col_imag = dft_tables(col_count)
-    col_a, col_b = column_tables(col_real, col_imag, wave_devices)
+    col_a = column_tables(col_real, col_imag, wave_devices)
 
     def all_weights(kernel_part):
         block = kernel_part.reshape(
@@ -141,7 +136,6 @@
             got_real,
             got_imag,
             col_a,
-            col_b,
             row_real,
             row_imag,
             wave_devices,

time: 271 us -> 267 us (0.985)
  waiting for transfers between devices: 121 us -> 131 us
  Pallas kernels: 38 us -> 29.5 us
  other arithmetic: 21 us -> 17.1 us
    pallas_call x2, Pallas kernels: 38 us -> 29.5 us  [spectra(): pl.pallas_call(spectrum_kernel, out_shape=jax.ShapeDtypeStruct((blocks, g...]
    ppermute x4, waiting for transfers between devices: 66.2 us -> 72.4 us  [from_partner(): return lax.ppermute(block, axis, route)]
    all_to_all x2, waiting for transfers between devices: 54.5 us -> 58.8 us  [shards(): got = lax.all_to_all(send, ('wave', 'angle'), 0, 0, tiled=True)]
  transfers between devices with their start and end apart: 6 -> 6, of which waited for: 6 -> 6; matrix products, arithmetic and copies ran while one was open for 19% -> 17% of each run, Pallas kernels for 7% -> 6%
where the time goes in v4:
time: 267 us; the launch traced here: 262 us
  waiting for transfers between devices  131 us (49%)
  local copies, waits for them, and re-layouts  46.2 us (17%)
  Pallas kernels  29.5 us (11%)
  starting transfers between devices  23.8 us (9%)
  other arithmetic  17.1 us (6%)
  matrix products  13.6 us (5%)
    ppermute x4, waiting for transfers between devices, from_partner(): return lax.ppermute(block, axis, route)  72.4 us
    all_to_all x2, waiting for transfers between devices, shards(): got = lax.all_to_all(send, ('wave', 'angle'), 0, 0, tiled=True)  58.8 us
    pallas_call x2, Pallas kernels, spectra(): pl.pallas_call(spectrum_kernel, out_shape=jax.ShapeDtypeStruct((blocks, g...  29.5 us
    all_to_all x2, starting transfers between devices, shards(): got = lax.all_to_all(send, ('wave', 'angle'), 0, 0, tiled=True)  18.2 us
    reshape x2, local copies, waits for them, and re-layouts, shards(): send = send.reshape(wave_devices * angle_devices, *send.shape[2:])  16.8 us
    all_to_all x2, local copies, waits for them, and re-layouts, shards(): got = lax.all_to_all(send, ('wave', 'angle'), 0, 0, tiled=True)  16 us
    convert_element_type x2, other arithmetic, dft_tables(): (-jnp.sin(phase) * factor).astype(jnp.bfloat16)  10.3 us
    dot_general x2, matrix products, shards(): jnp.einsum('swrn,swx->rnx', got, w_second, preferred_element_type=fp)  9.11 us
  transfers between devices with their start and end apart: 6, of which 6 were waited for; matrix products, arithmetic and copies ran while one was open for 17% of the time, Pallas kernels for 6%

profile of v4, /device:TPU:24, one launch (start us, length us, event | category | flops | bytes accessed | tf_op | source)
XLA Modules:
  0.0 262.4 jit_solution(2632081812444689361)
XLA Ops:
  0.6 2.0 collective-permute-start.2
  2.6 3.0 %collective-permute-start = (bf16[4,1,512,512]{3,2,1,0:T(8,128)(2,1)}, bf16[4,1,512,512]{3,2,1,0:T(8,128)(2,1)}, u32[]{:S(2)}, u32[]{:S(2)}) collective-permute-start(bf16[4,1,512,512]{3,2,1,0:T(8,128)(2,1)} %own_re.3), channel_id=1, source_target_pairs={{0,16},{16,0},{32,48},{48,32},{64,80},{80,64},{96,112},{112,96},{1... | collective-permute-start | bytes 6291464 | tf_op jit(solution)/shard_map/ppermute | solution.py:19
  5.7 0.1 collective-permute-start.3
  5.8 0.5 collective-permute-start.1
  6.3 4.3 %fusion.13 = bf16[512,8,1,64]{0,3,2,1:T(8,128)(2,1)S(1)} fusion(s32[8,64]{1,0:T(8,128)S(1)} %multiply_add_fusion), kind=kLoop, calls=%fused_computation.36 | loop fusion | flops 5242880 | bytes 526336 | tf_op jit(solution)/shard_map/neg | solution.py:43
  10.6 4.9 %multiply_convert_fusion.2 = (bf16[512,8,1,64]{0,3,2,1:T(8,128)(2,1)S(1)}, bf16[512,8,1,64]{0,3,2,1:T(8,128)(2,1)S(1)}) fusion(s32[8,64]{1,0:T(8,128)S(1)} %multiply_add_fusion), kind=kLoop, calls=%fused_computation.26 | loop fusion | flops 4980736 | bytes 1050624 | tf_op jit(solution)/shard_map/convert_element_type | solution.py:29
  15.5 0.2 pad_maximum_fusion.1
  15.7 0.5 copy.39
  16.2 0.0 copy-start.6
  16.2 0.5 copy.40
  16.8 5.3 %multiply_convert_fusion = (bf16[512,512]{1,0:T(8,128)(2,1)}, bf16[512,512]{1,0:T(8,128)(2,1)}) fusion(), kind=kLoop, calls=%fused_computation.22 | loop fusion | flops 4980736 | bytes 1048576 | tf_op jit(solution)/shard_map/convert_element_type | solution.py:29
  22.1 1.5 pad_maximum_fusion.col_a
  23.6 0.0 copy-done.6
  23.6 0.5 slice_bitcast_fusion.1
  24.1 25.4 %collective-permute-done.2.rest_0_.far_re = bf16[4,1,512,512]{3,2,1,0:T(8,128)(2,1)} collective-permute-done((bf16[4,1,512,512]{3,2,1,0:T(8,128)(2,1)}, bf16[4,1,512,512]{3,2,1,0:T(8,128)(2,1)}, u32[]{:S(2)}, u32[]{:S(2)}) %collective-permute-start.2) | collective-permute-done | bytes 2097184 | tf_op jit(solution)/shard_map/ppermute | solution.py:19
  49.5 3.5 %collective-permute-done.far_re.rest_0_ = bf16[4,1,512,512]{3,2,1,0:T(8,128)(2,1)} collective-permute-done((bf16[4,1,512,512]{3,2,1,0:T(8,128)(2,1)}, bf16[4,1,512,512]{3,2,1,0:T(8,128)(2,1)}, u32[]{:S(2)}, u32[]{:S(2)}) %collective-permute-start) | collective-permute-done | bytes 2097184 | tf_op jit(solution)/shard_map/ppermute | solution.py:19
  53.0 40.5 %collective-permute-done.3.rest_1_.far_im = bf16[4,1,512,512]{3,2,1,0:T(8,128)(2,1)} collective-permute-done((bf16[4,1,512,512]{3,2,1,0:T(8,128)(2,1)}, bf16[4,1,512,512]{3,2,1,0:T(8,128)(2,1)}, u32[]{:S(2)}, u32[]{:S(2)}) %collective-permute-start.3) | collective-permute-done | bytes 2097184 | tf_op jit(solution)/shard_map/ppermute | solution.py:19
  93.5 3.0 %collective-permute-done.1.far_im.rest_1_ = bf16[4,1,512,512]{3,2,1,0:T(8,128)(2,1)} collective-permute-done((bf16[4,1,512,512]{3,2,1,0:T(8,128)(2,1)}, bf16[4,1,512,512]{3,2,1,0:T(8,128)(2,1)}, u32[]{:S(2)}, u32[]{:S(2)}) %collective-permute-start.1) | collective-permute-done | bytes 2097184 | tf_op jit(solution)/shard_map/ppermute | solution.py:19
  96.5 14.8 %shard_map.68 = bf16[8,16,4,32,128]{4,3,2,1,0:T(8,128)(2,1)} custom-call(s32[4]{0:T(128)} %get-tuple-element.16.slot_ref, bf16[4,1,512,512]{3,2,1,0:T(8,128)(2,1)} %own_re.3, bf16[4,1,512,512]{3,2,1,0:T(8,128)(2,1)} %own_im.3, bf16[4,1,512,512]{3,2,1,0:T(8,128)(2,1)} %collective-permute-done.far_re.rest_0_, ...), custom_call_target="tpu_custom_call" | custom-call | flops 8589934592 | bytes 15728640 | tf_op jit(solution)/shard_map/pallas_call | solution.py:84
  111.2 8.4 %copy.41 = bf16[128,4,32,128]{3,1,2,0:T(4,128)(2,1)} copy(bf16[128,4,32,128]{3,2,1,0:T(8,128)(2,1)} %bitcast.57) | data formatting | bytes 8388608 | tf_op jit(solution)/shard_map/reshape | solution.py:145
  119.6 10.3 %all-to-all-start = ((bf16[128,4,32,128]{3,1,2,0:T(4,128)(2,1)}), bf16[128,4,32,128]{3,1,2,0:T(4,128)(2,1)}, u32[]{:S(2)}, u32[]{:S(2)}) async-start(bf16[128,4,32,128]{3,1,2,0:T(4,128)(2,1)} %copy.41), calls=%async_computation | async-start | bytes 8388608 | tf_op jit(solution)/shard_map/all_to_all | solution.py:146
  129.9 14.8 %shard_map.69 = bf16[8,16,4,32,128]{4,3,2,1,0:T(8,128)(2,1)} custom-call(s32[4]{0:T(128)} %get-tuple-element.17.slot_ref, bf16[4,1,512,512]{3,2,1,0:T(8,128)(2,1)} %own_re.3, bf16[4,1,512,512]{3,2,1,0:T(8,128)(2,1)} %own_im.3, bf16[4,1,512,512]{3,2,1,0:T(8,128)(2,1)} %collective-permute-done.2.rest_0_.far_re, ...), custom_call_target="tpu_custom_call" | custom-call | flops 8589934592 | bytes 15728640 | tf_op jit(solution)/shard_map/pallas_call | solution.py:84
  144.7 8.4 %copy.48 = bf16[128,4,32,128]{3,1,2,0:T(4,128)(2,1)} copy(bf16[128,4,32,128]{3,2,1,0:T(8,128)(2,1)} %bitcast.56) | data formatting | bytes 8388608 | tf_op jit(solution)/shard_map/reshape | solution.py:145
  153.1 0.0 copy-start.4
  153.1 0.0 copy-start.5
  153.1 27.3 %all-to-all-done = bf16[128,4,32,128]{3,1,2,0:T(4,128)(2,1)} async-done(((bf16[128,4,32,128]{3,1,2,0:T(4,128)(2,1)}), bf16[128,4,32,128]{3,1,2,0:T(4,128)(2,1)}, u32[]{:S(2)}, u32[]{:S(2)}) %all-to-all-start) | async-done | bytes 4194336 | tf_op jit(solution)/shard_map/all_to_all | solution.py:146
  180.3 7.9 %all-to-all-start.1 = ((bf16[128,4,32,128]{3,1,2,0:T(4,128)(2,1)}), bf16[128,4,32,128]{3,1,2,0:T(4,128)(2,1)}, u32[]{:S(2)}, u32[]{:S(2)}) async-start(bf16[128,4,32,128]{3,1,2,0:T(4,128)(2,1)} %copy.48), calls=%async_computation.1 | async-start | bytes 8388608 | tf_op jit(solution)/shard_map/all_to_all | solution.py:146
  188.3 0.0 copy-done.4
  188.4 0.0 copy-done.5
  188.5 0.3 copy.44
  188.8 0.2 reshape.207
  189.1 0.3 copy.51
  189.3 0.2 reshape.211
  189.5 0.3 copy.53
  189.8 0.2 reshape.213
  190.0 0.3 copy.46
  190.2 0.2 reshape.209
  190.4 8.0 %copy.45 = bf16[128,4,32,128]{0,3,1,2:T(8,128)(2,1)} copy(bf16[128,4,32,128]{3,1,2,0:T(4,128)(2,1)} %all-to-all-done) | data formatting | bytes 8388608 | tf_op jit(solution)/shard_map/all_to_all | solution.py:146
  198.4 0.0 copy-start
  198.4 5.5 %convolution_bitcast_fusion.2 = f32[32,128,256]{2,1,0:T(8,128)} fusion(bf16[128,4,32,128]{0,3,1,2:T(8,128)(2,1)} %copy.45, bf16[128,4,256,1]{2,0,1,3:T(8,128)(2,1)S(1)} %reshape.209), kind=kOutput, calls=%fused_computation.2 | convolution fusion | flops 1073741824 | bytes 8650752 | tf_op jit(solution)/shard_map/swrn,swx->rnx/dot_general | solution.py:152
  203.9 0.0 copy-done
  203.9 3.2 %convolution_bitcast_fusion.3 = f32[32,128,256]{2,1,0:T(8,128)} fusion(bf16[128,4,32,128]{0,3,1,2:T(8,128)(2,1)S(1)} %copy-done, bf16[128,4,256,1]{2,0,1,3:T(8,128)(2,1)S(1)} %reshape.207), kind=kOutput, calls=%fused_computation.3 | convolution fusion | flops 1073741824 | bytes 8650752 | tf_op jit(solution)/shard_map/swrn,swx->rnx/dot_general | solution.py:151
  207.1 31.6 %all-to-all-done.1 = bf16[128,4,32,128]{3,1,2,0:T(4,128)(2,1)} async-done(((bf16[128,4,32,128]{3,1,2,0:T(4,128)(2,1)}), bf16[128,4,32,128]{3,1,2,0:T(4,128)(2,1)}, u32[]{:S(2)}, u32[]{:S(2)}) %all-to-all-start.1) | async-done | bytes 4194336 | tf_op jit(solution)/shard_map/all_to_all | solution.py:146
  238.7 8.0 %copy.52 = bf16[128,4,32,128]{0,3,1,2:T(8,128)(2,1)} copy(bf16[128,4,32,128]{3,1,2,0:T(4,128)(2,1)} %all-to-all-done.1) | data formatting | bytes 8388608 | tf_op jit(solution)/shard_map/all_to_all | solution.py:146
  246.7 0.0 copy-start.1
  246.7 3.6 %convolution_bitcast_fusion = f32[32,128,256]{2,1,0:T(8,128)S(1)} fusion(bf16[128,4,32,128]{0,3,1,2:T(8,128)(2,1)} %copy.52, bf16[128,4,256,1]{2,0,1,3:T(8,128)(2,1)S(1)} %reshape.213), kind=kOutput, calls=%fused_computation | convolution fusion | flops 1073741824 | bytes 8650752 | tf_op jit(solution)/shard_map/swrn,swx->rnx/dot_general | solution.py:152
  250.3 0.0 copy-done.1
  250.3 0.0 copy-start.2
  250.3 0.0 copy-start.3
  250.3 1.2 convolution_bitcast_fusion.1
  251.6 0.9 copy-done.2
  252.5 1.3 copy-done.3
  253.8 0.8 fusion
  254.6 2.1 reshape.206
  256.6 5.7 %fusion.14 = (f32[32,64,1,128]{3,2,1,0:T(1,128)}, f32[32,64,1,128]{3,2,1,0:T(1,128)}) fusion(f32[32,64,2,128]{3,2,1,0:T(2,128)} %reshape.206), kind=kLoop, calls=%fused_computation.42 | loop fusion | bytes 4194304 | tf_op jit(solution)/shard_map/slice | solution.py:157
  (11 shorter events, 0.2 us)
Async XLA Ops:
  0.6 48.9 %collective-permute-start.2 = (bf16[4,1,512,512]{3,2,1,0:T(8,128)(2,1)}, bf16[4,1,512,512]{3,2,1,0:T(8,128)(2,1)}, u32[]{:S(2)}, u32[]{:S(2)}) collective-permute-start(bf16[4,1,512,512]{3,2,1,0:T(8,128)(2,1)} %own_re.3), channel_id=1, source_target_pairs={{0,32},{32,0},{16,48},{48,16},{64,96},{96,64},{80,112},{112,80},{1... | collective-permute-start | bytes 6291464 | tf_op jit(solution)/shard_map/ppermute | solution.py:19
  2.6 50.4 %collective-permute-start = (bf16[4,1,512,512]{3,2,1,0:T(8,128)(2,1)}, bf16[4,1,512,512]{3,2,1,0:T(8,128)(2,1)}, u32[]{:S(2)}, u32[]{:S(2)}) collective-permute-start(bf16[4,1,512,512]{3,2,1,0:T(8,128)(2,1)} %own_re.3), channel_id=1, source_target_pairs={{0,16},{16,0},{32,48},{48,32},{64,80},{80,64},{96,112},{112,96},{1... | collective-permute-start | bytes 6291464 | tf_op jit(solution)/shard_map/ppermute | solution.py:19
  5.7 87.9 %collective-permute-start.3 = (bf16[4,1,512,512]{3,2,1,0:T(8,128)(2,1)}, bf16[4,1,512,512]{3,2,1,0:T(8,128)(2,1)}, u32[]{:S(2)}, u32[]{:S(2)}) collective-permute-start(bf16[4,1,512,512]{3,2,1,0:T(8,128)(2,1)} %own_im.3), channel_id=1, source_target_pairs={{0,32},{32,0},{16,48},{48,16},{64,96},{96,64},{80,112},{112,80},{1... | collective-permute-start | bytes 6291464 | tf_op jit(solution)/shard_map/ppermute | solution.py:19
  5.8 90.7 %collective-permute-start.1 = (bf16[4,1,512,512]{3,2,1,0:T(8,128)(2,1)}, bf16[4,1,512,512]{3,2,1,0:T(8,128)(2,1)}, u32[]{:S(2)}, u32[]{:S(2)}) collective-permute-start(bf16[4,1,512,512]{3,2,1,0:T(8,128)(2,1)} %own_im.3), channel_id=1, source_target_pairs={{0,16},{16,0},{32,48},{48,32},{64,80},{80,64},{96,112},{112,96},{1... | collective-permute-start | bytes 6291464 | tf_op jit(solution)/shard_map/ppermute | solution.py:19
  16.2 7.4 %copy-start.6 = (s32[2,4]{1,0:T(2,128)S(1)}, s32[2,4]{1,0:T(2,128)}, u32[]{:S(2)}) copy-start(s32[2,4]{1,0:T(2,128)} %param.7) | copy-start | bytes 100
  119.6 60.7 %all-to-all-start = ((bf16[128,4,32,128]{3,1,2,0:T(4,128)(2,1)}), bf16[128,4,32,128]{3,1,2,0:T(4,128)(2,1)}, u32[]{:S(2)}, u32[]{:S(2)}) async-start(bf16[128,4,32,128]{3,1,2,0:T(4,128)(2,1)} %copy.41), calls=%async_computation | async-start | bytes 8388608 | tf_op jit(solution)/shard_map/all_to_all | solution.py:146
  153.1 35.2 %copy-start.4 = (bf16[32,2,16,128]{3,2,1,0:T(8,128)(2,1)S(1)}, bf16[32,2,16,128]{3,2,1,0:T(8,128)(2,1)}, u32[]{:S(2)}) copy-start(bf16[32,2,16,128]{3,2,1,0:T(8,128)(2,1)} %param.8) | copy-start | bytes 786436
  153.1 35.3 %copy-start.5 = (bf16[32,2,16,128]{3,2,1,0:T(8,128)(2,1)S(1)}, bf16[32,2,16,128]{3,2,1,0:T(8,128)(2,1)}, u32[]{:S(2)}) copy-start(bf16[32,2,16,128]{3,2,1,0:T(8,128)(2,1)} %param.9) | copy-start | bytes 786436
  180.3 58.3 %all-to-all-start.1 = ((bf16[128,4,32,128]{3,1,2,0:T(4,128)(2,1)}), bf16[128,4,32,128]{3,1,2,0:T(4,128)(2,1)}, u32[]{:S(2)}, u32[]{:S(2)}) async-start(bf16[128,4,32,128]{3,1,2,0:T(4,128)(2,1)} %copy.48), calls=%async_computation.1 | async-start | bytes 8388608 | tf_op jit(solution)/shard_map/all_to_all | solution.py:146
  198.4 5.5 %copy-start = (bf16[128,4,32,128]{0,3,1,2:T(8,128)(2,1)S(1)}, bf16[128,4,32,128]{0,3,1,2:T(8,128)(2,1)}, u32[]{:S(2)}) copy-start(bf16[128,4,32,128]{0,3,1,2:T(8,128)(2,1)} %copy.45) | copy-start | bytes 12582916
  246.7 3.6 %copy-start.1 = (bf16[128,4,32,128]{0,3,1,2:T(8,128)(2,1)S(1)}, bf16[128,4,32,128]{0,3,1,2:T(8,128)(2,1)}, u32[]{:S(2)}) copy-start(bf16[128,4,32,128]{0,3,1,2:T(8,128)(2,1)} %copy.52) | copy-start | bytes 12582916
  250.3 2.2 copy-start.2
  250.3 3.5 %copy-start.3 = (f32[32,128,256]{2,1,0:T(8,128)S(1)}, f32[32,128,256]{2,1,0:T(8,128)}, u32[]{:S(2)}) copy-start(f32[32,128,256]{2,1,0:T(8,128)} %convolution_bitcast_fusion.3) | copy-start | bytes 12582916

commit v5 on v4

--- a/solution.py
+++ b/solution.py
@@ -153,8 +153,7 @@
         half = got.shape[3] // 2
         part = t_first[:, :half] + t_second[:, half:]
         volume = part if volume is None else volume + part
-    volume = volume.reshape(volume.shape[0], volume.shape[1], 2, depth_count)
-    return (volume[:, :, 0, :], volume[:, :, 1, :])
+    return (volume[:, :, :depth_count], volume[:, :, depth_count:])
 
 
 def solution(mesh):

time: 267 us -> 261 us (0.978)
  local copies, waits for them, and re-layouts: 46.2 us -> 40 us
    slice x1, local copies, waits for them, and re-layouts: 5.72 us -> 1.6 us  [shards(): return (volume[:, :, :depth_count], volume[:, :, depth_count:])]
  transfers between devices with their start and end apart: 6 -> 6, of which waited for: 6 -> 6; matrix products, arithmetic and copies ran while one was open for 17% -> 18% of each run, Pallas kernels for 6% -> 6%
where the time goes in v5:
time: 261 us; the launch traced here: 256 us
  waiting for transfers between devices  131 us (50%)
  local copies, waits for them, and re-layouts  40 us (15%)
  Pallas kernels  29.5 us (11%)
  starting transfers between devices  23.8 us (9%)
  other arithmetic  17.3 us (7%)
  matrix products  13.6 us (5%)
    ppermute x4, waiting for transfers between devices, from_partner(): return lax.ppermute(block, axis, route)  72.4 us
    all_to_all x2, waiting for transfers between devices, shards(): got = lax.all_to_all(send, ('wave', 'angle'), 0, 0, tiled=True)  58.8 us
    pallas_call x2, Pallas kernels, spectra(): pl.pallas_call(spectrum_kernel, out_shape=jax.ShapeDtypeStruct((blocks, g...  29.5 us
    all_to_all x2, starting transfers between devices, shards(): got = lax.all_to_all(send, ('wave', 'angle'), 0, 0, tiled=True)  18.2 us
    reshape x2, local copies, waits for them, and re-layouts, shards(): send = send.reshape(wave_devices * angle_devices, *send.shape[2:])  16.8 us
    all_to_all x2, local copies, waits for them, and re-layouts, shards(): got = lax.all_to_all(send, ('wave', 'angle'), 0, 0, tiled=True)  16 us
    convert_element_type x2, other arithmetic, dft_tables(): (-jnp.sin(phase) * factor).astype(jnp.bfloat16)  10.3 us
    dot_general x2, matrix products, shards(): jnp.einsum('swrn,swx->rnx', got, w_second, preferred_element_type=fp)  9.11 us
  transfers between devices with their start and end apart: 6, of which 6 were waited for; matrix products, arithmetic and copies ran while one was open for 18% of the time, Pallas kernels for 6%

profile of v5, /device:TPU:24, one launch (start us, length us, event | category | flops | bytes accessed | tf_op | source)
XLA Modules:
  0.0 256.3 jit_solution(11966017545125300125)
XLA Ops:
  0.6 2.0 collective-permute-start.2
  2.6 3.0 %collective-permute-start = (bf16[4,1,512,512]{3,2,1,0:T(8,128)(2,1)}, bf16[4,1,512,512]{3,2,1,0:T(8,128)(2,1)}, u32[]{:S(2)}, u32[]{:S(2)}) collective-permute-start(bf16[4,1,512,512]{3,2,1,0:T(8,128)(2,1)} %own_re.3), channel_id=1, source_target_pairs={{0,16},{16,0},{32,48},{48,32},{64,80},{80,64},{96,112},{112,96},{1... | collective-permute-start | bytes 6291464 | tf_op jit(solution)/shard_map/ppermute | solution.py:19
  5.7 0.1 collective-permute-start.3
  5.8 0.5 collective-permute-start.1
  6.3 4.3 %fusion.13 = bf16[512,8,1,64]{0,3,2,1:T(8,128)(2,1)S(1)} fusion(s32[8,64]{1,0:T(8,128)S(1)} %multiply_add_fusion), kind=kLoop, calls=%fused_computation.36 | loop fusion | flops 5242880 | bytes 526336 | tf_op jit(solution)/shard_map/neg | solution.py:43
  10.6 4.9 %multiply_convert_fusion.2 = (bf16[512,8,1,64]{0,3,2,1:T(8,128)(2,1)S(1)}, bf16[512,8,1,64]{0,3,2,1:T(8,128)(2,1)S(1)}) fusion(s32[8,64]{1,0:T(8,128)S(1)} %multiply_add_fusion), kind=kLoop, calls=%fused_computation.26 | loop fusion | flops 4980736 | bytes 1050624 | tf_op jit(solution)/shard_map/convert_element_type | solution.py:29
  15.5 0.2 pad_maximum_fusion.1
  15.7 0.5 copy.33
  16.2 0.0 copy-start.6
  16.2 0.5 copy.34
  16.8 5.3 %multiply_convert_fusion = (bf16[512,512]{1,0:T(8,128)(2,1)}, bf16[512,512]{1,0:T(8,128)(2,1)}) fusion(), kind=kLoop, calls=%fused_computation.22 | loop fusion | flops 4980736 | bytes 1048576 | tf_op jit(solution)/shard_map/convert_element_type | solution.py:29
  22.1 1.5 pad_maximum_fusion.col_a
  23.6 0.0 copy-done.6
  23.6 0.5 slice_bitcast_fusion.1
  24.1 25.4 %collective-permute-done.2.rest_0_.far_re = bf16[4,1,512,512]{3,2,1,0:T(8,128)(2,1)} collective-permute-done((bf16[4,1,512,512]{3,2,1,0:T(8,128)(2,1)}, bf16[4,1,512,512]{3,2,1,0:T(8,128)(2,1)}, u32[]{:S(2)}, u32[]{:S(2)}) %collective-permute-start.2) | collective-permute-done | bytes 2097184 | tf_op jit(solution)/shard_map/ppermute | solution.py:19
  49.5 3.5 %collective-permute-done.far_re.rest_0_ = bf16[4,1,512,512]{3,2,1,0:T(8,128)(2,1)} collective-permute-done((bf16[4,1,512,512]{3,2,1,0:T(8,128)(2,1)}, bf16[4,1,512,512]{3,2,1,0:T(8,128)(2,1)}, u32[]{:S(2)}, u32[]{:S(2)}) %collective-permute-start) | collective-permute-done | bytes 2097184 | tf_op jit(solution)/shard_map/ppermute | solution.py:19
  53.0 40.5 %collective-permute-done.3.rest_1_.far_im = bf16[4,1,512,512]{3,2,1,0:T(8,128)(2,1)} collective-permute-done((bf16[4,1,512,512]{3,2,1,0:T(8,128)(2,1)}, bf16[4,1,512,512]{3,2,1,0:T(8,128)(2,1)}, u32[]{:S(2)}, u32[]{:S(2)}) %collective-permute-start.3) | collective-permute-done | bytes 2097184 | tf_op jit(solution)/shard_map/ppermute | solution.py:19
  93.5 3.0 %collective-permute-done.1.far_im.rest_1_ = bf16[4,1,512,512]{3,2,1,0:T(8,128)(2,1)} collective-permute-done((bf16[4,1,512,512]{3,2,1,0:T(8,128)(2,1)}, bf16[4,1,512,512]{3,2,1,0:T(8,128)(2,1)}, u32[]{:S(2)}, u32[]{:S(2)}) %collective-permute-start.1) | collective-permute-done | bytes 2097184 | tf_op jit(solution)/shard_map/ppermute | solution.py:19
  96.5 14.8 %shard_map.68 = bf16[8,16,4,32,128]{4,3,2,1,0:T(8,128)(2,1)} custom-call(s32[4]{0:T(128)} %get-tuple-element.16.slot_ref, bf16[4,1,512,512]{3,2,1,0:T(8,128)(2,1)} %own_re.3, bf16[4,1,512,512]{3,2,1,0:T(8,128)(2,1)} %own_im.3, bf16[4,1,512,512]{3,2,1,0:T(8,128)(2,1)} %collective-permute-done.far_re.rest_0_, ...), custom_call_target="tpu_custom_call" | custom-call | flops 8589934592 | bytes 15728640 | tf_op jit(solution)/shard_map/pallas_call | solution.py:84
  111.2 8.4 %copy.35 = bf16[128,4,32,128]{3,1,2,0:T(4,128)(2,1)} copy(bf16[128,4,32,128]{3,2,1,0:T(8,128)(2,1)} %bitcast.51) | data formatting | bytes 8388608 | tf_op jit(solution)/shard_map/reshape | solution.py:145
  119.6 10.3 %all-to-all-start = ((bf16[128,4,32,128]{3,1,2,0:T(4,128)(2,1)}), bf16[128,4,32,128]{3,1,2,0:T(4,128)(2,1)}, u32[]{:S(2)}, u32[]{:S(2)}) async-start(bf16[128,4,32,128]{3,1,2,0:T(4,128)(2,1)} %copy.35), calls=%async_computation | async-start | bytes 8388608 | tf_op jit(solution)/shard_map/all_to_all | solution.py:146
  129.9 14.8 %shard_map.69 = bf16[8,16,4,32,128]{4,3,2,1,0:T(8,128)(2,1)} custom-call(s32[4]{0:T(128)} %get-tuple-element.17.slot_ref, bf16[4,1,512,512]{3,2,1,0:T(8,128)(2,1)} %own_re.3, bf16[4,1,512,512]{3,2,1,0:T(8,128)(2,1)} %own_im.3, bf16[4,1,512,512]{3,2,1,0:T(8,128)(2,1)} %collective-permute-done.2.rest_0_.far_re, ...), custom_call_target="tpu_custom_call" | custom-call | flops 8589934592 | bytes 15728640 | tf_op jit(solution)/shard_map/pallas_call | solution.py:84
  144.7 8.4 %copy.42 = bf16[128,4,32,128]{3,1,2,0:T(4,128)(2,1)} copy(bf16[128,4,32,128]{3,2,1,0:T(8,128)(2,1)} %bitcast.50) | data formatting | bytes 8388608 | tf_op jit(solution)/shard_map/reshape | solution.py:145
  153.1 0.0 copy-start.4
  153.1 0.0 copy-start.5
  153.1 27.3 %all-to-all-done = bf16[128,4,32,128]{3,1,2,0:T(4,128)(2,1)} async-done(((bf16[128,4,32,128]{3,1,2,0:T(4,128)(2,1)}), bf16[128,4,32,128]{3,1,2,0:T(4,128)(2,1)}, u32[]{:S(2)}, u32[]{:S(2)}) %all-to-all-start) | async-done | bytes 4194336 | tf_op jit(solution)/shard_map/all_to_all | solution.py:146
  180.3 7.9 %all-to-all-start.1 = ((bf16[128,4,32,128]{3,1,2,0:T(4,128)(2,1)}), bf16[128,4,32,128]{3,1,2,0:T(4,128)(2,1)}, u32[]{:S(2)}, u32[]{:S(2)}) async-start(bf16[128,4,32,128]{3,1,2,0:T(4,128)(2,1)} %copy.42), calls=%async_computation.1 | async-start | bytes 8388608 | tf_op jit(solution)/shard_map/all_to_all | solution.py:146
  188.3 0.0 copy-done.4
  188.4 0.0 copy-done.5
  188.5 0.3 copy.38
  188.8 0.2 reshape.203
  189.1 0.3 copy.45
  189.3 0.2 reshape.207
  189.5 0.3 copy.47
  189.8 0.2 reshape.209
  190.0 0.3 copy.40
  190.2 0.2 reshape.205
  190.4 8.0 %copy.39 = bf16[128,4,32,128]{0,3,1,2:T(8,128)(2,1)} copy(bf16[128,4,32,128]{3,1,2,0:T(4,128)(2,1)} %all-to-all-done) | data formatting | bytes 8388608 | tf_op jit(solution)/shard_map/all_to_all | solution.py:146
  198.4 0.0 copy-start
  198.4 5.5 %convolution_bitcast_fusion.2 = f32[32,128,256]{2,1,0:T(8,128)} fusion(bf16[128,4,32,128]{0,3,1,2:T(8,128)(2,1)} %copy.39, bf16[128,4,256,1]{2,0,1,3:T(8,128)(2,1)S(1)} %reshape.205), kind=kOutput, calls=%fused_computation.2 | convolution fusion | flops 1073741824 | bytes 8650752 | tf_op jit(solution)/shard_map/swrn,swx->rnx/dot_general | solution.py:152
  203.9 0.0 copy-done
  203.9 3.2 %convolution_bitcast_fusion.3 = f32[32,128,256]{2,1,0:T(8,128)} fusion(bf16[128,4,32,128]{0,3,1,2:T(8,128)(2,1)S(1)} %copy-done, bf16[128,4,256,1]{2,0,1,3:T(8,128)(2,1)S(1)} %reshape.203), kind=kOutput, calls=%fused_computation.3 | convolution fusion | flops 1073741824 | bytes 8650752 | tf_op jit(solution)/shard_map/swrn,swx->rnx/dot_general | solution.py:151
  207.1 31.6 %all-to-all-done.1 = bf16[128,4,32,128]{3,1,2,0:T(4,128)(2,1)} async-done(((bf16[128,4,32,128]{3,1,2,0:T(4,128)(2,1)}), bf16[128,4,32,128]{3,1,2,0:T(4,128)(2,1)}, u32[]{:S(2)}, u32[]{:S(2)}) %all-to-all-start.1) | async-done | bytes 4194336 | tf_op jit(solution)/shard_map/all_to_all | solution.py:146
  238.7 8.0 %copy.46 = bf16[128,4,32,128]{0,3,1,2:T(8,128)(2,1)} copy(bf16[128,4,32,128]{3,1,2,0:T(4,128)(2,1)} %all-to-all-done.1) | data formatting | bytes 8388608 | tf_op jit(solution)/shard_map/all_to_all | solution.py:146
  246.7 0.0 copy-start.1
  246.7 3.6 %convolution_bitcast_fusion = f32[32,128,256]{2,1,0:T(8,128)S(1)} fusion(bf16[128,4,32,128]{0,3,1,2:T(8,128)(2,1)} %copy.46, bf16[128,4,256,1]{2,0,1,3:T(8,128)(2,1)S(1)} %reshape.209), kind=kOutput, calls=%fused_computation | convolution fusion | flops 1073741824 | bytes 8650752 | tf_op jit(solution)/shard_map/swrn,swx->rnx/dot_general | solution.py:152
  250.3 0.0 copy-done.1
  250.3 0.0 copy-start.2
  250.3 0.0 copy-start.3
  250.3 1.2 convolution_bitcast_fusion.1
  251.6 0.9 copy-done.2
  252.5 1.3 copy-done.3
  253.8 1.0 fusion
  254.7 1.6 fusion.14
  (11 shorter events, 0.2 us)
Async XLA Ops:
  0.6 48.9 %collective-permute-start.2 = (bf16[4,1,512,512]{3,2,1,0:T(8,128)(2,1)}, bf16[4,1,512,512]{3,2,1,0:T(8,128)(2,1)}, u32[]{:S(2)}, u32[]{:S(2)}) collective-permute-start(bf16[4,1,512,512]{3,2,1,0:T(8,128)(2,1)} %own_re.3), channel_id=1, source_target_pairs={{0,32},{32,0},{16,48},{48,16},{64,96},{96,64},{80,112},{112,80},{1... | collective-permute-start | bytes 6291464 | tf_op jit(solution)/shard_map/ppermute | solution.py:19
  2.6 50.4 %collective-permute-start = (bf16[4,1,512,512]{3,2,1,0:T(8,128)(2,1)}, bf16[4,1,512,512]{3,2,1,0:T(8,128)(2,1)}, u32[]{:S(2)}, u32[]{:S(2)}) collective-permute-start(bf16[4,1,512,512]{3,2,1,0:T(8,128)(2,1)} %own_re.3), channel_id=1, source_target_pairs={{0,16},{16,0},{32,48},{48,32},{64,80},{80,64},{96,112},{112,96},{1... | collective-permute-start | bytes 6291464 | tf_op jit(solution)/shard_map/ppermute | solution.py:19
  5.7 87.9 %collective-permute-start.3 = (bf16[4,1,512,512]{3,2,1,0:T(8,128)(2,1)}, bf16[4,1,512,512]{3,2,1,0:T(8,128)(2,1)}, u32[]{:S(2)}, u32[]{:S(2)}) collective-permute-start(bf16[4,1,512,512]{3,2,1,0:T(8,128)(2,1)} %own_im.3), channel_id=1, source_target_pairs={{0,32},{32,0},{16,48},{48,16},{64,96},{96,64},{80,112},{112,80},{1... | collective-permute-start | bytes 6291464 | tf_op jit(solution)/shard_map/ppermute | solution.py:19
  5.8 90.7 %collective-permute-start.1 = (bf16[4,1,512,512]{3,2,1,0:T(8,128)(2,1)}, bf16[4,1,512,512]{3,2,1,0:T(8,128)(2,1)}, u32[]{:S(2)}, u32[]{:S(2)}) collective-permute-start(bf16[4,1,512,512]{3,2,1,0:T(8,128)(2,1)} %own_im.3), channel_id=1, source_target_pairs={{0,16},{16,0},{32,48},{48,32},{64,80},{80,64},{96,112},{112,96},{1... | collective-permute-start | bytes 6291464 | tf_op jit(solution)/shard_map/ppermute | solution.py:19
  16.2 7.4 %copy-start.6 = (s32[2,4]{1,0:T(2,128)S(1)}, s32[2,4]{1,0:T(2,128)}, u32[]{:S(2)}) copy-start(s32[2,4]{1,0:T(2,128)} %param.7) | copy-start | bytes 100
  119.6 60.7 %all-to-all-start = ((bf16[128,4,32,128]{3,1,2,0:T(4,128)(2,1)}), bf16[128,4,32,128]{3,1,2,0:T(4,128)(2,1)}, u32[]{:S(2)}, u32[]{:S(2)}) async-start(bf16[128,4,32,128]{3,1,2,0:T(4,128)(2,1)} %copy.35), calls=%async_computation | async-start | bytes 8388608 | tf_op jit(solution)/shard_map/all_to_all | solution.py:146
  153.1 35.2 %copy-start.4 = (bf16[32,2,16,128]{3,2,1,0:T(8,128)(2,1)S(1)}, bf16[32,2,16,128]{3,2,1,0:T(8,128)(2,1)}, u32[]{:S(2)}) copy-start(bf16[32,2,16,128]{3,2,1,0:T(8,128)(2,1)} %param.8) | copy-start | bytes 786436
  153.1 35.3 %copy-start.5 = (bf16[32,2,16,128]{3,2,1,0:T(8,128)(2,1)S(1)}, bf16[32,2,16,128]{3,2,1,0:T(8,128)(2,1)}, u32[]{:S(2)}) copy-start(bf16[32,2,16,128]{3,2,1,0:T(8,128)(2,1)} %param.9) | copy-start | bytes 786436
  180.3 58.3 %all-to-all-start.1 = ((bf16[128,4,32,128]{3,1,2,0:T(4,128)(2,1)}), bf16[128,4,32,128]{3,1,2,0:T(4,128)(2,1)}, u32[]{:S(2)}, u32[]{:S(2)}) async-start(bf16[128,4,32,128]{3,1,2,0:T(4,128)(2,1)} %copy.42), calls=%async_computation.1 | async-start | bytes 8388608 | tf_op jit(solution)/shard_map/all_to_all | solution.py:146
  198.4 5.5 %copy-start = (bf16[128,4,32,128]{0,3,1,2:T(8,128)(2,1)S(1)}, bf16[128,4,32,128]{0,3,1,2:T(8,128)(2,1)}, u32[]{:S(2)}) copy-start(bf16[128,4,32,128]{0,3,1,2:T(8,128)(2,1)} %copy.39) | copy-start | bytes 12582916
  246.7 3.6 %copy-start.1 = (bf16[128,4,32,128]{0,3,1,2:T(8,128)(2,1)S(1)}, bf16[128,4,32,128]{0,3,1,2:T(8,128)(2,1)}, u32[]{:S(2)}) copy-start(bf16[128,4,32,128]{0,3,1,2:T(8,128)(2,1)} %copy.46) | copy-start | bytes 12582916
  250.3 2.2 copy-start.2
  250.3 3.5 %copy-start.3 = (f32[32,128,256]{2,1,0:T(8,128)S(1)}, f32[32,128,256]{2,1,0:T(8,128)}, u32[]{:S(2)}) copy-start(f32[32,128,256]{2,1,0:T(8,128)} %convolution_bitcast_fusion.3) | copy-start | bytes 12582916

commit v6 on v5

--- a/solution.py
+++ b/solution.py
@@ -5,6 +5,7 @@
 import jax.numpy as jnp
 from jax import lax
 from jax.experimental import pallas as pl
+from jax.experimental.layout import Layout, with_layout_constraint
 from jax.experimental.pallas import tpu as pltpu
 from jax.sharding import PartitionSpec as P
 
@@ -144,6 +145,7 @@
         )
         send = send.reshape(wave_devices * angle_devices, *send.shape[2:])
         got = lax.all_to_all(send, ("wave", "angle"), 0, 0, tiled=True)
+        got = with_layout_constraint(got, Layout(tuple(range(got.ndim))))
         kr = k_re[section_number]
         ki = k_im[section_number]
         w_first = jnp.stack([kr, ki], axis=2).reshape(kr.shape[0], kr.shape[1], -1)

time: 261 us -> 252 us (0.966)
  local copies, waits for them, and re-layouts: 40 us -> 5.13 us
  matrix products: 13.6 us -> 33.1 us
  waiting for transfers between devices: 131 us -> 138 us
    reshape x2 -> x0, local copies, waits for them, and re-layouts: 16.8 us -> none  [shards(): send = send.reshape(wave_devices * angle_devices, *send.shape[2:])]
    all_to_all x2 -> x0, local copies, waits for them, and re-layouts: 16 us -> none  [shards(): got = lax.all_to_all(send, ('wave', 'angle'), 0, 0, tiled=True)]
    dot_general x2, matrix products: 4.45 us -> 16.7 us  [shards(): jnp.einsum('swrn,swx->rnx', got, w_first, preferred_element_type=fp)]
    dot_general x2, matrix products: 9.11 us -> 16.3 us  [shards(): jnp.einsum('swrn,swx->rnx', got, w_second, preferred_element_type=fp)]
    all_to_all x2, waiting for transfers between devices: 58.8 us -> 65.4 us  [shards(): got = lax.all_to_all(send, ('wave', 'angle'), 0, 0, tiled=True)]
  transfers between devices with their start and end apart: 6 -> 6, of which waited for: 6 -> 6; matrix products, arithmetic and copies ran while one was open for 18% -> 15% of each run, Pallas kernels for 6% -> 6%
where the time goes in v6:
time: 252 us; the launch traced here: 248 us
  waiting for transfers between devices  138 us (55%)
  matrix products  33.1 us (13%)
  Pallas kernels  29.6 us (12%)
  starting transfers between devices  24.1 us (10%)
  other arithmetic  17.3 us (7%)
  local copies, waits for them, and re-layouts  5.13 us (2%)
    ppermute x4, waiting for transfers between devices, from_partner(): return lax.ppermute(block, axis, route)  72.3 us
    all_to_all x2, waiting for transfers between devices, shards(): got = lax.all_to_all(send, ('wave', 'angle'), 0, 0, tiled=True)  65.4 us
    pallas_call x2, Pallas kernels, spectra(): pl.pallas_call(spectrum_kernel, out_shape=jax.ShapeDtypeStruct((blocks, g...  29.6 us
    all_to_all x2, starting transfers between devices, shards(): got = lax.all_to_all(send, ('wave', 'angle'), 0, 0, tiled=True)  18.5 us
    dot_general x2, matrix products, shards(): jnp.einsum('swrn,swx->rnx', got, w_first, preferred_element_type=fp)  16.7 us
    dot_general x2, matrix products, shards(): jnp.einsum('swrn,swx->rnx', got, w_second, preferred_element_type=fp)  16.3 us
    convert_element_type x2, other arithmetic, dft_tables(): (-jnp.sin(phase) * factor).astype(jnp.bfloat16)  10.3 us
    ppermute x4, starting transfers between devices, from_partner(): return lax.ppermute(block, axis, route)  5.64 us
  transfers between devices with their start and end apart: 6, of which 6 were waited for; matrix products, arithmetic and copies ran while one was open for 15% of the time, Pallas kernels for 6%

profile of v6, /device:TPU:24, one launch (start us, length us, event | category | flops | bytes accessed | tf_op | source)
XLA Modules:
  0.0 247.8 jit_solution(5919625795730606237)
XLA Ops:
  0.6 2.0 collective-permute-start.2
  2.6 3.0 %collective-permute-start = (bf16[4,1,512,512]{3,2,1,0:T(8,128)(2,1)}, bf16[4,1,512,512]{3,2,1,0:T(8,128)(2,1)}, u32[]{:S(2)}, u32[]{:S(2)}) collective-permute-start(bf16[4,1,512,512]{3,2,1,0:T(8,128)(2,1)} %own_re.3), channel_id=1, source_target_pairs={{0,16},{16,0},{32,48},{48,32},{64,80},{80,64},{96,112},{112,96},{1... | collective-permute-start | bytes 6291464 | tf_op jit(solution)/shard_map/ppermute | solution.py:20
  5.7 0.1 collective-permute-start.3
  5.8 0.5 collective-permute-start.1
  6.3 4.3 %fusion.33 = bf16[512,8,1,64]{0,3,2,1:T(8,128)(2,1)S(1)} fusion(s32[8,64]{1,0:T(8,128)S(1)} %multiply_add_fusion), kind=kLoop, calls=%fused_computation.44 | loop fusion | flops 5242880 | bytes 526336 | tf_op jit(solution)/shard_map/neg | solution.py:44
  10.6 4.9 %multiply_convert_fusion.2 = (bf16[512,8,1,64]{0,3,2,1:T(8,128)(2,1)S(1)}, bf16[512,8,1,64]{0,3,2,1:T(8,128)(2,1)S(1)}) fusion(s32[8,64]{1,0:T(8,128)S(1)} %multiply_add_fusion), kind=kLoop, calls=%fused_computation.34 | loop fusion | flops 4980736 | bytes 1050624 | tf_op jit(solution)/shard_map/convert_element_type | solution.py:30
  15.5 0.2 pad_maximum_fusion.1
  15.7 0.5 copy.25
  16.2 0.0 copy-start.4
  16.2 0.5 copy.26
  16.8 5.3 %multiply_convert_fusion = (bf16[512,512]{1,0:T(8,128)(2,1)}, bf16[512,512]{1,0:T(8,128)(2,1)}) fusion(), kind=kLoop, calls=%fused_computation.30 | loop fusion | flops 4980736 | bytes 1048576 | tf_op jit(solution)/shard_map/convert_element_type | solution.py:30
  22.1 1.5 pad_maximum_fusion.col_a
  23.6 0.0 copy-done.4
  23.6 0.6 slice_bitcast_fusion.1
  24.2 25.3 %collective-permute-done.2.rest_0_.far_re = bf16[4,1,512,512]{3,2,1,0:T(8,128)(2,1)} collective-permute-done((bf16[4,1,512,512]{3,2,1,0:T(8,128)(2,1)}, bf16[4,1,512,512]{3,2,1,0:T(8,128)(2,1)}, u32[]{:S(2)}, u32[]{:S(2)}) %collective-permute-start.2) | collective-permute-done | bytes 2097184 | tf_op jit(solution)/shard_map/ppermute | solution.py:20
  49.5 3.5 %collective-permute-done.far_re.rest_0_ = bf16[4,1,512,512]{3,2,1,0:T(8,128)(2,1)} collective-permute-done((bf16[4,1,512,512]{3,2,1,0:T(8,128)(2,1)}, bf16[4,1,512,512]{3,2,1,0:T(8,128)(2,1)}, u32[]{:S(2)}, u32[]{:S(2)}) %collective-permute-start) | collective-permute-done | bytes 2097184 | tf_op jit(solution)/shard_map/ppermute | solution.py:20
  53.0 40.5 %collective-permute-done.3.rest_1_.far_im = bf16[4,1,512,512]{3,2,1,0:T(8,128)(2,1)} collective-permute-done((bf16[4,1,512,512]{3,2,1,0:T(8,128)(2,1)}, bf16[4,1,512,512]{3,2,1,0:T(8,128)(2,1)}, u32[]{:S(2)}, u32[]{:S(2)}) %collective-permute-start.3) | collective-permute-done | bytes 2097184 | tf_op jit(solution)/shard_map/ppermute | solution.py:20
  93.5 3.0 %collective-permute-done.1.far_im.rest_1_ = bf16[4,1,512,512]{3,2,1,0:T(8,128)(2,1)} collective-permute-done((bf16[4,1,512,512]{3,2,1,0:T(8,128)(2,1)}, bf16[4,1,512,512]{3,2,1,0:T(8,128)(2,1)}, u32[]{:S(2)}, u32[]{:S(2)}) %collective-permute-start.1) | collective-permute-done | bytes 2097184 | tf_op jit(solution)/shard_map/ppermute | solution.py:20
  96.5 14.8 %shard_map.68 = bf16[8,16,4,32,128]{4,3,2,1,0:T(8,128)(2,1)} custom-call(s32[4]{0:T(128)} %get-tuple-element.16.slot_ref, bf16[4,1,512,512]{3,2,1,0:T(8,128)(2,1)} %own_re.3, bf16[4,1,512,512]{3,2,1,0:T(8,128)(2,1)} %own_im.3, bf16[4,1,512,512]{3,2,1,0:T(8,128)(2,1)} %collective-permute-done.far_re.rest_0_, ...), custom_call_target="tpu_custom_call" | custom-call | flops 8589934592 | bytes 15728640 | tf_op jit(solution)/shard_map/pallas_call | solution.py:85
  111.2 10.3 %all-to-all-start = ((bf16[128,4,32,128]{3,2,1,0:T(8,128)(2,1)}), bf16[128,4,32,128]{3,2,1,0:T(8,128)(2,1)}, u32[]{:S(2)}, u32[]{:S(2)}) async-start(bf16[128,4,32,128]{3,2,1,0:T(8,128)(2,1)} %bitcast.47), calls=%async_computation | async-start | bytes 8388608 | tf_op jit(solution)/shard_map/all_to_all | solution.py:147
  121.5 14.8 %shard_map.69 = bf16[8,16,4,32,128]{4,3,2,1,0:T(8,128)(2,1)} custom-call(s32[4]{0:T(128)} %get-tuple-element.17.slot_ref, bf16[4,1,512,512]{3,2,1,0:T(8,128)(2,1)} %own_re.3, bf16[4,1,512,512]{3,2,1,0:T(8,128)(2,1)} %own_im.3, bf16[4,1,512,512]{3,2,1,0:T(8,128)(2,1)} %collective-permute-done.2.rest_0_.far_re, ...), custom_call_target="tpu_custom_call" | custom-call | flops 8589934592 | bytes 15728640 | tf_op jit(solution)/shard_map/pallas_call | solution.py:85
  136.3 35.6 %all-to-all-done = bf16[128,4,32,128]{3,2,1,0:T(8,128)(2,1)} async-done(((bf16[128,4,32,128]{3,2,1,0:T(8,128)(2,1)}), bf16[128,4,32,128]{3,2,1,0:T(8,128)(2,1)}, u32[]{:S(2)}, u32[]{:S(2)}) %all-to-all-start) | async-done | bytes 4194336 | tf_op jit(solution)/shard_map/all_to_all | solution.py:147
  171.9 0.0 copy-start.2
  172.0 0.0 copy-start.3
  172.0 8.2 %all-to-all-start.1 = ((bf16[128,4,32,128]{3,2,1,0:T(8,128)(2,1)}), bf16[128,4,32,128]{3,2,1,0:T(8,128)(2,1)}, u32[]{:S(2)}, u32[]{:S(2)}) async-start(bf16[128,4,32,128]{3,2,1,0:T(8,128)(2,1)} %bitcast.46), calls=%async_computation.1 | async-start | bytes 8388608 | tf_op jit(solution)/shard_map/all_to_all | solution.py:147
  180.2 0.0 copy-done.2
  180.3 0.0 copy-done.3
  180.4 0.3 copy.29
  180.7 0.2 reshape.203
  180.9 0.1 pad_maximum_fusion.5
  181.0 0.3 copy.35
  181.3 0.2 reshape.207
  181.4 0.3 copy.37
  181.7 0.2 reshape.209
  181.9 0.3 copy.31
  182.2 0.2 reshape.205
  182.3 9.1 %fusion.11 = f32[32,128,256]{2,1,0:T(8,128)} fusion(bf16[128,4,256,1]{2,0,1,3:T(8,128)(2,1)S(1)} %reshape.205, bf16[128,4,32,128]{3,2,1,0:T(8,128)(2,1)} %all-to-all-done), kind=kOutput, calls=%fused_computation.9 | convolution fusion | flops 1073741824 | bytes 8650752 | tf_op jit(solution)/shard_map/swrn,swx->rnx/dot_general | solution.py:154
  191.4 9.3 %fusion.8 = f32[32,128,256]{2,1,0:T(8,128)} fusion(bf16[128,4,256,1]{2,0,1,3:T(8,128)(2,1)S(1)} %reshape.203, bf16[128,4,32,128]{3,2,1,0:T(8,128)(2,1)} %all-to-all-done), kind=kOutput, calls=%fused_computation.8 | convolution fusion | flops 1073741824 | bytes 8650752 | tf_op jit(solution)/shard_map/swrn,swx->rnx/dot_general | solution.py:153
  200.7 29.7 %all-to-all-done.1 = bf16[128,4,32,128]{3,2,1,0:T(8,128)(2,1)} async-done(((bf16[128,4,32,128]{3,2,1,0:T(8,128)(2,1)}), bf16[128,4,32,128]{3,2,1,0:T(8,128)(2,1)}, u32[]{:S(2)}, u32[]{:S(2)}) %all-to-all-start.1) | async-done | bytes 4194336 | tf_op jit(solution)/shard_map/all_to_all | solution.py:147
  230.4 7.3 %fusion.17 = f32[32,128,256]{2,1,0:T(8,128)S(1)} fusion(bf16[128,4,256,1]{2,0,1,3:T(8,128)(2,1)S(1)} %reshape.209, bf16[128,4,32,128]{3,2,1,0:T(8,128)(2,1)} %all-to-all-done.1), kind=kOutput, calls=%fused_computation.11 | convolution fusion | flops 1073741824 | bytes 8650752 | tf_op jit(solution)/shard_map/swrn,swx->rnx/dot_general | solution.py:154
  237.7 0.0 copy-start
  237.7 0.0 copy-start.1
  237.7 7.5 %fusion.14 = f32[32,128,256]{2,1,0:T(8,128)S(1)} fusion(bf16[128,4,256,1]{2,0,1,3:T(8,128)(2,1)S(1)} %reshape.207, bf16[128,4,32,128]{3,2,1,0:T(8,128)(2,1)} %all-to-all-done.1), kind=kOutput, calls=%fused_computation.10 | convolution fusion | flops 1073741824 | bytes 8650752 | tf_op jit(solution)/shard_map/swrn,swx->rnx/dot_general | solution.py:153
  245.2 0.0 copy-done
  245.2 0.0 copy-done.1
  245.2 1.0 fusion.20
  246.2 1.6 fusion.34
  (10 shorter events, 0.2 us)
Async XLA Ops:
  0.6 48.9 %collective-permute-start.2 = (bf16[4,1,512,512]{3,2,1,0:T(8,128)(2,1)}, bf16[4,1,512,512]{3,2,1,0:T(8,128)(2,1)}, u32[]{:S(2)}, u32[]{:S(2)}) collective-permute-start(bf16[4,1,512,512]{3,2,1,0:T(8,128)(2,1)} %own_re.3), channel_id=1, source_target_pairs={{0,32},{32,0},{16,48},{48,16},{64,96},{96,64},{80,112},{112,80},{1... | collective-permute-start | bytes 6291464 | tf_op jit(solution)/shard_map/ppermute | solution.py:20
  2.6 50.4 %collective-permute-start = (bf16[4,1,512,512]{3,2,1,0:T(8,128)(2,1)}, bf16[4,1,512,512]{3,2,1,0:T(8,128)(2,1)}, u32[]{:S(2)}, u32[]{:S(2)}) collective-permute-start(bf16[4,1,512,512]{3,2,1,0:T(8,128)(2,1)} %own_re.3), channel_id=1, source_target_pairs={{0,16},{16,0},{32,48},{48,32},{64,80},{80,64},{96,112},{112,96},{1... | collective-permute-start | bytes 6291464 | tf_op jit(solution)/shard_map/ppermute | solution.py:20
  5.7 87.9 %collective-permute-start.3 = (bf16[4,1,512,512]{3,2,1,0:T(8,128)(2,1)}, bf16[4,1,512,512]{3,2,1,0:T(8,128)(2,1)}, u32[]{:S(2)}, u32[]{:S(2)}) collective-permute-start(bf16[4,1,512,512]{3,2,1,0:T(8,128)(2,1)} %own_im.3), channel_id=1, source_target_pairs={{0,32},{32,0},{16,48},{48,16},{64,96},{96,64},{80,112},{112,80},{1... | collective-permute-start | bytes 6291464 | tf_op jit(solution)/shard_map/ppermute | solution.py:20
  5.8 90.7 %collective-permute-start.1 = (bf16[4,1,512,512]{3,2,1,0:T(8,128)(2,1)}, bf16[4,1,512,512]{3,2,1,0:T(8,128)(2,1)}, u32[]{:S(2)}, u32[]{:S(2)}) collective-permute-start(bf16[4,1,512,512]{3,2,1,0:T(8,128)(2,1)} %own_im.3), channel_id=1, source_target_pairs={{0,16},{16,0},{32,48},{48,32},{64,80},{80,64},{96,112},{112,96},{1... | collective-permute-start | bytes 6291464 | tf_op jit(solution)/shard_map/ppermute | solution.py:20
  16.2 7.4 %copy-start.4 = (s32[2,4]{1,0:T(2,128)S(1)}, s32[2,4]{1,0:T(2,128)}, u32[]{:S(2)}) copy-start(s32[2,4]{1,0:T(2,128)} %param.7) | copy-start | bytes 100
  111.2 60.7 %all-to-all-start = ((bf16[128,4,32,128]{3,2,1,0:T(8,128)(2,1)}), bf16[128,4,32,128]{3,2,1,0:T(8,128)(2,1)}, u32[]{:S(2)}, u32[]{:S(2)}) async-start(bf16[128,4,32,128]{3,2,1,0:T(8,128)(2,1)} %bitcast.47), calls=%async_computation | async-start | bytes 8388608 | tf_op jit(solution)/shard_map/all_to_all | solution.py:147
  171.9 8.2 %copy-start.2 = (bf16[32,2,16,128]{3,2,1,0:T(8,128)(2,1)S(1)}, bf16[32,2,16,128]{3,2,1,0:T(8,128)(2,1)}, u32[]{:S(2)}) copy-start(bf16[32,2,16,128]{3,2,1,0:T(8,128)(2,1)} %param.8) | copy-start | bytes 786436
  172.0 8.3 %copy-start.3 = (bf16[32,2,16,128]{3,2,1,0:T(8,128)(2,1)S(1)}, bf16[32,2,16,128]{3,2,1,0:T(8,128)(2,1)}, u32[]{:S(2)}) copy-start(bf16[32,2,16,128]{3,2,1,0:T(8,128)(2,1)} %param.9) | copy-start | bytes 786436
  172.0 58.5 %all-to-all-start.1 = ((bf16[128,4,32,128]{3,2,1,0:T(8,128)(2,1)}), bf16[128,4,32,128]{3,2,1,0:T(8,128)(2,1)}, u32[]{:S(2)}, u32[]{:S(2)}) async-start(bf16[128,4,32,128]{3,2,1,0:T(8,128)(2,1)} %bitcast.46), calls=%async_computation.1 | async-start | bytes 8388608 | tf_op jit(solution)/shard_map/all_to_all | solution.py:147
  237.7 7.5 %copy-start = (f32[32,128,256]{2,1,0:T(8,128)S(1)}, f32[32,128,256]{2,1,0:T(8,128)}, u32[]{:S(2)}) copy-start(f32[32,128,256]{2,1,0:T(8,128)} %fusion.11) | copy-start | bytes 12582916
  237.7 7.5 %copy-start.1 = (f32[32,128,256]{2,1,0:T(8,128)S(1)}, f32[32,128,256]{2,1,0:T(8,128)}, u32[]{:S(2)}) copy-start(f32[32,128,256]{2,1,0:T(8,128)} %fusion.8) | copy-start | bytes 12582916

commit v7 on v6

--- a/solution.py
+++ b/solution.py
@@ -150,10 +150,11 @@
         ki = k_im[section_number]
         w_first = jnp.stack([kr, ki], axis=2).reshape(kr.shape[0], kr.shape[1], -1)
         w_second = jnp.stack([-ki, kr], axis=2).reshape(kr.shape[0], kr.shape[1], -1)
-        t_first = jnp.einsum("swrn,swx->rnx", got, w_first, preferred_element_type=fp)
-        t_second = jnp.einsum("swrn,swx->rnx", got, w_second, preferred_element_type=fp)
+        both = jnp.concatenate([w_first, w_second], axis=2)
+        t = jnp.einsum("swrn,swx->rnx", got, both, preferred_element_type=fp)
         half = got.shape[3] // 2
-        part = t_first[:, :half] + t_second[:, half:]
+        width = w_first.shape[2]
+        part = t[:, :half, :width] + t[:, half:, width:]
         volume = part if volume is None else volume + part
     return (volume[:, :, :depth_count], volume[:, :, depth_count:])
 

time: 252 us -> 245 us (0.972)
  matrix products: 33.1 us -> 20.3 us
  waiting for transfers between devices: 138 us -> 146 us
    dot_general x4 -> x2, matrix products: 33.1 us -> 20.3 us  [shards(): t = jnp.einsum('swrn,swx->rnx', got, both, preferred_element_type=fp)]
    all_to_all x2, waiting for transfers between devices: 65.4 us -> 74 us  [shards(): got = lax.all_to_all(send, ('wave', 'angle'), 0, 0, tiled=True)]
  transfers between devices with their start and end apart: 6 -> 6, of which waited for: 6 -> 6; matrix products, arithmetic and copies ran while one was open for 15% -> 12% of each run, Pallas kernels for 6% -> 6%
where the time goes in v7:
time: 245 us; the launch traced here: 241 us
  waiting for transfers between devices  146 us (60%)
  Pallas kernels  29.5 us (12%)
  starting transfers between devices  24 us (10%)
  matrix products  20.3 us (8%)
  other arithmetic  17 us (7%)
  local copies, waits for them, and re-layouts  3.4 us (1%)
    all_to_all x2, waiting for transfers between devices, shards(): got = lax.all_to_all(send, ('wave', 'angle'), 0, 0, tiled=True)  74 us
    ppermute x4, waiting for transfers between devices, from_partner(): return lax.ppermute(block, axis, route)  72.4 us
    pallas_call x2, Pallas kernels, spectra(): pl.pallas_call(spectrum_kernel, out_shape=jax.ShapeDtypeStruct((blocks, g...  29.5 us
    dot_general x2, matrix products, shards(): t = jnp.einsum('swrn,swx->rnx', got, both, preferred_element_type=fp)  20.3 us
    all_to_all x2, starting transfers between devices, shards(): got = lax.all_to_all(send, ('wave', 'angle'), 0, 0, tiled=True)  18.3 us
    convert_element_type x2, other arithmetic, dft_tables(): (-jnp.sin(phase) * factor).astype(jnp.bfloat16)  10.3 us
    ppermute x4, starting transfers between devices, from_partner(): return lax.ppermute(block, axis, route)  5.64 us
  transfers between devices with their start and end apart: 6, of which 6 were waited for; matrix products, arithmetic and copies ran while one was open for 12% of the time, Pallas kernels for 6%

profile of v7, /device:TPU:24, one launch (start us, length us, event | category | flops | bytes accessed | tf_op | source)
XLA Modules:
  0.0 241.4 jit_solution(4412673675880054169)
XLA Ops:
  0.6 2.0 collective-permute-start.2
  2.6 3.0 %collective-permute-start = (bf16[4,1,512,512]{3,2,1,0:T(8,128)(2,1)}, bf16[4,1,512,512]{3,2,1,0:T(8,128)(2,1)}, u32[]{:S(2)}, u32[]{:S(2)}) collective-permute-start(bf16[4,1,512,512]{3,2,1,0:T(8,128)(2,1)} %own_re.3), channel_id=1, source_target_pairs={{0,16},{16,0},{32,48},{48,32},{64,80},{80,64},{96,112},{112,96},{1... | collective-permute-start | bytes 6291464 | tf_op jit(solution)/shard_map/ppermute | solution.py:20
  5.7 0.1 collective-permute-start.3
  5.8 0.5 collective-permute-start.1
  6.3 4.3 %fusion.27 = bf16[512,8,1,64]{0,3,2,1:T(8,128)(2,1)S(1)} fusion(s32[8,64]{1,0:T(8,128)S(1)} %multiply_add_fusion), kind=kLoop, calls=%fused_computation.48 | loop fusion | flops 5242880 | bytes 526336 | tf_op jit(solution)/shard_map/neg | solution.py:44
  10.6 4.9 %multiply_convert_fusion.2 = (bf16[512,8,1,64]{0,3,2,1:T(8,128)(2,1)S(1)}, bf16[512,8,1,64]{0,3,2,1:T(8,128)(2,1)S(1)}) fusion(s32[8,64]{1,0:T(8,128)S(1)} %multiply_add_fusion), kind=kLoop, calls=%fused_computation.28 | loop fusion | flops 4980736 | bytes 1050624 | tf_op jit(solution)/shard_map/convert_element_type | solution.py:30
  15.5 0.2 pad_maximum_fusion.1
  15.7 0.5 copy.21
  16.2 0.0 copy-start.3
  16.2 0.5 copy.22
  16.8 5.3 %multiply_convert_fusion = (bf16[512,512]{1,0:T(8,128)(2,1)}, bf16[512,512]{1,0:T(8,128)(2,1)}) fusion(), kind=kLoop, calls=%fused_computation.24 | loop fusion | flops 4980736 | bytes 1048576 | tf_op jit(solution)/shard_map/convert_element_type | solution.py:30
  22.1 1.5 pad_maximum_fusion.col_a
  23.6 0.0 copy-done.3
  23.6 0.5 slice_bitcast_fusion.1
  24.1 25.4 %collective-permute-done.2.rest_0_.far_re = bf16[4,1,512,512]{3,2,1,0:T(8,128)(2,1)} collective-permute-done((bf16[4,1,512,512]{3,2,1,0:T(8,128)(2,1)}, bf16[4,1,512,512]{3,2,1,0:T(8,128)(2,1)}, u32[]{:S(2)}, u32[]{:S(2)}) %collective-permute-start.2) | collective-permute-done | bytes 2097184 | tf_op jit(solution)/shard_map/ppermute | solution.py:20
  49.5 3.5 %collective-permute-done.far_re.rest_0_ = bf16[4,1,512,512]{3,2,1,0:T(8,128)(2,1)} collective-permute-done((bf16[4,1,512,512]{3,2,1,0:T(8,128)(2,1)}, bf16[4,1,512,512]{3,2,1,0:T(8,128)(2,1)}, u32[]{:S(2)}, u32[]{:S(2)}) %collective-permute-start) | collective-permute-done | bytes 2097184 | tf_op jit(solution)/shard_map/ppermute | solution.py:20
  53.0 40.5 %collective-permute-done.3.rest_1_.far_im = bf16[4,1,512,512]{3,2,1,0:T(8,128)(2,1)} collective-permute-done((bf16[4,1,512,512]{3,2,1,0:T(8,128)(2,1)}, bf16[4,1,512,512]{3,2,1,0:T(8,128)(2,1)}, u32[]{:S(2)}, u32[]{:S(2)}) %collective-permute-start.3) | collective-permute-done | bytes 2097184 | tf_op jit(solution)/shard_map/ppermute | solution.py:20
  93.5 3.0 %collective-permute-done.1.far_im.rest_1_ = bf16[4,1,512,512]{3,2,1,0:T(8,128)(2,1)} collective-permute-done((bf16[4,1,512,512]{3,2,1,0:T(8,128)(2,1)}, bf16[4,1,512,512]{3,2,1,0:T(8,128)(2,1)}, u32[]{:S(2)}, u32[]{:S(2)}) %collective-permute-start.1) | collective-permute-done | bytes 2097184 | tf_op jit(solution)/shard_map/ppermute | solution.py:20
  96.5 14.8 %shard_map.68 = bf16[8,16,4,32,128]{4,3,2,1,0:T(8,128)(2,1)} custom-call(s32[4]{0:T(128)} %get-tuple-element.16.slot_ref, bf16[4,1,512,512]{3,2,1,0:T(8,128)(2,1)} %own_re.3, bf16[4,1,512,512]{3,2,1,0:T(8,128)(2,1)} %own_im.3, bf16[4,1,512,512]{3,2,1,0:T(8,128)(2,1)} %collective-permute-done.far_re.rest_0_, ...), custom_call_target="tpu_custom_call" | custom-call | flops 8589934592 | bytes 15728640 | tf_op jit(solution)/shard_map/pallas_call | solution.py:85
  111.2 10.3 %all-to-all-start = ((bf16[128,4,32,128]{3,2,1,0:T(8,128)(2,1)}), bf16[128,4,32,128]{3,2,1,0:T(8,128)(2,1)}, u32[]{:S(2)}, u32[]{:S(2)}) async-start(bf16[128,4,32,128]{3,2,1,0:T(8,128)(2,1)} %bitcast.51), calls=%async_computation | async-start | bytes 8388608 | tf_op jit(solution)/shard_map/all_to_all | solution.py:147
  121.5 14.8 %shard_map.69 = bf16[8,16,4,32,128]{4,3,2,1,0:T(8,128)(2,1)} custom-call(s32[4]{0:T(128)} %get-tuple-element.17.slot_ref, bf16[4,1,512,512]{3,2,1,0:T(8,128)(2,1)} %own_re.3, bf16[4,1,512,512]{3,2,1,0:T(8,128)(2,1)} %own_im.3, bf16[4,1,512,512]{3,2,1,0:T(8,128)(2,1)} %collective-permute-done.2.rest_0_.far_re, ...), custom_call_target="tpu_custom_call" | custom-call | flops 8589934592 | bytes 15728640 | tf_op jit(solution)/shard_map/pallas_call | solution.py:85
  136.3 35.7 %all-to-all-done = bf16[128,4,32,128]{3,2,1,0:T(8,128)(2,1)} async-done(((bf16[128,4,32,128]{3,2,1,0:T(8,128)(2,1)}), bf16[128,4,32,128]{3,2,1,0:T(8,128)(2,1)}, u32[]{:S(2)}, u32[]{:S(2)}) %all-to-all-start) | async-done | bytes 4194336 | tf_op jit(solution)/shard_map/all_to_all | solution.py:147
  171.9 0.0 copy-start.1
  171.9 0.0 copy-start.2
  171.9 8.1 %all-to-all-start.1 = ((bf16[128,4,32,128]{3,2,1,0:T(8,128)(2,1)}), bf16[128,4,32,128]{3,2,1,0:T(8,128)(2,1)}, u32[]{:S(2)}, u32[]{:S(2)}) async-start(bf16[128,4,32,128]{3,2,1,0:T(8,128)(2,1)} %bitcast.50), calls=%async_computation.1 | async-start | bytes 8388608 | tf_op jit(solution)/shard_map/all_to_all | solution.py:147
  180.0 0.0 copy-done.1
  180.1 0.0 copy-done.2
  180.3 0.1 copy_bitcast_fusion.2
  180.4 0.1 copy_bitcast_fusion
  180.5 11.6 %fusion.4 = f32[32,128,512]{2,1,0:T(8,128)} fusion(bf16[128,4,32,128]{3,2,1,0:T(8,128)(2,1)} %all-to-all-done, bf16[128,4,256]{2,0,1:T(8,128)(2,1)S(1)} %get-tuple-element.22, bf16[128,4,256]{2,0,1:T(8,128)(2,1)S(1)} %get-tuple-element.23), kind=kOutput, calls=%fused_computation.4 | convolution fusion | flops 2148532224 | bytes 13107200 | tf_op jit(solution)/shard_map/swrn,swx->rnx/dot_general | solution.py:154
  192.1 38.4 %all-to-all-done.1 = bf16[128,4,32,128]{3,2,1,0:T(8,128)(2,1)} async-done(((bf16[128,4,32,128]{3,2,1,0:T(8,128)(2,1)}), bf16[128,4,32,128]{3,2,1,0:T(8,128)(2,1)}, u32[]{:S(2)}, u32[]{:S(2)}) %all-to-all-start.1) | async-done | bytes 4194336 | tf_op jit(solution)/shard_map/all_to_all | solution.py:147
  230.4 0.0 copy-start
  230.4 8.7 %fusion.7 = f32[32,128,512]{2,1,0:T(8,128)S(1)} fusion(bf16[128,4,32,128]{3,2,1,0:T(8,128)(2,1)} %all-to-all-done.1, bf16[128,4,256]{2,0,1:T(8,128)(2,1)S(1)} %get-tuple-element.20, bf16[128,4,256]{2,0,1:T(8,128)(2,1)S(1)} %get-tuple-element.21), kind=kOutput, calls=%fused_computation.5 | convolution fusion | flops 2148532224 | bytes 13107200 | tf_op jit(solution)/shard_map/swrn,swx->rnx/dot_general | solution.py:154
  239.1 0.0 copy-done
  239.1 0.6 fusion.10
  239.8 1.6 fusion.30
  (11 shorter events, 0.2 us)
Async XLA Ops:
  0.6 48.9 %collective-permute-start.2 = (bf16[4,1,512,512]{3,2,1,0:T(8,128)(2,1)}, bf16[4,1,512,512]{3,2,1,0:T(8,128)(2,1)}, u32[]{:S(2)}, u32[]{:S(2)}) collective-permute-start(bf16[4,1,512,512]{3,2,1,0:T(8,128)(2,1)} %own_re.3), channel_id=1, source_target_pairs={{0,32},{32,0},{16,48},{48,16},{64,96},{96,64},{80,112},{112,80},{1... | collective-permute-start | bytes 6291464 | tf_op jit(solution)/shard_map/ppermute | solution.py:20
  2.6 50.4 %collective-permute-start = (bf16[4,1,512,512]{3,2,1,0:T(8,128)(2,1)}, bf16[4,1,512,512]{3,2,1,0:T(8,128)(2,1)}, u32[]{:S(2)}, u32[]{:S(2)}) collective-permute-start(bf16[4,1,512,512]{3,2,1,0:T(8,128)(2,1)} %own_re.3), channel_id=1, source_target_pairs={{0,16},{16,0},{32,48},{48,32},{64,80},{80,64},{96,112},{112,96},{1... | collective-permute-start | bytes 6291464 | tf_op jit(solution)/shard_map/ppermute | solution.py:20
  5.7 87.9 %collective-permute-start.3 = (bf16[4,1,512,512]{3,2,1,0:T(8,128)(2,1)}, bf16[4,1,512,512]{3,2,1,0:T(8,128)(2,1)}, u32[]{:S(2)}, u32[]{:S(2)}) collective-permute-start(bf16[4,1,512,512]{3,2,1,0:T(8,128)(2,1)} %own_im.3), channel_id=1, source_target_pairs={{0,32},{32,0},{16,48},{48,16},{64,96},{96,64},{80,112},{112,80},{1... | collective-permute-start | bytes 6291464 | tf_op jit(solution)/shard_map/ppermute | solution.py:20
  5.8 90.7 %collective-permute-start.1 = (bf16[4,1,512,512]{3,2,1,0:T(8,128)(2,1)}, bf16[4,1,512,512]{3,2,1,0:T(8,128)(2,1)}, u32[]{:S(2)}, u32[]{:S(2)}) collective-permute-start(bf16[4,1,512,512]{3,2,1,0:T(8,128)(2,1)} %own_im.3), channel_id=1, source_target_pairs={{0,16},{16,0},{32,48},{48,32},{64,80},{80,64},{96,112},{112,96},{1... | collective-permute-start | bytes 6291464 | tf_op jit(solution)/shard_map/ppermute | solution.py:20
  16.2 7.4 %copy-start.3 = (s32[2,4]{1,0:T(2,128)S(1)}, s32[2,4]{1,0:T(2,128)}, u32[]{:S(2)}) copy-start(s32[2,4]{1,0:T(2,128)} %param.7) | copy-start | bytes 100
  111.2 60.7 %all-to-all-start = ((bf16[128,4,32,128]{3,2,1,0:T(8,128)(2,1)}), bf16[128,4,32,128]{3,2,1,0:T(8,128)(2,1)}, u32[]{:S(2)}, u32[]{:S(2)}) async-start(bf16[128,4,32,128]{3,2,1,0:T(8,128)(2,1)} %bitcast.51), calls=%async_computation | async-start | bytes 8388608 | tf_op jit(solution)/shard_map/all_to_all | solution.py:147
  171.9 8.1 %copy-start.1 = (bf16[32,2,16,128]{3,2,1,0:T(8,128)(2,1)S(1)}, bf16[32,2,16,128]{3,2,1,0:T(8,128)(2,1)}, u32[]{:S(2)}) copy-start(bf16[32,2,16,128]{3,2,1,0:T(8,128)(2,1)} %param.8) | copy-start | bytes 786436
  171.9 8.1 %copy-start.2 = (bf16[32,2,16,128]{3,2,1,0:T(8,128)(2,1)S(1)}, bf16[32,2,16,128]{3,2,1,0:T(8,128)(2,1)}, u32[]{:S(2)}) copy-start(bf16[32,2,16,128]{3,2,1,0:T(8,128)(2,1)} %param.9) | copy-start | bytes 786436
  171.9 58.5 %all-to-all-start.1 = ((bf16[128,4,32,128]{3,2,1,0:T(8,128)(2,1)}), bf16[128,4,32,128]{3,2,1,0:T(8,128)(2,1)}, u32[]{:S(2)}, u32[]{:S(2)}) async-start(bf16[128,4,32,128]{3,2,1,0:T(8,128)(2,1)} %bitcast.50), calls=%async_computation.1 | async-start | bytes 8388608 | tf_op jit(solution)/shard_map/all_to_all | solution.py:147
  230.4 8.7 %copy-start = (f32[32,128,512]{2,1,0:T(8,128)S(1)}, f32[32,128,512]{2,1,0:T(8,128)}, u32[]{:S(2)}) copy-start(f32[32,128,512]{2,1,0:T(8,128)} %fusion.4) | copy-start | bytes 25165828

commit v8 on v7

--- a/solution.py
+++ b/solution.py
@@ -56,11 +56,8 @@
     b_im = far_im[0, 0].astype(fp)
     z_re = (a_re * b_re + a_im * b_im).astype(bf)
     z_im = (a_im * b_re - a_re * b_im).astype(bf)
-    n = z_re.shape[1]
-    y = (
-        jnp.dot(z_re, col_a[:n, :], preferred_element_type=fp)
-        + jnp.dot(z_im, col_a[n:, :], preferred_element_type=fp)
-    ).astype(bf)
+    z = jnp.concatenate([z_re, z_im], axis=1)
+    y = jnp.dot(z, col_a[...], preferred_element_type=fp).astype(bf)
     first = jnp.dot(row_re[...], y, preferred_element_type=fp)
     second = jnp.dot(row_im[...], y, preferred_element_type=fp)
     blocks, groups, _, rows_per, lanes = out_ref.shape

time: 245 us -> 245 us (level)
  no operation moved by 1% of the time
where the time goes in v8:
time: 245 us; the launch traced here: 241 us
  waiting for transfers between devices  146 us (60%)
  Pallas kernels  29.5 us (12%)
  starting transfers between devices  24 us (10%)
  matrix products  20.3 us (8%)
  other arithmetic  17 us (7%)
  local copies, waits for them, and re-layouts  3.4 us (1%)
    all_to_all x2, waiting for transfers between devices, shards(): got = lax.all_to_all(send, ('wave', 'angle'), 0, 0, tiled=True)  74 us
    ppermute x4, waiting for transfers between devices, from_partner(): return lax.ppermute(block, axis, route)  72.4 us
    pallas_call x2, Pallas kernels, spectra(): pl.pallas_call(spectrum_kernel, out_shape=jax.ShapeDtypeStruct((blocks, g...  29.5 us
    dot_general x2, matrix products, shards(): t = jnp.einsum('swrn,swx->rnx', got, both, preferred_element_type=fp)  20.3 us
    all_to_all x2, starting transfers between devices, shards(): got = lax.all_to_all(send, ('wave', 'angle'), 0, 0, tiled=True)  18.3 us
    convert_element_type x2, other arithmetic, dft_tables(): (-jnp.sin(phase) * factor).astype(jnp.bfloat16)  10.3 us
    ppermute x4, starting transfers between devices, from_partner(): return lax.ppermute(block, axis, route)  5.64 us
  transfers between devices with their start and end apart: 6, of which 6 were waited for; matrix products, arithmetic and copies ran while one was open for 12% of the time, Pallas kernels for 6%

profile of v8, /device:TPU:24, one launch (start us, length us, event | category | flops | bytes accessed | tf_op | source)
XLA Modules:
  0.0 241.4 jit_solution(15960396244860129974)
XLA Ops:
  0.6 2.0 collective-permute-start.2
  2.6 3.0 %collective-permute-start = (bf16[4,1,512,512]{3,2,1,0:T(8,128)(2,1)}, bf16[4,1,512,512]{3,2,1,0:T(8,128)(2,1)}, u32[]{:S(2)}, u32[]{:S(2)}) collective-permute-start(bf16[4,1,512,512]{3,2,1,0:T(8,128)(2,1)} %own_re.3), channel_id=1, source_target_pairs={{0,16},{16,0},{32,48},{48,32},{64,80},{80,64},{96,112},{112,96},{1... | collective-permute-start | bytes 6291464 | tf_op jit(solution)/shard_map/ppermute | solution.py:20
  5.7 0.1 collective-permute-start.3
  5.8 0.5 collective-permute-start.1
  6.3 4.3 %fusion.27 = bf16[512,8,1,64]{0,3,2,1:T(8,128)(2,1)S(1)} fusion(s32[8,64]{1,0:T(8,128)S(1)} %multiply_add_fusion), kind=kLoop, calls=%fused_computation.48 | loop fusion | flops 5242880 | bytes 526336 | tf_op jit(solution)/shard_map/neg | solution.py:44
  10.6 4.9 %multiply_convert_fusion.2 = (bf16[512,8,1,64]{0,3,2,1:T(8,128)(2,1)S(1)}, bf16[512,8,1,64]{0,3,2,1:T(8,128)(2,1)S(1)}) fusion(s32[8,64]{1,0:T(8,128)S(1)} %multiply_add_fusion), kind=kLoop, calls=%fused_computation.28 | loop fusion | flops 4980736 | bytes 1050624 | tf_op jit(solution)/shard_map/convert_element_type | solution.py:30
  15.5 0.2 pad_maximum_fusion.1
  15.7 0.5 copy.21
  16.2 0.0 copy-start.3
  16.2 0.5 copy.22
  16.8 5.3 %multiply_convert_fusion = (bf16[512,512]{1,0:T(8,128)(2,1)}, bf16[512,512]{1,0:T(8,128)(2,1)}) fusion(), kind=kLoop, calls=%fused_computation.24 | loop fusion | flops 4980736 | bytes 1048576 | tf_op jit(solution)/shard_map/convert_element_type | solution.py:30
  22.1 1.5 pad_maximum_fusion.col_a
  23.6 0.0 copy-done.3
  23.6 0.5 slice_bitcast_fusion.1
  24.1 25.4 %collective-permute-done.2.rest_0_.far_re = bf16[4,1,512,512]{3,2,1,0:T(8,128)(2,1)} collective-permute-done((bf16[4,1,512,512]{3,2,1,0:T(8,128)(2,1)}, bf16[4,1,512,512]{3,2,1,0:T(8,128)(2,1)}, u32[]{:S(2)}, u32[]{:S(2)}) %collective-permute-start.2) | collective-permute-done | bytes 2097184 | tf_op jit(solution)/shard_map/ppermute | solution.py:20
  49.5 3.5 %collective-permute-done.far_re.rest_0_ = bf16[4,1,512,512]{3,2,1,0:T(8,128)(2,1)} collective-permute-done((bf16[4,1,512,512]{3,2,1,0:T(8,128)(2,1)}, bf16[4,1,512,512]{3,2,1,0:T(8,128)(2,1)}, u32[]{:S(2)}, u32[]{:S(2)}) %collective-permute-start) | collective-permute-done | bytes 2097184 | tf_op jit(solution)/shard_map/ppermute | solution.py:20
  53.0 40.5 %collective-permute-done.3.rest_1_.far_im = bf16[4,1,512,512]{3,2,1,0:T(8,128)(2,1)} collective-permute-done((bf16[4,1,512,512]{3,2,1,0:T(8,128)(2,1)}, bf16[4,1,512,512]{3,2,1,0:T(8,128)(2,1)}, u32[]{:S(2)}, u32[]{:S(2)}) %collective-permute-start.3) | collective-permute-done | bytes 2097184 | tf_op jit(solution)/shard_map/ppermute | solution.py:20
  93.5 3.0 %collective-permute-done.1.far_im.rest_1_ = bf16[4,1,512,512]{3,2,1,0:T(8,128)(2,1)} collective-permute-done((bf16[4,1,512,512]{3,2,1,0:T(8,128)(2,1)}, bf16[4,1,512,512]{3,2,1,0:T(8,128)(2,1)}, u32[]{:S(2)}, u32[]{:S(2)}) %collective-permute-start.1) | collective-permute-done | bytes 2097184 | tf_op jit(solution)/shard_map/ppermute | solution.py:20
  96.5 14.8 %shard_map.68 = bf16[8,16,4,32,128]{4,3,2,1,0:T(8,128)(2,1)} custom-call(s32[4]{0:T(128)} %get-tuple-element.16.slot_ref, bf16[4,1,512,512]{3,2,1,0:T(8,128)(2,1)} %own_re.3, bf16[4,1,512,512]{3,2,1,0:T(8,128)(2,1)} %own_im.3, bf16[4,1,512,512]{3,2,1,0:T(8,128)(2,1)} %collective-permute-done.far_re.rest_0_, ...), custom_call_target="tpu_custom_call" | custom-call | flops 8589934592 | bytes 15728640 | tf_op jit(solution)/shard_map/pallas_call | solution.py:82
  111.2 10.3 %all-to-all-start = ((bf16[128,4,32,128]{3,2,1,0:T(8,128)(2,1)}), bf16[128,4,32,128]{3,2,1,0:T(8,128)(2,1)}, u32[]{:S(2)}, u32[]{:S(2)}) async-start(bf16[128,4,32,128]{3,2,1,0:T(8,128)(2,1)} %bitcast.51), calls=%async_computation | async-start | bytes 8388608 | tf_op jit(solution)/shard_map/all_to_all | solution.py:144
  121.5 14.8 %shard_map.69 = bf16[8,16,4,32,128]{4,3,2,1,0:T(8,128)(2,1)} custom-call(s32[4]{0:T(128)} %get-tuple-element.17.slot_ref, bf16[4,1,512,512]{3,2,1,0:T(8,128)(2,1)} %own_re.3, bf16[4,1,512,512]{3,2,1,0:T(8,128)(2,1)} %own_im.3, bf16[4,1,512,512]{3,2,1,0:T(8,128)(2,1)} %collective-permute-done.2.rest_0_.far_re, ...), custom_call_target="tpu_custom_call" | custom-call | flops 8589934592 | bytes 15728640 | tf_op jit(solution)/shard_map/pallas_call | solution.py:82
  136.3 35.7 %all-to-all-done = bf16[128,4,32,128]{3,2,1,0:T(8,128)(2,1)} async-done(((bf16[128,4,32,128]{3,2,1,0:T(8,128)(2,1)}), bf16[128,4,32,128]{3,2,1,0:T(8,128)(2,1)}, u32[]{:S(2)}, u32[]{:S(2)}) %all-to-all-start) | async-done | bytes 4194336 | tf_op jit(solution)/shard_map/all_to_all | solution.py:144
  171.9 0.0 copy-start.1
  171.9 0.0 copy-start.2
  171.9 8.1 %all-to-all-start.1 = ((bf16[128,4,32,128]{3,2,1,0:T(8,128)(2,1)}), bf16[128,4,32,128]{3,2,1,0:T(8,128)(2,1)}, u32[]{:S(2)}, u32[]{:S(2)}) async-start(bf16[128,4,32,128]{3,2,1,0:T(8,128)(2,1)} %bitcast.50), calls=%async_computation.1 | async-start | bytes 8388608 | tf_op jit(solution)/shard_map/all_to_all | solution.py:144
  180.0 0.0 copy-done.1
  180.1 0.0 copy-done.2
  180.3 0.1 copy_bitcast_fusion.2
  180.4 0.1 copy_bitcast_fusion
  180.5 11.6 %fusion.4 = f32[32,128,512]{2,1,0:T(8,128)} fusion(bf16[128,4,32,128]{3,2,1,0:T(8,128)(2,1)} %all-to-all-done, bf16[128,4,256]{2,0,1:T(8,128)(2,1)S(1)} %get-tuple-element.22, bf16[128,4,256]{2,0,1:T(8,128)(2,1)S(1)} %get-tuple-element.23), kind=kOutput, calls=%fused_computation.4 | convolution fusion | flops 2148532224 | bytes 13107200 | tf_op jit(solution)/shard_map/swrn,swx->rnx/dot_general | solution.py:151
  192.1 38.4 %all-to-all-done.1 = bf16[128,4,32,128]{3,2,1,0:T(8,128)(2,1)} async-done(((bf16[128,4,32,128]{3,2,1,0:T(8,128)(2,1)}), bf16[128,4,32,128]{3,2,1,0:T(8,128)(2,1)}, u32[]{:S(2)}, u32[]{:S(2)}) %all-to-all-start.1) | async-done | bytes 4194336 | tf_op jit(solution)/shard_map/all_to_all | solution.py:144
  230.4 0.0 copy-start
  230.4 8.7 %fusion.7 = f32[32,128,512]{2,1,0:T(8,128)S(1)} fusion(bf16[128,4,32,128]{3,2,1,0:T(8,128)(2,1)} %all-to-all-done.1, bf16[128,4,256]{2,0,1:T(8,128)(2,1)S(1)} %get-tuple-element.20, bf16[128,4,256]{2,0,1:T(8,128)(2,1)S(1)} %get-tuple-element.21), kind=kOutput, calls=%fused_computation.5 | convolution fusion | flops 2148532224 | bytes 13107200 | tf_op jit(solution)/shard_map/swrn,swx->rnx/dot_general | solution.py:151
  239.1 0.0 copy-done
  239.1 0.6 fusion.10
  239.8 1.6 fusion.30
  (11 shorter events, 0.2 us)
Async XLA Ops:
  0.6 48.9 %collective-permute-start.2 = (bf16[4,1,512,512]{3,2,1,0:T(8,128)(2,1)}, bf16[4,1,512,512]{3,2,1,0:T(8,128)(2,1)}, u32[]{:S(2)}, u32[]{:S(2)}) collective-permute-start(bf16[4,1,512,512]{3,2,1,0:T(8,128)(2,1)} %own_re.3), channel_id=1, source_target_pairs={{0,32},{32,0},{16,48},{48,16},{64,96},{96,64},{80,112},{112,80},{1... | collective-permute-start | bytes 6291464 | tf_op jit(solution)/shard_map/ppermute | solution.py:20
  2.6 50.4 %collective-permute-start = (bf16[4,1,512,512]{3,2,1,0:T(8,128)(2,1)}, bf16[4,1,512,512]{3,2,1,0:T(8,128)(2,1)}, u32[]{:S(2)}, u32[]{:S(2)}) collective-permute-start(bf16[4,1,512,512]{3,2,1,0:T(8,128)(2,1)} %own_re.3), channel_id=1, source_target_pairs={{0,16},{16,0},{32,48},{48,32},{64,80},{80,64},{96,112},{112,96},{1... | collective-permute-start | bytes 6291464 | tf_op jit(solution)/shard_map/ppermute | solution.py:20
  5.7 87.9 %collective-permute-start.3 = (bf16[4,1,512,512]{3,2,1,0:T(8,128)(2,1)}, bf16[4,1,512,512]{3,2,1,0:T(8,128)(2,1)}, u32[]{:S(2)}, u32[]{:S(2)}) collective-permute-start(bf16[4,1,512,512]{3,2,1,0:T(8,128)(2,1)} %own_im.3), channel_id=1, source_target_pairs={{0,32},{32,0},{16,48},{48,16},{64,96},{96,64},{80,112},{112,80},{1... | collective-permute-start | bytes 6291464 | tf_op jit(solution)/shard_map/ppermute | solution.py:20
  5.8 90.7 %collective-permute-start.1 = (bf16[4,1,512,512]{3,2,1,0:T(8,128)(2,1)}, bf16[4,1,512,512]{3,2,1,0:T(8,128)(2,1)}, u32[]{:S(2)}, u32[]{:S(2)}) collective-permute-start(bf16[4,1,512,512]{3,2,1,0:T(8,128)(2,1)} %own_im.3), channel_id=1, source_target_pairs={{0,16},{16,0},{32,48},{48,32},{64,80},{80,64},{96,112},{112,96},{1... | collective-permute-start | bytes 6291464 | tf_op jit(solution)/shard_map/ppermute | solution.py:20
  16.2 7.4 %copy-start.3 = (s32[2,4]{1,0:T(2,128)S(1)}, s32[2,4]{1,0:T(2,128)}, u32[]{:S(2)}) copy-start(s32[2,4]{1,0:T(2,128)} %param.7) | copy-start | bytes 100
  111.2 60.7 %all-to-all-start = ((bf16[128,4,32,128]{3,2,1,0:T(8,128)(2,1)}), bf16[128,4,32,128]{3,2,1,0:T(8,128)(2,1)}, u32[]{:S(2)}, u32[]{:S(2)}) async-start(bf16[128,4,32,128]{3,2,1,0:T(8,128)(2,1)} %bitcast.51), calls=%async_computation | async-start | bytes 8388608 | tf_op jit(solution)/shard_map/all_to_all | solution.py:144
  171.9 8.1 %copy-start.1 = (bf16[32,2,16,128]{3,2,1,0:T(8,128)(2,1)S(1)}, bf16[32,2,16,128]{3,2,1,0:T(8,128)(2,1)}, u32[]{:S(2)}) copy-start(bf16[32,2,16,128]{3,2,1,0:T(8,128)(2,1)} %param.8) | copy-start | bytes 786436
  171.9 8.1 %copy-start.2 = (bf16[32,2,16,128]{3,2,1,0:T(8,128)(2,1)S(1)}, bf16[32,2,16,128]{3,2,1,0:T(8,128)(2,1)}, u32[]{:S(2)}) copy-start(bf16[32,2,16,128]{3,2,1,0:T(8,128)(2,1)} %param.9) | copy-start | bytes 786436
  171.9 58.5 %all-to-all-start.1 = ((bf16[128,4,32,128]{3,2,1,0:T(8,128)(2,1)}), bf16[128,4,32,128]{3,2,1,0:T(8,128)(2,1)}, u32[]{:S(2)}, u32[]{:S(2)}) async-start(bf16[128,4,32,128]{3,2,1,0:T(8,128)(2,1)} %bitcast.50), calls=%async_computation.1 | async-start | bytes 8388608 | tf_op jit(solution)/shard_map/all_to_all | solution.py:144
  230.4 8.7 %copy-start = (f32[32,128,512]{2,1,0:T(8,128)S(1)}, f32[32,128,512]{2,1,0:T(8,128)}, u32[]{:S(2)}) copy-start(f32[32,128,512]{2,1,0:T(8,128)} %fusion.4) | copy-start | bytes 25165828

commit v9 on v8

--- a/solution.py
+++ b/solution.py
@@ -44,12 +44,11 @@
     return join([er, ei], [-ei, er])
 
 
-def spectrum_kernel(
-    slot_ref, own_re, own_im, far_re, far_im, col_a, row_re, row_im, *rest
-):
-    out_ref = rest[-1]
+def spectrum_kernel(slot_ref, own_re, own_im, far_re, far_im, col_a, row_re, row_im, *rest):
     fp = jnp.float32
     bf = jnp.bfloat16
+    out_ref = rest[-1]
+    final = len(out_ref.shape) == 5
     a_re = own_re[0, 0].astype(fp)
     a_im = own_im[0, 0].astype(fp)
     b_re = far_re[0, 0].astype(fp)
@@ -60,42 +59,61 @@
     y = jnp.dot(z, col_a[...], preferred_element_type=fp).astype(bf)
     first = jnp.dot(row_re[...], y, preferred_element_type=fp)
     second = jnp.dot(row_im[...], y, preferred_element_type=fp)
-    blocks, groups, _, rows_per, lanes = out_ref.shape
+    lanes = out_ref.shape[-1] if final else 128
+    blocks = first.shape[1] // lanes
     lane = lax.broadcasted_iota(jnp.int32, (first.shape[0], lanes), 1)
     for block in range(blocks):
         cut = slice(block * lanes, (block + 1) * lanes)
         swapped = pltpu.roll(second[:, cut], lanes // 2, 1)
         swapped = jnp.where(lane < lanes // 2, -swapped, swapped)
-        spec = (first[:, cut] + swapped).astype(bf)
-        out_ref[block, :, 0, :, :] = spec.reshape(groups, rows_per, lanes)
-
-
-def spectra(slots, own_re, own_im, far_re, far_im, col_a, row_re, row_im, blocks, groups, after):
+        total = first[:, cut] + swapped
+        if final:
+            total = (rest[-2][0, :, cut] + total).astype(bf)
+            _, groups, _, rows_per, _ = out_ref.shape
+            out_ref[block, :, 0, :, :] = total.reshape(groups, rows_per, lanes)
+        else:
+            out_ref[0, :, cut] = total
+
+
+def spectra(slots, own_re, own_im, far_re, far_im, tables, half, blocks, groups, after, partial):
+    col_a, row_re, row_im = tables
     waves, _, rows, cols = own_re.shape
+    h = far_re.shape[2]
     lanes = 2 * cols // blocks
     rows_per = rows // groups
-    field = pl.BlockSpec((1, 1, rows, cols), lambda i, sl: (i, 0, 0, 0))
-    partner = pl.BlockSpec((1, 1, rows, cols), lambda i, sl: (sl[i], 0, 0, 0))
+    field = pl.BlockSpec((1, 1, h, cols), lambda i, sl: (i, 0, half, 0))
+    partner = pl.BlockSpec((1, 1, h, cols), lambda i, sl: (sl[i], 0, 0, 0))
     whole_col = pl.BlockSpec((2 * cols, 2 * cols), lambda i, sl: (0, 0))
-    whole_row = pl.BlockSpec((rows, rows), lambda i, sl: (0, 0))
-    flops = waves * (2 * rows * (2 * cols) * (2 * cols) + 2 * 2 * rows * rows * (2 * cols))
+    row_part = pl.BlockSpec((rows, h), lambda i, sl: (0, half))
+    per_wave = pl.BlockSpec((1, rows, 2 * cols), lambda i, sl: (i, 0, 0))
+    flops = waves * (2 * h * (2 * cols) * (2 * cols) + 2 * 2 * rows * h * (2 * cols))
+    in_specs = [field, field, partner, partner, whole_col, row_part, row_part]
+    in_specs += [pl.BlockSpec(memory_space=pl.ANY)] * len(after)
+    extra = list(after)
+    if partial is None:
+        out_shape = jax.ShapeDtypeStruct((waves, rows, 2 * cols), jnp.float32)
+        out_spec = per_wave
+    else:
+        in_specs.append(per_wave)
+        extra.append(partial)
+        out_shape = jax.ShapeDtypeStruct((blocks, groups, waves, rows_per, lanes), jnp.bfloat16)
+        out_spec = pl.BlockSpec(
+            (blocks, groups, 1, rows_per, lanes), lambda i, sl: (0, 0, i, 0, 0)
+        )
     return pl.pallas_call(
         spectrum_kernel,
-        out_shape=jax.ShapeDtypeStruct((blocks, groups, waves, rows_per, lanes), jnp.bfloat16),
+        out_shape=out_shape,
         grid_spec=pltpu.PrefetchScalarGridSpec(
             num_scalar_prefetch=1,
             grid=(waves,),
-            in_specs=[field, field, partner, partner, whole_col, whole_row, whole_row]
-            + [pl.BlockSpec(memory_space=pl.ANY)] * len(after),
-            out_specs=pl.BlockSpec(
-                (blocks, groups, 1, rows_per, lanes), lambda i, sl: (0, 0, i, 0, 0)
-            ),
+            in_specs=in_specs,
+            out_specs=out_spec,
         ),
         compiler_params=pltpu.CompilerParams(vmem_limit_bytes=60 * 1024 * 1024),
         cost_estimate=pl.CostEstimate(
-            flops=flops, transcendentals=0, bytes_accessed=waves * rows * cols * 12 + 12 * cols * cols
+            flops=flops, transcendentals=0, bytes_accessed=waves * rows * cols * 14 + 8 * cols * cols
         ),
-    )(slots, own_re, own_im, far_re, far_im, col_a, row_re, row_im, *after)
+    )(slots, own_re, own_im, far_re, far_im, col_a, row_re, row_im, *extra)
 
 
 def shards(hologram_real, hologram_imaginary, pair_slot, kernel_real, kernel_imaginary):
@@ -120,26 +138,42 @@
     k_re = all_weights(kernel_real)
     k_im = all_weights(kernel_imaginary)
     volume = None
+    halves = 2
+    h = row_count // halves
     received = [
-        from_partner((hologram_real, hologram_imaginary), "wave", section_number)
+        [
+            from_partner(
+                (hologram_real[:, :, c * h : (c + 1) * h], hologram_imaginary[:, :, c * h : (c + 1) * h]),
+                "wave",
+                section_number,
+            )
+            for c in range(halves)
+        ]
         for section_number in range(section_count)
     ]
+    tables = (col_a, row_real, row_imag)
+    volume = None
     for section_number in range(section_count):
-        got_real, got_imag = received[section_number]
-        after = [a for other, got in enumerate(received) if other != section_number for a in got]
-        send = spectra(
-            pair_slot[section_number],
-            hologram_real,
-            hologram_imaginary,
-            got_real,
-            got_imag,
-            col_a,
-            row_real,
-            row_imag,
-            wave_devices,
-            angle_devices,
-            after,
-        )
+        partial = None
+        for c in range(halves):
+            got_real, got_imag = received[section_number][c]
+            after = [
+                a for other in range(section_count) if other != section_number for a in received[other][c]
+            ]
+            partial = spectra(
+                pair_slot[section_number],
+                hologram_real,
+                hologram_imaginary,
+                got_real,
+                got_imag,
+                tables,
+                c,
+                wave_devices,
+                angle_devices,
+                after,
+                partial,
+            )
+        send = partial
         send = send.reshape(wave_devices * angle_devices, *send.shape[2:])
         got = lax.all_to_all(send, ("wave", "angle"), 0, 0, tiled=True)
         got = with_layout_constraint(got, Layout(tuple(range(got.ndim))))

time: 245 us -> 247 us (level)
  waiting for transfers between devices: 146 us -> 110 us
  Pallas kernels: 29.5 us -> 46.2 us
  starting transfers between devices: 24 us -> 34 us
  local copies, waits for them, and re-layouts: 3.4 us -> 11.5 us
  other arithmetic: 17 us -> 20 us
    ppermute x4 -> x8, waiting for transfers between devices: 72.4 us -> 44.5 us  [from_partner(): return lax.ppermute(block, axis, route)]
    pallas_call x2 -> x4, Pallas kernels: 29.5 us -> 46.2 us  [spectra(): pl.pallas_call(spectrum_kernel, out_shape=out_shape, grid_spec=pltpu.Pref...]
    ppermute x4 -> x8, starting transfers between devices: 5.64 us -> 15.4 us  [from_partner(): return lax.ppermute(block, axis, route)]
    all_to_all x2, waiting for transfers between devices: 74 us -> 65.7 us  [shards(): got = lax.all_to_all(send, ('wave', 'angle'), 0, 0, tiled=True)]
    slice x0 -> x2, local copies, waits for them, and re-layouts: none -> 4.47 us  [the longest x1 2.86 us: shards(): hologram_real[:, :, c * h:(c + 1) * h]]
  transfers between devices with their start and end apart: 6 -> 10, of which waited for: 6 -> 6; matrix products, arithmetic and copies ran while one was open for 12% -> 16% of each run, Pallas kernels for 6% -> 14%
where the time goes in v9:
time: 247 us; the launch traced here: 243 us
  waiting for transfers between devices  110 us (45%)
  Pallas kernels  46.2 us (19%)
  starting transfers between devices  34 us (14%)
  matrix products  20.3 us (8%)
  other arithmetic  20 us (8%)
  local copies, waits for them, and re-layouts  11.5 us (5%)
    all_to_all x2, waiting for transfers between devices, shards(): got = lax.all_to_all(send, ('wave', 'angle'), 0, 0, tiled=True)  65.7 us
    pallas_call x4, Pallas kernels, spectra(): pl.pallas_call(spectrum_kernel, out_shape=out_shape, grid_spec=pltpu.Pref...  46.2 us
    ppermute x8, waiting for transfers between devices, from_partner(): return lax.ppermute(block, axis, route)  44.5 us
    dot_general x2, matrix products, shards(): t = jnp.einsum('swrn,swx->rnx', got, both, preferred_element_type=fp)  20.3 us
    all_to_all x2, starting transfers between devices, shards(): got = lax.all_to_all(send, ('wave', 'angle'), 0, 0, tiled=True)  18.6 us
    ppermute x8, starting transfers between devices, from_partner(): return lax.ppermute(block, axis, route)  15.4 us
    convert_element_type x2, other arithmetic, dft_tables(): (-jnp.sin(phase) * factor).astype(jnp.bfloat16)  10.3 us
  transfers between devices with their start and end apart: 10, of which 6 were waited for; matrix products, arithmetic and copies ran while one was open for 16% of the time, Pallas kernels for 14%

profile of v9, /device:TPU:24, one launch (start us, length us, event | category | flops | bytes accessed | tf_op | source)
XLA Modules:
  0.0 243.0 jit_solution(8079190228648035530)
XLA Ops:
  0.6 0.0 copy-start
  0.6 2.9 %fusion.32 = (bf16[4,1,256,512]{3,2,1,0:T(8,128)(2,1)S(1)}, bf16[4,1,256,512]{3,2,1,0:T(8,128)(2,1)}) fusion(bf16[4,1,512,512]{3,2,1,0:T(8,128)(2,1)} %own_re.7), kind=kLoop, calls=%fused_computation.58 | loop fusion | bytes 4194304 | tf_op jit(solution)/shard_map/slice | solution.py:146
  3.5 3.0 %collective-permute-start.4 = (bf16[4,1,256,512]{3,2,1,0:T(8,128)(2,1)S(1)}, bf16[4,1,256,512]{3,2,1,0:T(8,128)(2,1)S(1)}, u32[]{:S(2)}, u32[]{:S(2)}) collective-permute-start(bf16[4,1,256,512]{3,2,1,0:T(8,128)(2,1)S(1)} %get-tuple-element.6), channel_id=1, source_target_pairs={{0,16},{16,0},{32,48},{48,32},{64,80},{80,64},{96,112},{112,96},{1... | collective-permute-start | bytes 3145736 | tf_op jit(solution)/shard_map/ppermute | solution.py:20
  6.5 0.0 copy-done
  6.5 1.6 fusion.31
  8.1 0.5 collective-permute-start.5
  8.6 1.9 collective-permute-start.6
  10.6 0.1 collective-permute-start.7
  10.7 3.0 %collective-permute-start = (bf16[4,1,256,512]{3,2,1,0:T(8,128)(2,1)}, bf16[4,1,256,512]{3,2,1,0:T(8,128)(2,1)}, u32[]{:S(2)}, u32[]{:S(2)}) collective-permute-start(bf16[4,1,256,512]{3,2,1,0:T(8,128)(2,1)} %get-tuple-element.7), channel_id=1, source_target_pairs={{0,16},{16,0},{32,48},{48,32},{64,80},{80,64},{96,112},{112,96},{1... | collective-permute-start | bytes 3145736 | tf_op jit(solution)/shard_map/ppermute | solution.py:20
  13.7 4.3 %fusion.27 = bf16[512,8,1,64]{0,3,2,1:T(8,128)(2,1)S(1)} fusion(s32[8,64]{1,0:T(8,128)S(1)} %multiply_add_fusion), kind=kLoop, calls=%fused_computation.48 | loop fusion | flops 5242880 | bytes 526336 | tf_op jit(solution)/shard_map/neg | solution.py:44
  18.0 4.9 %multiply_convert_fusion.2 = (bf16[512,8,1,64]{0,3,2,1:T(8,128)(2,1)S(1)}, bf16[512,8,1,64]{0,3,2,1:T(8,128)(2,1)S(1)}) fusion(s32[8,64]{1,0:T(8,128)S(1)} %multiply_add_fusion), kind=kLoop, calls=%fused_computation.28 | loop fusion | flops 4980736 | bytes 1050624 | tf_op jit(solution)/shard_map/convert_element_type | solution.py:30
  22.9 8.1 %collective-permute-done.4.far_re.rest_0_ = bf16[4,1,256,512]{3,2,1,0:T(8,128)(2,1)S(1)} collective-permute-done((bf16[4,1,256,512]{3,2,1,0:T(8,128)(2,1)S(1)}, bf16[4,1,256,512]{3,2,1,0:T(8,128)(2,1)S(1)}, u32[]{:S(2)}, u32[]{:S(2)}) %collective-permute-start.4) | collective-permute-done | bytes 1048608 | tf_op jit(solution)/shard_map/ppermute | solution.py:20
  31.1 0.0 copy-start.2
  31.1 1.9 collective-permute-start.2
  33.0 20.6 %collective-permute-done.5.far_im.rest_1_ = bf16[4,1,256,512]{3,2,1,0:T(8,128)(2,1)S(1)} collective-permute-done((bf16[4,1,256,512]{3,2,1,0:T(8,128)(2,1)}, bf16[4,1,256,512]{3,2,1,0:T(8,128)(2,1)S(1)}, u32[]{:S(2)}, u32[]{:S(2)}) %collective-permute-start.5) | collective-permute-done | bytes 1048608 | tf_op jit(solution)/shard_map/ppermute | solution.py:20
  53.5 0.0 copy-start.3
  53.5 3.0 %collective-permute-start.1 = (bf16[4,1,256,512]{3,2,1,0:T(8,128)(2,1)}, bf16[4,1,256,512]{3,2,1,0:T(8,128)(2,1)}, u32[]{:S(2)}, u32[]{:S(2)}) collective-permute-start(bf16[4,1,256,512]{3,2,1,0:T(8,128)(2,1)} %get-tuple-element.5), channel_id=1, source_target_pairs={{0,16},{16,0},{32,48},{48,32},{64,80},{80,64},{96,112},{112,96},{1... | collective-permute-start | bytes 3145736 | tf_op jit(solution)/shard_map/ppermute | solution.py:20
  56.6 0.0 collective-permute-done.6.rest_0_.far_re
  56.6 0.0 copy-start.4
  56.6 1.9 collective-permute-start.3
  58.5 1.5 pad_maximum_fusion.1
  60.0 2.3 copy.21
  62.3 0.0 copy-start.7
  62.3 2.3 copy.22
  64.6 5.4 %multiply_convert_fusion = (bf16[512,512]{1,0:T(8,128)(2,1)}, bf16[512,512]{1,0:T(8,128)(2,1)}) fusion(), kind=kLoop, calls=%fused_computation.24 | loop fusion | flops 4980736 | bytes 1048576 | tf_op jit(solution)/shard_map/convert_element_type | solution.py:30
  70.0 0.0 copy-done.2
  70.0 0.0 copy-done.3
  70.0 0.0 copy-done.4
  70.0 3.1 %pad_maximum_fusion.col_a = bf16[1024,1024]{1,0:T(8,128)(2,1)} fusion(bf16[512,1024]{1,0:T(8,128)(2,1)} %copy.22, bf16[512,1024]{1,0:T(8,128)(2,1)} %copy.21), kind=kLoop, calls=%fused_computation.9 | loop fusion | flops 4194304 | bytes 4194304 | tf_op jit(solution)/shard_map/concatenate | solution.py:42
  73.0 0.0 copy-done.7
  73.1 0.6 slice_bitcast_fusion.1
  73.6 0.0 collective-permute-done.7.rest_1_.far_im
  73.6 11.2 %shard_map.68.rest_2_ = f32[4,512,1024]{2,1,0:T(8,128)} custom-call(s32[4]{0:T(128)} %get-tuple-element.20.slot_ref, bf16[4,1,512,512]{3,2,1,0:T(8,128)(2,1)} %own_re.7, bf16[4,1,512,512]{3,2,1,0:T(8,128)(2,1)} %own_im.7, bf16[4,1,256,512]{3,2,1,0:T(8,128)(2,1)} %copy-done.2, bf16[4,1,256,512]{3,2,1,0:T(8,128)(2,1)} %copy-done.3, ...), custom_call_target="tpu_custom_call" | custom-call | flops 4294967296 | bytes 16777216 | tf_op jit(solution)/shard_map/pallas_call | solution.py:103
  84.9 0.0 collective-permute-done.far_re.rest_0_
  84.9 12.5 %collective-permute-done.1.far_im.rest_1_ = bf16[4,1,256,512]{3,2,1,0:T(8,128)(2,1)} collective-permute-done((bf16[4,1,256,512]{3,2,1,0:T(8,128)(2,1)}, bf16[4,1,256,512]{3,2,1,0:T(8,128)(2,1)}, u32[]{:S(2)}, u32[]{:S(2)}) %collective-permute-start.1) | collective-permute-done | bytes 1048608 | tf_op jit(solution)/shard_map/ppermute | solution.py:20
  97.4 0.0 collective-permute-done.2.rest_0_.far_re
  97.4 3.2 %collective-permute-done.3.rest_1_.far_im = bf16[4,1,256,512]{3,2,1,0:T(8,128)(2,1)} collective-permute-done((bf16[4,1,256,512]{3,2,1,0:T(8,128)(2,1)}, bf16[4,1,256,512]{3,2,1,0:T(8,128)(2,1)}, u32[]{:S(2)}, u32[]{:S(2)}) %collective-permute-start.3) | collective-permute-done | bytes 1048608 | tf_op jit(solution)/shard_map/ppermute | solution.py:20
  100.7 11.9 %shard_map.69 = bf16[8,16,4,32,128]{4,3,2,1,0:T(8,128)(2,1)} custom-call(s32[4]{0:T(128)} %get-tuple-element.20.slot_ref, bf16[4,1,512,512]{3,2,1,0:T(8,128)(2,1)} %own_re.7, bf16[4,1,512,512]{3,2,1,0:T(8,128)(2,1)} %own_im.7, bf16[4,1,256,512]{3,2,1,0:T(8,128)(2,1)} %collective-permute-done.far_re.rest_0_, ...), custom_call_target="tpu_custom_call" | custom-call | flops 4294967296 | bytes 16777216 | tf_op jit(solution)/shard_map/pallas_call | solution.py:103
  112.6 10.6 %all-to-all-start = ((bf16[128,4,32,128]{3,2,1,0:T(8,128)(2,1)}), bf16[128,4,32,128]{3,2,1,0:T(8,128)(2,1)}, u32[]{:S(2)}, u32[]{:S(2)}) async-start(bf16[128,4,32,128]{3,2,1,0:T(8,128)(2,1)} %bitcast.49), calls=%async_computation | async-start | bytes 8388608 | tf_op jit(solution)/shard_map/all_to_all | solution.py:178
  123.1 11.2 %shard_map.70.rest_2_ = f32[4,512,1024]{2,1,0:T(8,128)} custom-call(s32[4]{0:T(128)} %get-tuple-element.21.slot_ref, bf16[4,1,512,512]{3,2,1,0:T(8,128)(2,1)} %own_re.7, bf16[4,1,512,512]{3,2,1,0:T(8,128)(2,1)} %own_im.7, bf16[4,1,256,512]{3,2,1,0:T(8,128)(2,1)} %copy-done.4, bf16[4,1,256,512]{3,2,1,0:T(8,128)(2,1)} %collective-permute-done.7.rest_1_.far_im, ...), custom_call_target="tpu_custom_call" | custom-call | flops 4294967296 | bytes 16777216 | tf_op jit(solution)/shard_map/pallas_call | solution.py:103
  134.4 11.8 %shard_map.71 = bf16[8,16,4,32,128]{4,3,2,1,0:T(8,128)(2,1)} custom-call(s32[4]{0:T(128)} %get-tuple-element.21.slot_ref, bf16[4,1,512,512]{3,2,1,0:T(8,128)(2,1)} %own_re.7, bf16[4,1,512,512]{3,2,1,0:T(8,128)(2,1)} %own_im.7, bf16[4,1,256,512]{3,2,1,0:T(8,128)(2,1)} %collective-permute-done.2.rest_0_.far_re, ...), custom_call_target="tpu_custom_call" | custom-call | flops 4294967296 | bytes 16777216 | tf_op jit(solution)/shard_map/pallas_call | solution.py:103
  146.2 27.3 %all-to-all-done = bf16[128,4,32,128]{3,2,1,0:T(8,128)(2,1)} async-done(((bf16[128,4,32,128]{3,2,1,0:T(8,128)(2,1)}), bf16[128,4,32,128]{3,2,1,0:T(8,128)(2,1)}, u32[]{:S(2)}, u32[]{:S(2)}) %all-to-all-start) | async-done | bytes 4194336 | tf_op jit(solution)/shard_map/all_to_all | solution.py:178
  173.5 0.0 copy-start.5
  173.5 0.0 copy-start.6
  173.5 8.0 %all-to-all-start.1 = ((bf16[128,4,32,128]{3,2,1,0:T(8,128)(2,1)}), bf16[128,4,32,128]{3,2,1,0:T(8,128)(2,1)}, u32[]{:S(2)}, u32[]{:S(2)}) async-start(bf16[128,4,32,128]{3,2,1,0:T(8,128)(2,1)} %bitcast.48), calls=%async_computation.1 | async-start | bytes 8388608 | tf_op jit(solution)/shard_map/all_to_all | solution.py:178
  181.6 0.0 copy-done.5
  181.7 0.0 copy-done.6
  181.9 0.1 copy_bitcast_fusion.2
  182.0 0.1 copy_bitcast_fusion
  182.1 11.6 %fusion.4 = f32[32,128,512]{2,1,0:T(8,128)} fusion(bf16[128,4,32,128]{3,2,1,0:T(8,128)(2,1)} %all-to-all-done, bf16[128,4,256]{2,0,1:T(8,128)(2,1)S(1)} %get-tuple-element.26, bf16[128,4,256]{2,0,1:T(8,128)(2,1)S(1)} %get-tuple-element.27), kind=kOutput, calls=%fused_computation.4 | convolution fusion | flops 2148532224 | bytes 13107200 | tf_op jit(solution)/shard_map/swrn,swx->rnx/dot_general | solution.py:185
  193.7 38.4 %all-to-all-done.1 = bf16[128,4,32,128]{3,2,1,0:T(8,128)(2,1)} async-done(((bf16[128,4,32,128]{3,2,1,0:T(8,128)(2,1)}), bf16[128,4,32,128]{3,2,1,0:T(8,128)(2,1)}, u32[]{:S(2)}, u32[]{:S(2)}) %all-to-all-start.1) | async-done | bytes 4194336 | tf_op jit(solution)/shard_map/all_to_all | solution.py:178
  232.0 0.0 copy-start.1
  232.0 8.7 %fusion.7 = f32[32,128,512]{2,1,0:T(8,128)S(1)} fusion(bf16[128,4,32,128]{3,2,1,0:T(8,128)(2,1)} %all-to-all-done.1, bf16[128,4,256]{2,0,1:T(8,128)(2,1)S(1)} %get-tuple-element.24, bf16[128,4,256]{2,0,1:T(8,128)(2,1)S(1)} %get-tuple-element.25), kind=kOutput, calls=%fused_computation.5 | convolution fusion | flops 2148532224 | bytes 13107200 | tf_op jit(solution)/shard_map/swrn,swx->rnx/dot_general | solution.py:185
  240.7 0.0 copy-done.1
  240.7 0.6 fusion.10
  241.4 1.6 fusion.30
  (11 shorter events, 0.2 us)
Async XLA Ops:
  0.6 5.9 %copy-start = (bf16[4,1,512,512]{3,2,1,0:T(8,128)(2,1)S(1)}, bf16[4,1,512,512]{3,2,1,0:T(8,128)(2,1)}, u32[]{:S(2)}) copy-start(bf16[4,1,512,512]{3,2,1,0:T(8,128)(2,1)} %own_im.7) | copy-start | bytes 6291460
  3.5 27.5 %collective-permute-start.4 = (bf16[4,1,256,512]{3,2,1,0:T(8,128)(2,1)S(1)}, bf16[4,1,256,512]{3,2,1,0:T(8,128)(2,1)S(1)}, u32[]{:S(2)}, u32[]{:S(2)}) collective-permute-start(bf16[4,1,256,512]{3,2,1,0:T(8,128)(2,1)S(1)} %get-tuple-element.6), channel_id=1, source_target_pairs={{0,16},{16,0},{32,48},{48,32},{64,80},{80,64},{96,112},{112,96},{1... | collective-permute-start | bytes 3145736 | tf_op jit(solution)/shard_map/ppermute | solution.py:20
  8.1 45.4 %collective-permute-start.5 = (bf16[4,1,256,512]{3,2,1,0:T(8,128)(2,1)}, bf16[4,1,256,512]{3,2,1,0:T(8,128)(2,1)S(1)}, u32[]{:S(2)}, u32[]{:S(2)}) collective-permute-start(bf16[4,1,256,512]{3,2,1,0:T(8,128)(2,1)} %get-tuple-element.4), channel_id=1, source_target_pairs={{0,16},{16,0},{32,48},{48,32},{64,80},{80,64},{96,112},{112,96},{1... | collective-permute-start | bytes 3145736 | tf_op jit(solution)/shard_map/ppermute | solution.py:20
  8.6 47.9 %collective-permute-start.6 = (bf16[4,1,256,512]{3,2,1,0:T(8,128)(2,1)S(1)}, bf16[4,1,256,512]{3,2,1,0:T(8,128)(2,1)S(1)}, u32[]{:S(2)}, u32[]{:S(2)}) collective-permute-start(bf16[4,1,256,512]{3,2,1,0:T(8,128)(2,1)S(1)} %get-tuple-element.6), channel_id=1, source_target_pairs={{0,32},{32,0},{16,48},{48,16},{64,96},{96,64},{80,112},{112,80},{1... | collective-permute-start | bytes 3145736 | tf_op jit(solution)/shard_map/ppermute | solution.py:20
  10.6 63.1 %collective-permute-start.7 = (bf16[4,1,256,512]{3,2,1,0:T(8,128)(2,1)}, bf16[4,1,256,512]{3,2,1,0:T(8,128)(2,1)}, u32[]{:S(2)}, u32[]{:S(2)}) collective-permute-start(bf16[4,1,256,512]{3,2,1,0:T(8,128)(2,1)} %get-tuple-element.4), channel_id=1, source_target_pairs={{0,32},{32,0},{16,48},{48,16},{64,96},{96,64},{80,112},{112,80},{1... | collective-permute-start | bytes 3145736 | tf_op jit(solution)/shard_map/ppermute | solution.py:20
  10.7 74.2 %collective-permute-start = (bf16[4,1,256,512]{3,2,1,0:T(8,128)(2,1)}, bf16[4,1,256,512]{3,2,1,0:T(8,128)(2,1)}, u32[]{:S(2)}, u32[]{:S(2)}) collective-permute-start(bf16[4,1,256,512]{3,2,1,0:T(8,128)(2,1)} %get-tuple-element.7), channel_id=1, source_target_pairs={{0,16},{16,0},{32,48},{48,32},{64,80},{80,64},{96,112},{112,96},{1... | collective-permute-start | bytes 3145736 | tf_op jit(solution)/shard_map/ppermute | solution.py:20
  31.1 38.9 %copy-start.2 = (bf16[4,1,256,512]{3,2,1,0:T(8,128)(2,1)}, bf16[4,1,256,512]{3,2,1,0:T(8,128)(2,1)S(1)}, u32[]{:S(2)}) copy-start(bf16[4,1,256,512]{3,2,1,0:T(8,128)(2,1)S(1)} %collective-permute-done.4.far_re.rest_0_) | copy-start | bytes 3145732
  31.1 66.4 %collective-permute-start.2 = (bf16[4,1,256,512]{3,2,1,0:T(8,128)(2,1)}, bf16[4,1,256,512]{3,2,1,0:T(8,128)(2,1)}, u32[]{:S(2)}, u32[]{:S(2)}) collective-permute-start(bf16[4,1,256,512]{3,2,1,0:T(8,128)(2,1)} %get-tuple-element.7), channel_id=1, source_target_pairs={{0,32},{32,0},{16,48},{48,16},{64,96},{96,64},{80,112},{112,80},{1... | collective-permute-start | bytes 3145736 | tf_op jit(solution)/shard_map/ppermute | solution.py:20
  53.5 16.4 %copy-start.3 = (bf16[4,1,256,512]{3,2,1,0:T(8,128)(2,1)}, bf16[4,1,256,512]{3,2,1,0:T(8,128)(2,1)S(1)}, u32[]{:S(2)}) copy-start(bf16[4,1,256,512]{3,2,1,0:T(8,128)(2,1)S(1)} %collective-permute-done.5.far_im.rest_1_) | copy-start | bytes 3145732
  53.5 43.9 %collective-permute-start.1 = (bf16[4,1,256,512]{3,2,1,0:T(8,128)(2,1)}, bf16[4,1,256,512]{3,2,1,0:T(8,128)(2,1)}, u32[]{:S(2)}, u32[]{:S(2)}) collective-permute-start(bf16[4,1,256,512]{3,2,1,0:T(8,128)(2,1)} %get-tuple-element.5), channel_id=1, source_target_pairs={{0,16},{16,0},{32,48},{48,32},{64,80},{80,64},{96,112},{112,96},{1... | collective-permute-start | bytes 3145736 | tf_op jit(solution)/shard_map/ppermute | solution.py:20
  56.6 13.4 %copy-start.4 = (bf16[4,1,256,512]{3,2,1,0:T(8,128)(2,1)}, bf16[4,1,256,512]{3,2,1,0:T(8,128)(2,1)S(1)}, u32[]{:S(2)}) copy-start(bf16[4,1,256,512]{3,2,1,0:T(8,128)(2,1)S(1)} %collective-permute-done.6.rest_0_.far_re) | copy-start | bytes 3145732
  56.6 44.1 %collective-permute-start.3 = (bf16[4,1,256,512]{3,2,1,0:T(8,128)(2,1)}, bf16[4,1,256,512]{3,2,1,0:T(8,128)(2,1)}, u32[]{:S(2)}, u32[]{:S(2)}) collective-permute-start(bf16[4,1,256,512]{3,2,1,0:T(8,128)(2,1)} %get-tuple-element.5), channel_id=1, source_target_pairs={{0,32},{32,0},{16,48},{48,16},{64,96},{96,64},{80,112},{112,80},{1... | collective-permute-start | bytes 3145736 | tf_op jit(solution)/shard_map/ppermute | solution.py:20
  62.3 10.8 %copy-start.7 = (s32[2,4]{1,0:T(2,128)S(1)}, s32[2,4]{1,0:T(2,128)}, u32[]{:S(2)}) copy-start(s32[2,4]{1,0:T(2,128)} %param.7) | copy-start | bytes 100
  112.6 61.0 %all-to-all-start = ((bf16[128,4,32,128]{3,2,1,0:T(8,128)(2,1)}), bf16[128,4,32,128]{3,2,1,0:T(8,128)(2,1)}, u32[]{:S(2)}, u32[]{:S(2)}) async-start(bf16[128,4,32,128]{3,2,1,0:T(8,128)(2,1)} %bitcast.49), calls=%async_computation | async-start | bytes 8388608 | tf_op jit(solution)/shard_map/all_to_all | solution.py:178
  173.5 8.1 %copy-start.5 = (bf16[32,2,16,128]{3,2,1,0:T(8,128)(2,1)S(1)}, bf16[32,2,16,128]{3,2,1,0:T(8,128)(2,1)}, u32[]{:S(2)}) copy-start(bf16[32,2,16,128]{3,2,1,0:T(8,128)(2,1)} %param.9) | copy-start | bytes 786436
  173.5 8.1 %copy-start.6 = (bf16[32,2,16,128]{3,2,1,0:T(8,128)(2,1)S(1)}, bf16[32,2,16,128]{3,2,1,0:T(8,128)(2,1)}, u32[]{:S(2)}) copy-start(bf16[32,2,16,128]{3,2,1,0:T(8,128)(2,1)} %param.8) | copy-start | bytes 786436
  173.5 58.5 %all-to-all-start.1 = ((bf16[128,4,32,128]{3,2,1,0:T(8,128)(2,1)}), bf16[128,4,32,128]{3,2,1,0:T(8,128)(2,1)}, u32[]{:S(2)}, u32[]{:S(2)}) async-start(bf16[128,4,32,128]{3,2,1,0:T(8,128)(2,1)} %bitcast.48), calls=%async_computation.1 | async-start | bytes 8388608 | tf_op jit(solution)/shard_map/all_to_all | solution.py:178
  232.0 8.7 %copy-start.1 = (f32[32,128,512]{2,1,0:T(8,128)S(1)}, f32[32,128,512]{2,1,0:T(8,128)}, u32[]{:S(2)}) copy-start(f32[32,128,512]{2,1,0:T(8,128)} %fusion.4) | copy-start | bytes 25165828

commit v10 on v8

--- a/solution.py
+++ b/solution.py
@@ -70,32 +70,34 @@
         out_ref[block, :, 0, :, :] = spec.reshape(groups, rows_per, lanes)
 
 
-def spectra(slots, own_re, own_im, far_re, far_im, col_a, row_re, row_im, blocks, groups, after):
-    waves, _, rows, cols = own_re.shape
-    lanes = 2 * cols // blocks
-    rows_per = rows // groups
-    field = pl.BlockSpec((1, 1, rows, cols), lambda i, sl: (i, 0, 0, 0))
-    partner = pl.BlockSpec((1, 1, rows, cols), lambda i, sl: (sl[i], 0, 0, 0))
+def spectra(slots, own_re, own_im, far_re, far_im, tables, shape, first, waves, slot, after, into):
+    col_a, row_re, row_im = tables
+    _, _, rows, cols = own_re.shape
+    blocks, groups, _, rows_per, lanes = shape
+    field = pl.BlockSpec((1, 1, rows, cols), lambda i, sl: (first + i, 0, 0, 0))
+    partner = pl.BlockSpec((1, 1, rows, cols), lambda i, sl: (sl[first + i], 0, 0, 0))
     whole_col = pl.BlockSpec((2 * cols, 2 * cols), lambda i, sl: (0, 0))
     whole_row = pl.BlockSpec((rows, rows), lambda i, sl: (0, 0))
     flops = waves * (2 * rows * (2 * cols) * (2 * cols) + 2 * 2 * rows * rows * (2 * cols))
+    extra = list(after) + ([] if into is None else [into])
     return pl.pallas_call(
         spectrum_kernel,
-        out_shape=jax.ShapeDtypeStruct((blocks, groups, waves, rows_per, lanes), jnp.bfloat16),
+        out_shape=jax.ShapeDtypeStruct(shape, jnp.bfloat16),
         grid_spec=pltpu.PrefetchScalarGridSpec(
             num_scalar_prefetch=1,
             grid=(waves,),
             in_specs=[field, field, partner, partner, whole_col, whole_row, whole_row]
-            + [pl.BlockSpec(memory_space=pl.ANY)] * len(after),
+            + [pl.BlockSpec(memory_space=pl.ANY)] * len(extra),
             out_specs=pl.BlockSpec(
-                (blocks, groups, 1, rows_per, lanes), lambda i, sl: (0, 0, i, 0, 0)
+                (blocks, groups, 1, rows_per, lanes), lambda i, sl: (0, 0, slot + i, 0, 0)
             ),
         ),
+        input_output_aliases={} if into is None else {8 + len(after): 0},
         compiler_params=pltpu.CompilerParams(vmem_limit_bytes=60 * 1024 * 1024),
         cost_estimate=pl.CostEstimate(
             flops=flops, transcendentals=0, bytes_accessed=waves * rows * cols * 12 + 12 * cols * cols
         ),
-    )(slots, own_re, own_im, far_re, far_im, col_a, row_re, row_im, *after)
+    )(slots, own_re, own_im, far_re, far_im, col_a, row_re, row_im, *extra)
 
 
 def shards(hologram_real, hologram_imaginary, pair_slot, kernel_real, kernel_imaginary):
@@ -107,44 +109,57 @@
     depth_count = kernel_real.shape[3]
     row_real, row_imag = dft_tables(row_count)
     col_real, col_imag = dft_tables(col_count)
-    col_a = column_tables(col_real, col_imag, wave_devices)
+    tables = (column_tables(col_real, col_imag, wave_devices), row_real, row_imag)
+    lanes = 2 * col_count // wave_devices
+    rows_per = row_count // angle_devices
 
     def all_weights(kernel_part):
         block = kernel_part.reshape(
             wave_devices, local_waves, section_count, angle_devices, depth_count
         )
-        return jnp.transpose(block, (2, 0, 3, 1, 4)).reshape(
-            section_count, wave_devices * angle_devices, local_waves, depth_count
+        return jnp.transpose(block, (0, 3, 2, 1, 4)).reshape(
+            wave_devices * angle_devices, section_count * local_waves, depth_count
         )
 
     k_re = all_weights(kernel_real)
     k_im = all_weights(kernel_imaginary)
-    volume = None
     received = [
         from_partner((hologram_real, hologram_imaginary), "wave", section_number)
         for section_number in range(section_count)
     ]
-    for section_number in range(section_count):
-        got_real, got_imag = received[section_number]
-        after = [a for other, got in enumerate(received) if other != section_number for a in got]
-        send = spectra(
-            pair_slot[section_number],
-            hologram_real,
-            hologram_imaginary,
-            got_real,
-            got_imag,
-            col_a,
-            row_real,
-            row_imag,
-            wave_devices,
-            angle_devices,
-            after,
-        )
+    total = section_count * local_waves
+    small = local_waves // 2
+    split = [(total - small, total), (0, total - small)]
+    volume = None
+    for low, high in split:
+        shape = (wave_devices, angle_devices, high - low, rows_per, lanes)
+        send = None
+        for section_number in range(section_count):
+            lo = max(low, section_number * local_waves)
+            hi = min(high, (section_number + 1) * local_waves)
+            if lo >= hi:
+                continue
+            got_real, got_imag = received[section_number]
+            after = [a for other, got in enumerate(received) if other != section_number for a in got]
+            send = spectra(
+                pair_slot[section_number],
+                hologram_real,
+                hologram_imaginary,
+                got_real,
+                got_imag,
+                tables,
+                shape,
+                lo - section_number * local_waves,
+                hi - lo,
+                lo - low,
+                after,
+                send,
+            )
         send = send.reshape(wave_devices * angle_devices, *send.shape[2:])
         got = lax.all_to_all(send, ("wave", "angle"), 0, 0, tiled=True)
         got = with_layout_constraint(got, Layout(tuple(range(got.ndim))))
-        kr = k_re[section_number]
-        ki = k_im[section_number]
+        kr = k_re[:, low:high]
+        ki = k_im[:, low:high]
         w_first = jnp.stack([kr, ki], axis=2).reshape(kr.shape[0], kr.shape[1], -1)
         w_second = jnp.stack([-ki, kr], axis=2).reshape(kr.shape[0], kr.shape[1], -1)
         both = jnp.concatenate([w_first, w_second], axis=2)

time: 245 us -> 239 us (0.976)
  waiting for transfers between devices: 146 us -> 137 us
  matrix products: 20.3 us -> 13.8 us
  Pallas kernels: 29.5 us -> 33.9 us
  local copies, waits for them, and re-layouts: 3.4 us -> 5.9 us
  other arithmetic: 17 us -> 19.5 us
    dot_general x2, matrix products: 20.3 us -> 13.8 us  [shards(): t = jnp.einsum('swrn,swx->rnx', got, both, preferred_element_type=fp)]
    ppermute x4, waiting for transfers between devices: 72.4 us -> 67.4 us  [from_partner(): return lax.ppermute(block, axis, route)]
    pallas_call x2 -> x3, Pallas kernels: 29.5 us -> 33.9 us  [spectra(): pl.pallas_call(spectrum_kernel, out_shape=jax.ShapeDtypeStruct(shape, jnp...]
    all_to_all x2, waiting for transfers between devices: 74 us -> 69.8 us  [shards(): got = lax.all_to_all(send, ('wave', 'angle'), 0, 0, tiled=True)]
  transfers between devices with their start and end apart: 6 -> 6, of which waited for: 6 -> 5; matrix products, arithmetic and copies ran while one was open for 12% -> 13% of each run, Pallas kernels for 6% -> 10%
where the time goes in v10:
time: 239 us; the launch traced here: 235 us
  waiting for transfers between devices  137 us (57%)
  Pallas kernels  33.9 us (14%)
  starting transfers between devices  23.5 us (10%)
  other arithmetic  19.5 us (8%)
  matrix products  13.8 us (6%)
  local copies, waits for them, and re-layouts  5.9 us (2%)
    all_to_all x2, waiting for transfers between devices, shards(): got = lax.all_to_all(send, ('wave', 'angle'), 0, 0, tiled=True)  69.8 us
    ppermute x4, waiting for transfers between devices, from_partner(): return lax.ppermute(block, axis, route)  67.4 us
    pallas_call x3, Pallas kernels, spectra(): pl.pallas_call(spectrum_kernel, out_shape=jax.ShapeDtypeStruct(shape, jnp...  33.9 us
    all_to_all x2, starting transfers between devices, shards(): got = lax.all_to_all(send, ('wave', 'angle'), 0, 0, tiled=True)  17.9 us
    dot_general x2, matrix products, shards(): t = jnp.einsum('swrn,swx->rnx', got, both, preferred_element_type=fp)  13.8 us
    convert_element_type x2, other arithmetic, dft_tables(): (-jnp.sin(phase) * factor).astype(jnp.bfloat16)  10.3 us
    ppermute x4, starting transfers between devices, from_partner(): return lax.ppermute(block, axis, route)  5.64 us
  transfers between devices with their start and end apart: 6, of which 5 were waited for; matrix products, arithmetic and copies ran while one was open for 13% of the time, Pallas kernels for 10%

profile of v10, /device:TPU:24, one launch (start us, length us, event | category | flops | bytes accessed | tf_op | source)
XLA Modules:
  0.0 234.7 jit_solution(17725264717347357534)
XLA Ops:
  0.6 2.0 collective-permute-start
  2.6 0.1 collective-permute-start.1
  2.7 3.0 %collective-permute-start.2 = (bf16[4,1,512,512]{3,2,1,0:T(8,128)(2,1)}, bf16[4,1,512,512]{3,2,1,0:T(8,128)(2,1)}, u32[]{:S(2)}, u32[]{:S(2)}) collective-permute-start(bf16[4,1,512,512]{3,2,1,0:T(8,128)(2,1)} %own_re.5), channel_id=1, source_target_pairs={{0,16},{16,0},{32,48},{48,32},{64,80},{80,64},{96,112},{112,96},{1... | collective-permute-start | bytes 6291464 | tf_op jit(solution)/shard_map/ppermute | solution.py:20
  5.8 0.5 collective-permute-start.3
  6.3 4.3 %fusion.23 = bf16[512,8,1,64]{0,3,2,1:T(8,128)(2,1)S(1)} fusion(s32[8,64]{1,0:T(8,128)S(1)} %multiply_add_fusion), kind=kLoop, calls=%fused_computation.46 | loop fusion | flops 5242880 | bytes 526336 | tf_op jit(solution)/shard_map/neg | solution.py:44
  10.6 4.9 %multiply_convert_fusion.2 = (bf16[512,8,1,64]{0,3,2,1:T(8,128)(2,1)S(1)}, bf16[512,8,1,64]{0,3,2,1:T(8,128)(2,1)S(1)}) fusion(s32[8,64]{1,0:T(8,128)S(1)} %multiply_add_fusion), kind=kLoop, calls=%fused_computation.27 | loop fusion | flops 4980736 | bytes 1050624 | tf_op jit(solution)/shard_map/convert_element_type | solution.py:30
  15.5 1.1 pad_maximum_fusion.1
  16.6 2.3 copy.15
  18.9 1.3 copy.16
  20.2 5.3 %multiply_convert_fusion = (bf16[512,512]{1,0:T(8,128)(2,1)}, bf16[512,512]{1,0:T(8,128)(2,1)}) fusion(), kind=kLoop, calls=%fused_computation.23 | loop fusion | flops 4980736 | bytes 1048576 | tf_op jit(solution)/shard_map/convert_element_type | solution.py:30
  25.5 0.0 copy-start.4
  25.5 3.1 %pad_maximum_fusion.col_a = bf16[1024,1024]{1,0:T(8,128)(2,1)} fusion(bf16[512,1024]{1,0:T(8,128)(2,1)} %copy.16, bf16[512,1024]{1,0:T(8,128)(2,1)} %copy.15), kind=kLoop, calls=%fused_computation.7 | loop fusion | flops 4194304 | bytes 4194304 | tf_op jit(solution)/shard_map/concatenate | solution.py:42
  28.6 0.0 copy-done.4
  28.6 0.5 slice_bitcast_fusion.4
  29.2 20.3 %collective-permute-done.far_re.rest_0_ = bf16[4,1,512,512]{3,2,1,0:T(8,128)(2,1)S(1)} collective-permute-done((bf16[4,1,512,512]{3,2,1,0:T(8,128)(2,1)}, bf16[4,1,512,512]{3,2,1,0:T(8,128)(2,1)S(1)}, u32[]{:S(2)}, u32[]{:S(2)}) %collective-permute-start) | collective-permute-done | bytes 2097184 | tf_op jit(solution)/shard_map/ppermute | solution.py:20
  49.4 0.0 copy-start.1
  49.4 44.1 %collective-permute-done.1.far_im.rest_1_ = bf16[4,1,512,512]{3,2,1,0:T(8,128)(2,1)} collective-permute-done((bf16[4,1,512,512]{3,2,1,0:T(8,128)(2,1)}, bf16[4,1,512,512]{3,2,1,0:T(8,128)(2,1)}, u32[]{:S(2)}, u32[]{:S(2)}) %collective-permute-start.1) | collective-permute-done | bytes 2097184 | tf_op jit(solution)/shard_map/ppermute | solution.py:20
  93.5 0.0 collective-permute-done.2.rest_0_.far_re
  93.5 3.1 %collective-permute-done.3.rest_1_.far_im = bf16[4,1,512,512]{3,2,1,0:T(8,128)(2,1)} collective-permute-done((bf16[4,1,512,512]{3,2,1,0:T(8,128)(2,1)}, bf16[4,1,512,512]{3,2,1,0:T(8,128)(2,1)}, u32[]{:S(2)}, u32[]{:S(2)}) %collective-permute-start.3) | collective-permute-done | bytes 2097184 | tf_op jit(solution)/shard_map/ppermute | solution.py:20
  96.6 0.0 copy-done.1
  96.6 9.6 %shard_map.68 = bf16[8,16,2,32,128]{4,3,2,1,0:T(8,128)(2,1)} custom-call(s32[4]{0:T(128)} %get-tuple-element.17.slot_ref, bf16[4,1,512,512]{3,2,1,0:T(8,128)(2,1)} %own_re.5, bf16[4,1,512,512]{3,2,1,0:T(8,128)(2,1)} %own_im.5, bf16[4,1,512,512]{3,2,1,0:T(8,128)(2,1)} %copy-done.1, bf16[4,1,512,512]{3,2,1,0:T(8,128)(2,1)} %collective-permute-done.1.far_im.rest_1_, ...), custom_call_target="tpu_custom_call" | custom-call | flops 4294967296 | bytes 9437184 | tf_op jit(solution)/shard_map/pallas_call | solution.py:83
  106.2 10.0 %all-to-all-start = ((bf16[128,2,32,128]{3,2,1,0:T(8,128)(2,1)}), bf16[128,2,32,128]{3,2,1,0:T(8,128)(2,1)S(1)}, u32[]{:S(2)}, u32[]{:S(2)}) async-start(bf16[128,2,32,128]{3,2,1,0:T(8,128)(2,1)} %bitcast.57), calls=%async_computation | async-start | bytes 4194304 | tf_op jit(solution)/shard_map/all_to_all | solution.py:159
  116.2 14.8 %shard_map.69.rest_2_ = bf16[8,16,6,32,128]{4,3,2,1,0:T(8,128)(2,1)} custom-call(s32[4]{0:T(128)} %get-tuple-element.16.slot_ref, bf16[4,1,512,512]{3,2,1,0:T(8,128)(2,1)} %own_re.5, bf16[4,1,512,512]{3,2,1,0:T(8,128)(2,1)} %own_im.5, bf16[4,1,512,512]{3,2,1,0:T(8,128)(2,1)} %collective-permute-done.2.rest_0_.far_re, ...), custom_call_target="tpu_custom_call" | custom-call | flops 8589934592 | bytes 15728640 | tf_op jit(solution)/shard_map/pallas_call | solution.py:83
  130.9 9.5 %shard_map.70 = bf16[8,16,6,32,128]{4,3,2,1,0:T(8,128)(2,1)} custom-call(s32[4]{0:T(128)} %get-tuple-element.17.slot_ref, bf16[4,1,512,512]{3,2,1,0:T(8,128)(2,1)} %own_re.5, bf16[4,1,512,512]{3,2,1,0:T(8,128)(2,1)} %own_im.5, bf16[4,1,512,512]{3,2,1,0:T(8,128)(2,1)} %copy-done.1, ...), custom_call_target="tpu_custom_call", output_to_operand_aliasing={{}: (10, {})} | custom-call | flops 4294967296 | bytes 9437184 | tf_op jit(solution)/shard_map/pallas_call | solution.py:83
  140.5 4.0 %all-to-all-done = bf16[128,2,32,128]{3,2,1,0:T(8,128)(2,1)S(1)} async-done(((bf16[128,2,32,128]{3,2,1,0:T(8,128)(2,1)}), bf16[128,2,32,128]{3,2,1,0:T(8,128)(2,1)S(1)}, u32[]{:S(2)}, u32[]{:S(2)}) %all-to-all-start) | async-done | bytes 2097184 | tf_op jit(solution)/shard_map/all_to_all | solution.py:159
  144.5 0.0 copy-start.2
  144.5 0.0 copy-start.3
  144.5 7.9 %all-to-all-start.1 = ((bf16[128,6,32,128]{3,2,1,0:T(8,128)(2,1)}), bf16[128,6,32,128]{3,2,1,0:T(8,128)(2,1)}, u32[]{:S(2)}, u32[]{:S(2)}) async-start(bf16[128,6,32,128]{3,2,1,0:T(8,128)(2,1)} %bitcast.56), calls=%async_computation.1 | async-start | bytes 12582912 | tf_op jit(solution)/shard_map/all_to_all | solution.py:159
  152.4 0.0 copy-done.2
  152.5 0.0 copy-done.3
  152.6 0.1 maximum_bitcast_fusion.2
  152.7 0.1 copy_bitcast_fusion
  152.9 6.5 %convolution_bitcast_fusion = f32[32,128,512]{2,1,0:T(8,128)} fusion(bf16[128,2,32,128]{3,2,1,0:T(8,128)(2,1)S(1)} %all-to-all-done, bf16[128,2,256]{2,0,1:T(8,128)(2,1)S(1)} %get-tuple-element.22, bf16[128,2,256]{2,0,1:T(8,128)(2,1)S(1)} %get-tuple-element.23), kind=kOutput, calls=%fused_computation.3 | convolution fusion | flops 1074266112 | bytes 10747904 | tf_op jit(solution)/shard_map/swrn,swx->rnx/dot_general | solution.py:166
  159.3 65.7 %all-to-all-done.1 = bf16[128,6,32,128]{3,2,1,0:T(8,128)(2,1)} async-done(((bf16[128,6,32,128]{3,2,1,0:T(8,128)(2,1)}), bf16[128,6,32,128]{3,2,1,0:T(8,128)(2,1)}, u32[]{:S(2)}, u32[]{:S(2)}) %all-to-all-start.1) | async-done | bytes 6291488 | tf_op jit(solution)/shard_map/all_to_all | solution.py:159
  225.0 0.0 copy-start
  225.0 7.4 %fusion.2 = f32[32,128,512]{2,1,0:T(8,128)S(1)} fusion(bf16[128,6,32,128]{3,2,1,0:T(8,128)(2,1)} %all-to-all-done.1, bf16[128,6,256]{2,0,1:T(8,128)(2,1)S(1)} %get-tuple-element.20, bf16[128,6,256]{2,0,1:T(8,128)(2,1)S(1)} %get-tuple-element.21), kind=kOutput, calls=%fused_computation.2 | convolution fusion | flops 3222798336 | bytes 15466496 | tf_op jit(solution)/shard_map/swrn,swx->rnx/dot_general | solution.py:166
  232.4 0.0 copy-done
  232.4 0.6 fusion.5
  233.0 1.6 fusion.26
  (9 shorter events, 0.2 us)
Async XLA Ops:
  0.6 48.8 %collective-permute-start = (bf16[4,1,512,512]{3,2,1,0:T(8,128)(2,1)}, bf16[4,1,512,512]{3,2,1,0:T(8,128)(2,1)S(1)}, u32[]{:S(2)}, u32[]{:S(2)}) collective-permute-start(bf16[4,1,512,512]{3,2,1,0:T(8,128)(2,1)} %own_re.5), channel_id=1, source_target_pairs={{0,32},{32,0},{16,48},{48,16},{64,96},{96,64},{80,112},{112,80},{1... | collective-permute-start | bytes 6291464 | tf_op jit(solution)/shard_map/ppermute | solution.py:20
  2.6 90.9 %collective-permute-start.1 = (bf16[4,1,512,512]{3,2,1,0:T(8,128)(2,1)}, bf16[4,1,512,512]{3,2,1,0:T(8,128)(2,1)}, u32[]{:S(2)}, u32[]{:S(2)}) collective-permute-start(bf16[4,1,512,512]{3,2,1,0:T(8,128)(2,1)} %own_im.5), channel_id=1, source_target_pairs={{0,32},{32,0},{16,48},{48,16},{64,96},{96,64},{80,112},{112,80},{1... | collective-permute-start | bytes 6291464 | tf_op jit(solution)/shard_map/ppermute | solution.py:20
  2.7 90.8 %collective-permute-start.2 = (bf16[4,1,512,512]{3,2,1,0:T(8,128)(2,1)}, bf16[4,1,512,512]{3,2,1,0:T(8,128)(2,1)}, u32[]{:S(2)}, u32[]{:S(2)}) collective-permute-start(bf16[4,1,512,512]{3,2,1,0:T(8,128)(2,1)} %own_re.5), channel_id=1, source_target_pairs={{0,16},{16,0},{32,48},{48,32},{64,80},{80,64},{96,112},{112,96},{1... | collective-permute-start | bytes 6291464 | tf_op jit(solution)/shard_map/ppermute | solution.py:20
  5.8 90.8 %collective-permute-start.3 = (bf16[4,1,512,512]{3,2,1,0:T(8,128)(2,1)}, bf16[4,1,512,512]{3,2,1,0:T(8,128)(2,1)}, u32[]{:S(2)}, u32[]{:S(2)}) collective-permute-start(bf16[4,1,512,512]{3,2,1,0:T(8,128)(2,1)} %own_im.5), channel_id=1, source_target_pairs={{0,16},{16,0},{32,48},{48,32},{64,80},{80,64},{96,112},{112,96},{1... | collective-permute-start | bytes 6291464 | tf_op jit(solution)/shard_map/ppermute | solution.py:20
  25.5 3.1 %copy-start.4 = (s32[2,4]{1,0:T(2,128)S(1)}, s32[2,4]{1,0:T(2,128)}, u32[]{:S(2)}) copy-start(s32[2,4]{1,0:T(2,128)} %param.7) | copy-start | bytes 100
  49.4 47.2 %copy-start.1 = (bf16[4,1,512,512]{3,2,1,0:T(8,128)(2,1)}, bf16[4,1,512,512]{3,2,1,0:T(8,128)(2,1)S(1)}, u32[]{:S(2)}) copy-start(bf16[4,1,512,512]{3,2,1,0:T(8,128)(2,1)S(1)} %collective-permute-done.far_re.rest_0_) | copy-start | bytes 6291460
  106.2 38.4 %all-to-all-start = ((bf16[128,2,32,128]{3,2,1,0:T(8,128)(2,1)}), bf16[128,2,32,128]{3,2,1,0:T(8,128)(2,1)S(1)}, u32[]{:S(2)}, u32[]{:S(2)}) async-start(bf16[128,2,32,128]{3,2,1,0:T(8,128)(2,1)} %bitcast.57), calls=%async_computation | async-start | bytes 4194304 | tf_op jit(solution)/shard_map/all_to_all | solution.py:159
  144.5 7.9 %copy-start.2 = (bf16[32,2,16,128]{3,2,1,0:T(8,128)(2,1)S(1)}, bf16[32,2,16,128]{3,2,1,0:T(8,128)(2,1)}, u32[]{:S(2)}) copy-start(bf16[32,2,16,128]{3,2,1,0:T(8,128)(2,1)} %param.9) | copy-start | bytes 786436
  144.5 7.9 %copy-start.3 = (bf16[32,2,16,128]{3,2,1,0:T(8,128)(2,1)S(1)}, bf16[32,2,16,128]{3,2,1,0:T(8,128)(2,1)}, u32[]{:S(2)}) copy-start(bf16[32,2,16,128]{3,2,1,0:T(8,128)(2,1)} %param.8) | copy-start | bytes 786436
  144.5 80.5 %all-to-all-start.1 = ((bf16[128,6,32,128]{3,2,1,0:T(8,128)(2,1)}), bf16[128,6,32,128]{3,2,1,0:T(8,128)(2,1)}, u32[]{:S(2)}, u32[]{:S(2)}) async-start(bf16[128,6,32,128]{3,2,1,0:T(8,128)(2,1)} %bitcast.56), calls=%async_computation.1 | async-start | bytes 12582912 | tf_op jit(solution)/shard_map/all_to_all | solution.py:159
  225.0 7.4 %copy-start = (f32[32,128,512]{2,1,0:T(8,128)S(1)}, f32[32,128,512]{2,1,0:T(8,128)}, u32[]{:S(2)}) copy-start(f32[32,128,512]{2,1,0:T(8,128)} %convolution_bitcast_fusion) | copy-start | bytes 25165828

commit v11 on v10

--- a/solution.py
+++ b/solution.py
@@ -130,6 +130,11 @@
     total = section_count * local_waves
     small = local_waves // 2
     split = [(total - small, total), (0, total - small)]
+    devices = wave_devices * angle_devices
+    warm = lax.all_to_all(
+        hologram_real[0, 0, :devices, :], ("wave", "angle"), 0, 0, tiled=True
+    )
+    warmed = [warm]
     volume = None
     for low, high in split:
         shape = (wave_devices, angle_devices, high - low, rows_per, lanes)
@@ -141,6 +146,8 @@
                 continue
             got_real, got_imag = received[section_number]
             after = [a for other, got in enumerate(received) if other != section_number for a in got]
+            after = after + warmed
+            warmed = []
             send = spectra(
                 pair_slot[section_number],
                 hologram_real,

time: 239 us -> 244 us (1.021)
  waiting for transfers between devices: 137 us -> 129 us
  starting transfers between devices: 23.5 us -> 31.2 us
  local copies, waits for them, and re-layouts: 5.9 us -> 10.1 us
    ppermute x4, waiting for transfers between devices: 67.4 us -> 0.01 us  [from_partner(): return lax.ppermute(block, axis, route)]
    all_to_all x0 -> x1, waiting for transfers between devices: none -> 59.5 us  [shards(): lax.all_to_all(hologram_real[0, 0, :devices, :], ('wave', 'angle'), 0, 0,...]
    all_to_all x0 -> x1, starting transfers between devices: none -> 10.3 us  [shards(): lax.all_to_all(hologram_real[0, 0, :devices, :], ('wave', 'angle'), 0, 0,...]
    unnamed x10 -> x13, local copies, waits for them, and re-layouts: 0.02 us -> 2.74 us
    all_to_all x2, starting transfers between devices: 17.9 us -> 15.3 us  [shards(): got = lax.all_to_all(send, ('wave', 'angle'), 0, 0, tiled=True)]
  transfers between devices with their start and end apart: 6 -> 7, of which waited for: 5 -> 3; matrix products, arithmetic and copies ran while one was open for 13% -> 14% of each run, Pallas kernels for 10% -> 10%
where the time goes in v11:
time: 244 us; the launch traced here: 239 us
  waiting for transfers between devices  129 us (53%)
  Pallas kernels  33.8 us (14%)
  starting transfers between devices  31.2 us (13%)
  other arithmetic  20.2 us (8%)
  matrix products  13.8 us (6%)
  local copies, waits for them, and re-layouts  10.1 us (4%)
    all_to_all x2, waiting for transfers between devices, shards(): got = lax.all_to_all(send, ('wave', 'angle'), 0, 0, tiled=True)  69.8 us
    all_to_all x1, waiting for transfers between devices, shards(): lax.all_to_all(hologram_real[0, 0, :devices, :], ('wave', 'angle'), 0, 0,...  59.5 us
    pallas_call x3, Pallas kernels, spectra(): pl.pallas_call(spectrum_kernel, out_shape=jax.ShapeDtypeStruct(shape, jnp...  33.8 us
    all_to_all x2, starting transfers between devices, shards(): got = lax.all_to_all(send, ('wave', 'angle'), 0, 0, tiled=True)  15.3 us
    dot_general x2, matrix products, shards(): t = jnp.einsum('swrn,swx->rnx', got, both, preferred_element_type=fp)  13.8 us
    convert_element_type x2, other arithmetic, dft_tables(): (-jnp.sin(phase) * factor).astype(jnp.bfloat16)  10.3 us
    all_to_all x1, starting transfers between devices, shards(): lax.all_to_all(hologram_real[0, 0, :devices, :], ('wave', 'angle'), 0, 0,...  10.3 us
    ppermute x4, starting transfers between devices, from_partner(): return lax.ppermute(block, axis, route)  5.64 us
  transfers between devices with their start and end apart: 7, of which 3 were waited for; matrix products, arithmetic and copies ran while one was open for 14% of the time, Pallas kernels for 10%

profile of v11, /device:TPU:24, one launch (start us, length us, event | category | flops | bytes accessed | tf_op | source)
XLA Modules:
  0.0 239.3 jit_solution(13791594597344780686)
XLA Ops:
  0.6 2.0 collective-permute-start
  2.6 0.1 collective-permute-start.1
  2.7 3.0 %collective-permute-start.2 = (bf16[4,1,512,512]{3,2,1,0:T(8,128)(2,1)}, bf16[4,1,512,512]{3,2,1,0:T(8,128)(2,1)}, u32[]{:S(2)}, u32[]{:S(2)}) collective-permute-start(bf16[4,1,512,512]{3,2,1,0:T(8,128)(2,1)} %own_re.5), channel_id=1, source_target_pairs={{0,16},{16,0},{32,48},{48,32},{64,80},{80,64},{96,112},{112,96},{1... | collective-permute-start | bytes 6291464 | tf_op jit(solution)/shard_map/ppermute | solution.py:20
  5.8 0.5 collective-permute-start.3
  6.3 0.9 slice_bitcast_fusion.2
  7.2 0.5 broadcast.227
  7.7 0.7 reduce
  8.4 0.7 reshape.186
  9.1 10.3 %all-to-all-start = ((bf16[128,2,256]{2,1,0:T(2,128)(2,1)}), bf16[128,2,256]{2,1,0:T(2,128)(2,1)S(1)}, u32[]{:S(2)}, u32[]{:S(2)}) async-start(bf16[128,2,256]{2,1,0:T(2,128)(2,1)} %reshape.186), calls=%async_computation | async-start | bytes 262144 | tf_op jit(solution)/shard_map/all_to_all | solution.py:134
  19.3 4.3 %fusion.23 = bf16[512,8,1,64]{0,3,2,1:T(8,128)(2,1)S(1)} fusion(s32[8,64]{1,0:T(8,128)S(1)} %multiply_add_fusion), kind=kLoop, calls=%fused_computation.46 | loop fusion | flops 5242880 | bytes 526336 | tf_op jit(solution)/shard_map/neg | solution.py:44
  23.6 4.9 %multiply_convert_fusion.2 = (bf16[512,8,1,64]{0,3,2,1:T(8,128)(2,1)S(1)}, bf16[512,8,1,64]{0,3,2,1:T(8,128)(2,1)S(1)}) fusion(s32[8,64]{1,0:T(8,128)S(1)} %multiply_add_fusion), kind=kLoop, calls=%fused_computation.27 | loop fusion | flops 4980736 | bytes 1050624 | tf_op jit(solution)/shard_map/convert_element_type | solution.py:30
  28.6 1.1 pad_maximum_fusion.1
  29.7 2.3 copy.35
  32.0 1.3 copy.36
  33.3 0.0 copy-start.4
  33.3 3.1 %pad_maximum_fusion.col_a = bf16[1024,1024]{1,0:T(8,128)(2,1)} fusion(bf16[512,1024]{1,0:T(8,128)(2,1)} %copy.36, bf16[512,1024]{1,0:T(8,128)(2,1)} %copy.35), kind=kLoop, calls=%fused_computation.7 | loop fusion | flops 4194304 | bytes 4194304 | tf_op jit(solution)/shard_map/concatenate | solution.py:42
  36.4 0.0 copy-done.4
  36.4 0.6 slice_bitcast_fusion.5
  37.0 5.3 %multiply_convert_fusion = (bf16[512,512]{1,0:T(8,128)(2,1)}, bf16[512,512]{1,0:T(8,128)(2,1)}) fusion(), kind=kLoop, calls=%fused_computation.23 | loop fusion | flops 4980736 | bytes 1048576 | tf_op jit(solution)/shard_map/convert_element_type | solution.py:30
  42.3 59.5 %all-to-all-done = bf16[128,2,256]{2,1,0:T(2,128)(2,1)S(1)} async-done(((bf16[128,2,256]{2,1,0:T(2,128)(2,1)}), bf16[128,2,256]{2,1,0:T(2,128)(2,1)S(1)}, u32[]{:S(2)}, u32[]{:S(2)}) %all-to-all-start) | async-done | bytes 131104 | tf_op jit(solution)/shard_map/all_to_all | solution.py:134
  101.8 0.1 reshape.187
  101.9 0.7 copy.64
  102.5 0.0 collective-permute-done.far_re.rest_0_
  102.6 0.0 copy-start.1
  102.6 0.0 collective-permute-done.1.far_im.rest_1_
  102.6 0.0 collective-permute-done.2.rest_0_.far_re
  102.6 0.0 collective-permute-done.3.rest_1_.far_im
  102.6 1.3 copy-done.1
  103.9 9.5 %shard_map.68 = bf16[8,16,2,32,128]{4,3,2,1,0:T(8,128)(2,1)} custom-call(s32[4]{0:T(128)} %get-tuple-element.17.slot_ref, bf16[4,1,512,512]{3,2,1,0:T(8,128)(2,1)} %own_re.5, bf16[4,1,512,512]{3,2,1,0:T(8,128)(2,1)} %own_im.5, bf16[4,1,512,512]{3,2,1,0:T(8,128)(2,1)} %copy-done.1, bf16[4,1,512,512]{3,2,1,0:T(8,128)(2,1)} %collective-permute-done.1.far_im.rest_1_, ...), custom_call_target="tpu_custom_call" | custom-call | flops 4294967296 | bytes 9437184 | tf_op jit(solution)/shard_map/pallas_call | solution.py:83
  113.4 7.4 %all-to-all-start.1 = ((bf16[128,2,32,128]{3,2,1,0:T(8,128)(2,1)}), bf16[128,2,32,128]{3,2,1,0:T(8,128)(2,1)S(1)}, u32[]{:S(2)}, u32[]{:S(2)}) async-start(bf16[128,2,32,128]{3,2,1,0:T(8,128)(2,1)} %bitcast.62), calls=%async_computation.1 | async-start | bytes 4194304 | tf_op jit(solution)/shard_map/all_to_all | solution.py:166
  120.8 14.8 %shard_map.69.rest_2_ = bf16[8,16,6,32,128]{4,3,2,1,0:T(8,128)(2,1)} custom-call(s32[4]{0:T(128)} %get-tuple-element.16.slot_ref, bf16[4,1,512,512]{3,2,1,0:T(8,128)(2,1)} %own_re.5, bf16[4,1,512,512]{3,2,1,0:T(8,128)(2,1)} %own_im.5, bf16[4,1,512,512]{3,2,1,0:T(8,128)(2,1)} %collective-permute-done.2.rest_0_.far_re, ...), custom_call_target="tpu_custom_call" | custom-call | flops 8589934592 | bytes 15728640 | tf_op jit(solution)/shard_map/pallas_call | solution.py:83
  135.6 9.5 %shard_map.70 = bf16[8,16,6,32,128]{4,3,2,1,0:T(8,128)(2,1)} custom-call(s32[4]{0:T(128)} %get-tuple-element.17.slot_ref, bf16[4,1,512,512]{3,2,1,0:T(8,128)(2,1)} %own_re.5, bf16[4,1,512,512]{3,2,1,0:T(8,128)(2,1)} %own_im.5, bf16[4,1,512,512]{3,2,1,0:T(8,128)(2,1)} %copy-done.1, ...), custom_call_target="tpu_custom_call", output_to_operand_aliasing={{}: (10, {})} | custom-call | flops 4294967296 | bytes 9437184 | tf_op jit(solution)/shard_map/pallas_call | solution.py:83
  145.1 4.0 %all-to-all-done.1 = bf16[128,2,32,128]{3,2,1,0:T(8,128)(2,1)S(1)} async-done(((bf16[128,2,32,128]{3,2,1,0:T(8,128)(2,1)}), bf16[128,2,32,128]{3,2,1,0:T(8,128)(2,1)S(1)}, u32[]{:S(2)}, u32[]{:S(2)}) %all-to-all-start.1) | async-done | bytes 2097184 | tf_op jit(solution)/shard_map/all_to_all | solution.py:166
  149.1 0.0 copy-start.2
  149.1 0.0 copy-start.3
  149.1 7.9 %all-to-all-start.2 = ((bf16[128,6,32,128]{3,2,1,0:T(8,128)(2,1)}), bf16[128,6,32,128]{3,2,1,0:T(8,128)(2,1)}, u32[]{:S(2)}, u32[]{:S(2)}) async-start(bf16[128,6,32,128]{3,2,1,0:T(8,128)(2,1)} %bitcast.61), calls=%async_computation.2 | async-start | bytes 12582912 | tf_op jit(solution)/shard_map/all_to_all | solution.py:166
  157.0 0.0 copy-done.2
  157.1 0.0 copy-done.3
  157.3 0.1 maximum_bitcast_fusion.2
  157.4 0.1 copy_bitcast_fusion
  157.5 6.5 %convolution_bitcast_fusion = f32[32,128,512]{2,1,0:T(8,128)} fusion(bf16[128,2,32,128]{3,2,1,0:T(8,128)(2,1)S(1)} %all-to-all-done.1, bf16[128,2,256]{2,0,1:T(8,128)(2,1)S(1)} %get-tuple-element.22, bf16[128,2,256]{2,0,1:T(8,128)(2,1)S(1)} %get-tuple-element.23), kind=kOutput, calls=%fused_computation.3 | convolution fusion | flops 1074266112 | bytes 10747904 | tf_op jit(solution)/shard_map/swrn,swx->rnx/dot_general | solution.py:173
  163.9 65.7 %all-to-all-done.2 = bf16[128,6,32,128]{3,2,1,0:T(8,128)(2,1)} async-done(((bf16[128,6,32,128]{3,2,1,0:T(8,128)(2,1)}), bf16[128,6,32,128]{3,2,1,0:T(8,128)(2,1)}, u32[]{:S(2)}, u32[]{:S(2)}) %all-to-all-start.2) | async-done | bytes 6291488 | tf_op jit(solution)/shard_map/all_to_all | solution.py:166
  229.6 0.0 copy-start
  229.6 7.4 %fusion.2 = f32[32,128,512]{2,1,0:T(8,128)S(1)} fusion(bf16[128,6,32,128]{3,2,1,0:T(8,128)(2,1)} %all-to-all-done.2, bf16[128,6,256]{2,0,1:T(8,128)(2,1)S(1)} %get-tuple-element.20, bf16[128,6,256]{2,0,1:T(8,128)(2,1)S(1)} %get-tuple-element.21), kind=kOutput, calls=%fused_computation.2 | convolution fusion | flops 3222798336 | bytes 15466496 | tf_op jit(solution)/shard_map/swrn,swx->rnx/dot_general | solution.py:173
  237.0 0.0 copy-done
  237.1 0.6 fusion.5
  237.7 1.6 fusion.26
  (9 shorter events, 0.2 us)
Async XLA Ops:
  0.6 101.9 %collective-permute-start = (bf16[4,1,512,512]{3,2,1,0:T(8,128)(2,1)}, bf16[4,1,512,512]{3,2,1,0:T(8,128)(2,1)S(1)}, u32[]{:S(2)}, u32[]{:S(2)}) collective-permute-start(bf16[4,1,512,512]{3,2,1,0:T(8,128)(2,1)} %own_re.5), channel_id=1, source_target_pairs={{0,32},{32,0},{16,48},{48,16},{64,96},{96,64},{80,112},{112,80},{1... | collective-permute-start | bytes 6291464 | tf_op jit(solution)/shard_map/ppermute | solution.py:20
  2.6 99.9 %collective-permute-start.1 = (bf16[4,1,512,512]{3,2,1,0:T(8,128)(2,1)}, bf16[4,1,512,512]{3,2,1,0:T(8,128)(2,1)}, u32[]{:S(2)}, u32[]{:S(2)}) collective-permute-start(bf16[4,1,512,512]{3,2,1,0:T(8,128)(2,1)} %own_im.5), channel_id=1, source_target_pairs={{0,32},{32,0},{16,48},{48,16},{64,96},{96,64},{80,112},{112,80},{1... | collective-permute-start | bytes 6291464 | tf_op jit(solution)/shard_map/ppermute | solution.py:20
  2.7 99.8 %collective-permute-start.2 = (bf16[4,1,512,512]{3,2,1,0:T(8,128)(2,1)}, bf16[4,1,512,512]{3,2,1,0:T(8,128)(2,1)}, u32[]{:S(2)}, u32[]{:S(2)}) collective-permute-start(bf16[4,1,512,512]{3,2,1,0:T(8,128)(2,1)} %own_re.5), channel_id=1, source_target_pairs={{0,16},{16,0},{32,48},{48,32},{64,80},{80,64},{96,112},{112,96},{1... | collective-permute-start | bytes 6291464 | tf_op jit(solution)/shard_map/ppermute | solution.py:20
  5.8 96.8 %collective-permute-start.3 = (bf16[4,1,512,512]{3,2,1,0:T(8,128)(2,1)}, bf16[4,1,512,512]{3,2,1,0:T(8,128)(2,1)}, u32[]{:S(2)}, u32[]{:S(2)}) collective-permute-start(bf16[4,1,512,512]{3,2,1,0:T(8,128)(2,1)} %own_im.5), channel_id=1, source_target_pairs={{0,16},{16,0},{32,48},{48,32},{64,80},{80,64},{96,112},{112,96},{1... | collective-permute-start | bytes 6291464 | tf_op jit(solution)/shard_map/ppermute | solution.py:20
  9.1 92.7 %all-to-all-start = ((bf16[128,2,256]{2,1,0:T(2,128)(2,1)}), bf16[128,2,256]{2,1,0:T(2,128)(2,1)S(1)}, u32[]{:S(2)}, u32[]{:S(2)}) async-start(bf16[128,2,256]{2,1,0:T(2,128)(2,1)} %reshape.186), calls=%async_computation | async-start | bytes 262144 | tf_op jit(solution)/shard_map/all_to_all | solution.py:134
  33.3 3.1 %copy-start.4 = (s32[2,4]{1,0:T(2,128)S(1)}, s32[2,4]{1,0:T(2,128)}, u32[]{:S(2)}) copy-start(s32[2,4]{1,0:T(2,128)} %param.7) | copy-start | bytes 100
  102.6 1.3 copy-start.1
  113.4 35.7 %all-to-all-start.1 = ((bf16[128,2,32,128]{3,2,1,0:T(8,128)(2,1)}), bf16[128,2,32,128]{3,2,1,0:T(8,128)(2,1)S(1)}, u32[]{:S(2)}, u32[]{:S(2)}) async-start(bf16[128,2,32,128]{3,2,1,0:T(8,128)(2,1)} %bitcast.62), calls=%async_computation.1 | async-start | bytes 4194304 | tf_op jit(solution)/shard_map/all_to_all | solution.py:166
  149.1 7.9 %copy-start.2 = (bf16[32,2,16,128]{3,2,1,0:T(8,128)(2,1)S(1)}, bf16[32,2,16,128]{3,2,1,0:T(8,128)(2,1)}, u32[]{:S(2)}) copy-start(bf16[32,2,16,128]{3,2,1,0:T(8,128)(2,1)} %param.9) | copy-start | bytes 786436
  149.1 7.9 %copy-start.3 = (bf16[32,2,16,128]{3,2,1,0:T(8,128)(2,1)S(1)}, bf16[32,2,16,128]{3,2,1,0:T(8,128)(2,1)}, u32[]{:S(2)}) copy-start(bf16[32,2,16,128]{3,2,1,0:T(8,128)(2,1)} %param.8) | copy-start | bytes 786436
  149.1 80.5 %all-to-all-start.2 = ((bf16[128,6,32,128]{3,2,1,0:T(8,128)(2,1)}), bf16[128,6,32,128]{3,2,1,0:T(8,128)(2,1)}, u32[]{:S(2)}, u32[]{:S(2)}) async-start(bf16[128,6,32,128]{3,2,1,0:T(8,128)(2,1)} %bitcast.61), calls=%async_computation.2 | async-start | bytes 12582912 | tf_op jit(solution)/shard_map/all_to_all | solution.py:166
  229.6 7.4 %copy-start = (f32[32,128,512]{2,1,0:T(8,128)S(1)}, f32[32,128,512]{2,1,0:T(8,128)}, u32[]{:S(2)}) copy-start(f32[32,128,512]{2,1,0:T(8,128)} %convolution_bitcast_fusion) | copy-start | bytes 25165828

commit v12 on v11

--- a/solution.py
+++ b/solution.py
@@ -134,7 +134,7 @@
     warm = lax.all_to_all(
         hologram_real[0, 0, :devices, :], ("wave", "angle"), 0, 0, tiled=True
     )
-    warmed = [warm]
+    warmed = []
     volume = None
     for low, high in split:
         shape = (wave_devices, angle_devices, high - low, rows_per, lanes)
@@ -164,6 +164,7 @@
             )
         send = send.reshape(wave_devices * angle_devices, *send.shape[2:])
         got = lax.all_to_all(send, ("wave", "angle"), 0, 0, tiled=True)
+        warmed = [warm] if low == split[0][0] else []
         got = with_layout_constraint(got, Layout(tuple(range(got.ndim))))
         kr = k_re[:, low:high]
         ki = k_im[:, low:high]

time: 244 us -> 240 us (0.984)
  waiting for transfers between devices: 129 us -> 124 us
  starting transfers between devices: 31.2 us -> 33.8 us
    all_to_all x1, waiting for transfers between devices: 59.5 us -> 0.01 us  [shards(): lax.all_to_all(hologram_real[0, 0, :devices, :], ('wave', 'angle'), 0, 0,...]
    ppermute x4, waiting for transfers between devices: 0.01 us -> 55.1 us  [from_partner(): return lax.ppermute(block, axis, route)]
    all_to_all x2, starting transfers between devices: 15.3 us -> 17.9 us  [shards(): got = lax.all_to_all(send, ('wave', 'angle'), 0, 0, tiled=True)]
  transfers between devices with their start and end apart: 7 -> 7, of which waited for: 3 -> 5; matrix products, arithmetic and copies ran while one was open for 14% -> 14% of each run, Pallas kernels for 10% -> 14%
where the time goes in v12:
time: 240 us; the launch traced here: 235 us
  waiting for transfers between devices  124 us (52%)
  Pallas kernels  33.9 us (14%)
  starting transfers between devices  33.8 us (14%)
  other arithmetic  20.2 us (8%)
  matrix products  13.9 us (6%)
  local copies, waits for them, and re-layouts  8.85 us (4%)
    all_to_all x2, waiting for transfers between devices, shards(): got = lax.all_to_all(send, ('wave', 'angle'), 0, 0, tiled=True)  69 us
    ppermute x4, waiting for transfers between devices, from_partner(): return lax.ppermute(block, axis, route)  55.1 us
    pallas_call x3, Pallas kernels, spectra(): pl.pallas_call(spectrum_kernel, out_shape=jax.ShapeDtypeStruct(shape, jnp...  33.9 us
    all_to_all x2, starting transfers between devices, shards(): got = lax.all_to_all(send, ('wave', 'angle'), 0, 0, tiled=True)  17.9 us
    dot_general x2, matrix products, shards(): t = jnp.einsum('swrn,swx->rnx', got, both, preferred_element_type=fp)  13.9 us
    convert_element_type x2, other arithmetic, dft_tables(): (-jnp.sin(phase) * factor).astype(jnp.bfloat16)  10.3 us
    all_to_all x1, starting transfers between devices, shards(): lax.all_to_all(hologram_real[0, 0, :devices, :], ('wave', 'angle'), 0, 0,...  10.3 us
    ppermute x4, starting transfers between devices, from_partner(): return lax.ppermute(block, axis, route)  5.64 us
  transfers between devices with their start and end apart: 7, of which 5 were waited for; matrix products, arithmetic and copies ran while one was open for 14% of the time, Pallas kernels for 14%

profile of v12, /device:TPU:24, one launch (start us, length us, event | category | flops | bytes accessed | tf_op | source)
XLA Modules:
  0.0 235.4 jit_solution(3565232106255969386)
XLA Ops:
  0.6 2.0 collective-permute-start
  2.6 0.1 collective-permute-start.1
  2.7 3.0 %collective-permute-start.2 = (bf16[4,1,512,512]{3,2,1,0:T(8,128)(2,1)}, bf16[4,1,512,512]{3,2,1,0:T(8,128)(2,1)}, u32[]{:S(2)}, u32[]{:S(2)}) collective-permute-start(bf16[4,1,512,512]{3,2,1,0:T(8,128)(2,1)} %own_re.5), channel_id=1, source_target_pairs={{0,16},{16,0},{32,48},{48,32},{64,80},{80,64},{96,112},{112,96},{1... | collective-permute-start | bytes 6291464 | tf_op jit(solution)/shard_map/ppermute | solution.py:20
  5.8 0.5 collective-permute-start.3
  6.3 0.9 slice_bitcast_fusion.2
  7.2 0.5 broadcast.227
  7.7 0.7 reduce
  8.4 0.7 reshape.186
  9.1 10.3 %all-to-all-start.1 = ((bf16[128,2,256]{2,1,0:T(2,128)(2,1)}), bf16[128,2,256]{2,1,0:T(2,128)(2,1)S(1)}, u32[]{:S(2)}, u32[]{:S(2)}) async-start(bf16[128,2,256]{2,1,0:T(2,128)(2,1)} %reshape.186), calls=%async_computation.1 | async-start | bytes 262144 | tf_op jit(solution)/shard_map/all_to_all | solution.py:134
  19.3 4.3 %fusion.23 = bf16[512,8,1,64]{0,3,2,1:T(8,128)(2,1)S(1)} fusion(s32[8,64]{1,0:T(8,128)S(1)} %multiply_add_fusion), kind=kLoop, calls=%fused_computation.46 | loop fusion | flops 5242880 | bytes 526336 | tf_op jit(solution)/shard_map/neg | solution.py:44
  23.6 4.9 %multiply_convert_fusion.2 = (bf16[512,8,1,64]{0,3,2,1:T(8,128)(2,1)S(1)}, bf16[512,8,1,64]{0,3,2,1:T(8,128)(2,1)S(1)}) fusion(s32[8,64]{1,0:T(8,128)S(1)} %multiply_add_fusion), kind=kLoop, calls=%fused_computation.27 | loop fusion | flops 4980736 | bytes 1050624 | tf_op jit(solution)/shard_map/convert_element_type | solution.py:30
  28.6 1.1 pad_maximum_fusion.1
  29.7 2.3 copy.35
  32.0 1.3 copy.36
  33.3 5.3 %multiply_convert_fusion = (bf16[512,512]{1,0:T(8,128)(2,1)}, bf16[512,512]{1,0:T(8,128)(2,1)}) fusion(), kind=kLoop, calls=%fused_computation.23 | loop fusion | flops 4980736 | bytes 1048576 | tf_op jit(solution)/shard_map/convert_element_type | solution.py:30
  38.6 0.0 copy-start.4
  38.6 3.0 %pad_maximum_fusion.col_a = bf16[1024,1024]{1,0:T(8,128)(2,1)} fusion(bf16[512,1024]{1,0:T(8,128)(2,1)} %copy.36, bf16[512,1024]{1,0:T(8,128)(2,1)} %copy.35), kind=kLoop, calls=%fused_computation.7 | loop fusion | flops 4194304 | bytes 4194304 | tf_op jit(solution)/shard_map/concatenate | solution.py:42
  41.7 0.0 copy-done.4
  41.7 0.6 slice_bitcast_fusion.5
  42.3 7.5 %collective-permute-done.far_re.rest_0_ = bf16[4,1,512,512]{3,2,1,0:T(8,128)(2,1)S(1)} collective-permute-done((bf16[4,1,512,512]{3,2,1,0:T(8,128)(2,1)}, bf16[4,1,512,512]{3,2,1,0:T(8,128)(2,1)S(1)}, u32[]{:S(2)}, u32[]{:S(2)}) %collective-permute-start) | collective-permute-done | bytes 2097184 | tf_op jit(solution)/shard_map/ppermute | solution.py:20
  49.7 0.0 copy-start.1
  49.7 44.1 %collective-permute-done.1.far_im.rest_1_ = bf16[4,1,512,512]{3,2,1,0:T(8,128)(2,1)} collective-permute-done((bf16[4,1,512,512]{3,2,1,0:T(8,128)(2,1)}, bf16[4,1,512,512]{3,2,1,0:T(8,128)(2,1)}, u32[]{:S(2)}, u32[]{:S(2)}) %collective-permute-start.1) | collective-permute-done | bytes 2097184 | tf_op jit(solution)/shard_map/ppermute | solution.py:20
  93.9 0.0 collective-permute-done.2.rest_0_.far_re
  93.9 3.4 %collective-permute-done.3.rest_1_.far_im = bf16[4,1,512,512]{3,2,1,0:T(8,128)(2,1)} collective-permute-done((bf16[4,1,512,512]{3,2,1,0:T(8,128)(2,1)}, bf16[4,1,512,512]{3,2,1,0:T(8,128)(2,1)}, u32[]{:S(2)}, u32[]{:S(2)}) %collective-permute-start.3) | collective-permute-done | bytes 2097184 | tf_op jit(solution)/shard_map/ppermute | solution.py:20
  97.3 0.0 copy-done.1
  97.3 9.6 %shard_map.68 = bf16[8,16,2,32,128]{4,3,2,1,0:T(8,128)(2,1)} custom-call(s32[4]{0:T(128)} %get-tuple-element.17.slot_ref, bf16[4,1,512,512]{3,2,1,0:T(8,128)(2,1)} %own_re.5, bf16[4,1,512,512]{3,2,1,0:T(8,128)(2,1)} %own_im.5, bf16[4,1,512,512]{3,2,1,0:T(8,128)(2,1)} %copy-done.1, bf16[4,1,512,512]{3,2,1,0:T(8,128)(2,1)} %collective-permute-done.1.far_im.rest_1_, ...), custom_call_target="tpu_custom_call" | custom-call | flops 4294967296 | bytes 9437184 | tf_op jit(solution)/shard_map/pallas_call | solution.py:83
  106.9 0.0 all-to-all-done.1
  106.9 10.0 %all-to-all-start = ((bf16[128,2,32,128]{3,2,1,0:T(8,128)(2,1)}), bf16[128,2,32,128]{3,2,1,0:T(8,128)(2,1)S(1)}, u32[]{:S(2)}, u32[]{:S(2)}) async-start(bf16[128,2,32,128]{3,2,1,0:T(8,128)(2,1)} %bitcast.62), calls=%async_computation | async-start | bytes 4194304 | tf_op jit(solution)/shard_map/all_to_all | solution.py:166
  116.9 0.1 reshape.187
  117.0 0.7 copy.64
  117.7 14.8 %shard_map.69.rest_2_ = bf16[8,16,6,32,128]{4,3,2,1,0:T(8,128)(2,1)} custom-call(s32[4]{0:T(128)} %get-tuple-element.16.slot_ref, bf16[4,1,512,512]{3,2,1,0:T(8,128)(2,1)} %own_re.5, bf16[4,1,512,512]{3,2,1,0:T(8,128)(2,1)} %own_im.5, bf16[4,1,512,512]{3,2,1,0:T(8,128)(2,1)} %collective-permute-done.2.rest_0_.far_re, ...), custom_call_target="tpu_custom_call" | custom-call | flops 8589934592 | bytes 15728640 | tf_op jit(solution)/shard_map/pallas_call | solution.py:83
  132.5 9.5 %shard_map.70 = bf16[8,16,6,32,128]{4,3,2,1,0:T(8,128)(2,1)} custom-call(s32[4]{0:T(128)} %get-tuple-element.17.slot_ref, bf16[4,1,512,512]{3,2,1,0:T(8,128)(2,1)} %own_re.5, bf16[4,1,512,512]{3,2,1,0:T(8,128)(2,1)} %own_im.5, bf16[4,1,512,512]{3,2,1,0:T(8,128)(2,1)} %copy-done.1, ...), custom_call_target="tpu_custom_call", output_to_operand_aliasing={{}: (10, {})} | custom-call | flops 4294967296 | bytes 9437184 | tf_op jit(solution)/shard_map/pallas_call | solution.py:83
  142.0 3.3 %all-to-all-done = bf16[128,2,32,128]{3,2,1,0:T(8,128)(2,1)S(1)} async-done(((bf16[128,2,32,128]{3,2,1,0:T(8,128)(2,1)}), bf16[128,2,32,128]{3,2,1,0:T(8,128)(2,1)S(1)}, u32[]{:S(2)}, u32[]{:S(2)}) %all-to-all-start) | async-done | bytes 2097184 | tf_op jit(solution)/shard_map/all_to_all | solution.py:166
  145.3 0.0 copy-start.2
  145.3 0.0 copy-start.3
  145.3 7.9 %all-to-all-start.2 = ((bf16[128,6,32,128]{3,2,1,0:T(8,128)(2,1)}), bf16[128,6,32,128]{3,2,1,0:T(8,128)(2,1)}, u32[]{:S(2)}, u32[]{:S(2)}) async-start(bf16[128,6,32,128]{3,2,1,0:T(8,128)(2,1)} %bitcast.61), calls=%async_computation.2 | async-start | bytes 12582912 | tf_op jit(solution)/shard_map/all_to_all | solution.py:166
  153.2 0.0 copy-done.2
  153.2 0.0 copy-done.3
  153.4 0.1 maximum_bitcast_fusion.2
  153.5 0.1 copy_bitcast_fusion
  153.6 6.5 %convolution_bitcast_fusion = f32[32,128,512]{2,1,0:T(8,128)} fusion(bf16[128,2,32,128]{3,2,1,0:T(8,128)(2,1)S(1)} %all-to-all-done, bf16[128,2,256]{2,0,1:T(8,128)(2,1)S(1)} %get-tuple-element.22, bf16[128,2,256]{2,0,1:T(8,128)(2,1)S(1)} %get-tuple-element.23), kind=kOutput, calls=%fused_computation.3 | convolution fusion | flops 1074266112 | bytes 10747904 | tf_op jit(solution)/shard_map/swrn,swx->rnx/dot_general | solution.py:174
  160.1 65.7 %all-to-all-done.2 = bf16[128,6,32,128]{3,2,1,0:T(8,128)(2,1)} async-done(((bf16[128,6,32,128]{3,2,1,0:T(8,128)(2,1)}), bf16[128,6,32,128]{3,2,1,0:T(8,128)(2,1)}, u32[]{:S(2)}, u32[]{:S(2)}) %all-to-all-start.2) | async-done | bytes 6291488 | tf_op jit(solution)/shard_map/all_to_all | solution.py:166
  225.8 0.0 copy-start
  225.8 7.4 %fusion.2 = f32[32,128,512]{2,1,0:T(8,128)S(1)} fusion(bf16[128,6,32,128]{3,2,1,0:T(8,128)(2,1)} %all-to-all-done.2, bf16[128,6,256]{2,0,1:T(8,128)(2,1)S(1)} %get-tuple-element.20, bf16[128,6,256]{2,0,1:T(8,128)(2,1)S(1)} %get-tuple-element.21), kind=kOutput, calls=%fused_computation.2 | convolution fusion | flops 3222798336 | bytes 15466496 | tf_op jit(solution)/shard_map/swrn,swx->rnx/dot_general | solution.py:174
  233.2 0.0 copy-done
  233.2 0.6 fusion.5
  233.8 1.6 fusion.26
  (9 shorter events, 0.2 us)
Async XLA Ops:
  0.6 49.1 %collective-permute-start = (bf16[4,1,512,512]{3,2,1,0:T(8,128)(2,1)}, bf16[4,1,512,512]{3,2,1,0:T(8,128)(2,1)S(1)}, u32[]{:S(2)}, u32[]{:S(2)}) collective-permute-start(bf16[4,1,512,512]{3,2,1,0:T(8,128)(2,1)} %own_re.5), channel_id=1, source_target_pairs={{0,32},{32,0},{16,48},{48,16},{64,96},{96,64},{80,112},{112,80},{1... | collective-permute-start | bytes 6291464 | tf_op jit(solution)/shard_map/ppermute | solution.py:20
  2.6 91.2 %collective-permute-start.1 = (bf16[4,1,512,512]{3,2,1,0:T(8,128)(2,1)}, bf16[4,1,512,512]{3,2,1,0:T(8,128)(2,1)}, u32[]{:S(2)}, u32[]{:S(2)}) collective-permute-start(bf16[4,1,512,512]{3,2,1,0:T(8,128)(2,1)} %own_im.5), channel_id=1, source_target_pairs={{0,32},{32,0},{16,48},{48,16},{64,96},{96,64},{80,112},{112,80},{1... | collective-permute-start | bytes 6291464 | tf_op jit(solution)/shard_map/ppermute | solution.py:20
  2.7 91.1 %collective-permute-start.2 = (bf16[4,1,512,512]{3,2,1,0:T(8,128)(2,1)}, bf16[4,1,512,512]{3,2,1,0:T(8,128)(2,1)}, u32[]{:S(2)}, u32[]{:S(2)}) collective-permute-start(bf16[4,1,512,512]{3,2,1,0:T(8,128)(2,1)} %own_re.5), channel_id=1, source_target_pairs={{0,16},{16,0},{32,48},{48,32},{64,80},{80,64},{96,112},{112,96},{1... | collective-permute-start | bytes 6291464 | tf_op jit(solution)/shard_map/ppermute | solution.py:20
  5.8 91.6 %collective-permute-start.3 = (bf16[4,1,512,512]{3,2,1,0:T(8,128)(2,1)}, bf16[4,1,512,512]{3,2,1,0:T(8,128)(2,1)}, u32[]{:S(2)}, u32[]{:S(2)}) collective-permute-start(bf16[4,1,512,512]{3,2,1,0:T(8,128)(2,1)} %own_im.5), channel_id=1, source_target_pairs={{0,16},{16,0},{32,48},{48,32},{64,80},{80,64},{96,112},{112,96},{1... | collective-permute-start | bytes 6291464 | tf_op jit(solution)/shard_map/ppermute | solution.py:20
  9.1 97.9 %all-to-all-start.1 = ((bf16[128,2,256]{2,1,0:T(2,128)(2,1)}), bf16[128,2,256]{2,1,0:T(2,128)(2,1)S(1)}, u32[]{:S(2)}, u32[]{:S(2)}) async-start(bf16[128,2,256]{2,1,0:T(2,128)(2,1)} %reshape.186), calls=%async_computation.1 | async-start | bytes 262144 | tf_op jit(solution)/shard_map/all_to_all | solution.py:134
  38.6 3.1 %copy-start.4 = (s32[2,4]{1,0:T(2,128)S(1)}, s32[2,4]{1,0:T(2,128)}, u32[]{:S(2)}) copy-start(s32[2,4]{1,0:T(2,128)} %param.7) | copy-start | bytes 100
  49.7 47.6 %copy-start.1 = (bf16[4,1,512,512]{3,2,1,0:T(8,128)(2,1)}, bf16[4,1,512,512]{3,2,1,0:T(8,128)(2,1)S(1)}, u32[]{:S(2)}) copy-start(bf16[4,1,512,512]{3,2,1,0:T(8,128)(2,1)S(1)} %collective-permute-done.far_re.rest_0_) | copy-start | bytes 6291460
  106.9 38.4 %all-to-all-start = ((bf16[128,2,32,128]{3,2,1,0:T(8,128)(2,1)}), bf16[128,2,32,128]{3,2,1,0:T(8,128)(2,1)S(1)}, u32[]{:S(2)}, u32[]{:S(2)}) async-start(bf16[128,2,32,128]{3,2,1,0:T(8,128)(2,1)} %bitcast.62), calls=%async_computation | async-start | bytes 4194304 | tf_op jit(solution)/shard_map/all_to_all | solution.py:166
  145.3 7.9 %copy-start.2 = (bf16[32,2,16,128]{3,2,1,0:T(8,128)(2,1)S(1)}, bf16[32,2,16,128]{3,2,1,0:T(8,128)(2,1)}, u32[]{:S(2)}) copy-start(bf16[32,2,16,128]{3,2,1,0:T(8,128)(2,1)} %param.9) | copy-start | bytes 786436
  145.3 7.9 %copy-start.3 = (bf16[32,2,16,128]{3,2,1,0:T(8,128)(2,1)S(1)}, bf16[32,2,16,128]{3,2,1,0:T(8,128)(2,1)}, u32[]{:S(2)}) copy-start(bf16[32,2,16,128]{3,2,1,0:T(8,128)(2,1)} %param.8) | copy-start | bytes 786436
  145.3 80.5 %all-to-all-start.2 = ((bf16[128,6,32,128]{3,2,1,0:T(8,128)(2,1)}), bf16[128,6,32,128]{3,2,1,0:T(8,128)(2,1)}, u32[]{:S(2)}, u32[]{:S(2)}) async-start(bf16[128,6,32,128]{3,2,1,0:T(8,128)(2,1)} %bitcast.61), calls=%async_computation.2 | async-start | bytes 12582912 | tf_op jit(solution)/shard_map/all_to_all | solution.py:166
  225.8 7.4 %copy-start = (f32[32,128,512]{2,1,0:T(8,128)S(1)}, f32[32,128,512]{2,1,0:T(8,128)}, u32[]{:S(2)}) copy-start(f32[32,128,512]{2,1,0:T(8,128)} %convolution_bitcast_fusion) | copy-start | bytes 25165828

commit v13 on v10

--- a/solution.py
+++ b/solution.py
@@ -76,8 +76,8 @@
     blocks, groups, _, rows_per, lanes = shape
     field = pl.BlockSpec((1, 1, rows, cols), lambda i, sl: (first + i, 0, 0, 0))
     partner = pl.BlockSpec((1, 1, rows, cols), lambda i, sl: (sl[first + i], 0, 0, 0))
-    whole_col = pl.BlockSpec((2 * cols, 2 * cols), lambda i, sl: (0, 0))
-    whole_row = pl.BlockSpec((rows, rows), lambda i, sl: (0, 0))
+    whole_col = pl.BlockSpec(memory_space=pltpu.VMEM)
+    whole_row = pl.BlockSpec(memory_space=pltpu.VMEM)
     flops = waves * (2 * rows * (2 * cols) * (2 * cols) + 2 * 2 * rows * rows * (2 * cols))
     extra = list(after) + ([] if into is None else [into])
     return pl.pallas_call(

time: 239 us -> 239 us (level)
  no operation moved by 1% of the time
where the time goes in v13:
time: 239 us; the launch traced here: 235 us
  waiting for transfers between devices  137 us (57%)
  Pallas kernels  33.9 us (14%)
  starting transfers between devices  23.5 us (10%)
  other arithmetic  19.5 us (8%)
  matrix products  13.8 us (6%)
  local copies, waits for them, and re-layouts  5.9 us (2%)
    all_to_all x2, waiting for transfers between devices, shards(): got = lax.all_to_all(send, ('wave', 'angle'), 0, 0, tiled=True)  69.8 us
    ppermute x4, waiting for transfers between devices, from_partner(): return lax.ppermute(block, axis, route)  67.4 us
    pallas_call x3, Pallas kernels, spectra(): pl.pallas_call(spectrum_kernel, out_shape=jax.ShapeDtypeStruct(shape, jnp...  33.9 us
    all_to_all x2, starting transfers between devices, shards(): got = lax.all_to_all(send, ('wave', 'angle'), 0, 0, tiled=True)  17.9 us
    dot_general x2, matrix products, shards(): t = jnp.einsum('swrn,swx->rnx', got, both, preferred_element_type=fp)  13.8 us
    convert_element_type x2, other arithmetic, dft_tables(): (-jnp.sin(phase) * factor).astype(jnp.bfloat16)  10.3 us
    ppermute x4, starting transfers between devices, from_partner(): return lax.ppermute(block, axis, route)  5.64 us
  transfers between devices with their start and end apart: 6, of which 5 were waited for; matrix products, arithmetic and copies ran while one was open for 13% of the time, Pallas kernels for 10%

profile of v13, /device:TPU:24, one launch (start us, length us, event | category | flops | bytes accessed | tf_op | source)
XLA Modules:
  0.0 234.7 jit_solution(17725264717347357534)
XLA Ops:
  0.6 2.0 collective-permute-start
  2.6 0.1 collective-permute-start.1
  2.7 3.0 %collective-permute-start.2 = (bf16[4,1,512,512]{3,2,1,0:T(8,128)(2,1)}, bf16[4,1,512,512]{3,2,1,0:T(8,128)(2,1)}, u32[]{:S(2)}, u32[]{:S(2)}) collective-permute-start(bf16[4,1,512,512]{3,2,1,0:T(8,128)(2,1)} %own_re.5), channel_id=1, source_target_pairs={{0,16},{16,0},{32,48},{48,32},{64,80},{80,64},{96,112},{112,96},{1... | collective-permute-start | bytes 6291464 | tf_op jit(solution)/shard_map/ppermute | solution.py:20
  5.8 0.5 collective-permute-start.3
  6.3 4.3 %fusion.23 = bf16[512,8,1,64]{0,3,2,1:T(8,128)(2,1)S(1)} fusion(s32[8,64]{1,0:T(8,128)S(1)} %multiply_add_fusion), kind=kLoop, calls=%fused_computation.46 | loop fusion | flops 5242880 | bytes 526336 | tf_op jit(solution)/shard_map/neg | solution.py:44
  10.6 4.9 %multiply_convert_fusion.2 = (bf16[512,8,1,64]{0,3,2,1:T(8,128)(2,1)S(1)}, bf16[512,8,1,64]{0,3,2,1:T(8,128)(2,1)S(1)}) fusion(s32[8,64]{1,0:T(8,128)S(1)} %multiply_add_fusion), kind=kLoop, calls=%fused_computation.27 | loop fusion | flops 4980736 | bytes 1050624 | tf_op jit(solution)/shard_map/convert_element_type | solution.py:30
  15.5 1.1 pad_maximum_fusion.1
  16.6 2.3 copy.15
  18.9 1.3 copy.16
  20.2 5.3 %multiply_convert_fusion = (bf16[512,512]{1,0:T(8,128)(2,1)}, bf16[512,512]{1,0:T(8,128)(2,1)}) fusion(), kind=kLoop, calls=%fused_computation.23 | loop fusion | flops 4980736 | bytes 1048576 | tf_op jit(solution)/shard_map/convert_element_type | solution.py:30
  25.5 0.0 copy-start.4
  25.5 3.1 %pad_maximum_fusion.col_a = bf16[1024,1024]{1,0:T(8,128)(2,1)} fusion(bf16[512,1024]{1,0:T(8,128)(2,1)} %copy.16, bf16[512,1024]{1,0:T(8,128)(2,1)} %copy.15), kind=kLoop, calls=%fused_computation.7 | loop fusion | flops 4194304 | bytes 4194304 | tf_op jit(solution)/shard_map/concatenate | solution.py:42
  28.6 0.0 copy-done.4
  28.6 0.5 slice_bitcast_fusion.4
  29.2 20.3 %collective-permute-done.far_re.rest_0_ = bf16[4,1,512,512]{3,2,1,0:T(8,128)(2,1)S(1)} collective-permute-done((bf16[4,1,512,512]{3,2,1,0:T(8,128)(2,1)}, bf16[4,1,512,512]{3,2,1,0:T(8,128)(2,1)S(1)}, u32[]{:S(2)}, u32[]{:S(2)}) %collective-permute-start) | collective-permute-done | bytes 2097184 | tf_op jit(solution)/shard_map/ppermute | solution.py:20
  49.4 0.0 copy-start.1
  49.4 44.1 %collective-permute-done.1.far_im.rest_1_ = bf16[4,1,512,512]{3,2,1,0:T(8,128)(2,1)} collective-permute-done((bf16[4,1,512,512]{3,2,1,0:T(8,128)(2,1)}, bf16[4,1,512,512]{3,2,1,0:T(8,128)(2,1)}, u32[]{:S(2)}, u32[]{:S(2)}) %collective-permute-start.1) | collective-permute-done | bytes 2097184 | tf_op jit(solution)/shard_map/ppermute | solution.py:20
  93.5 0.0 collective-permute-done.2.rest_0_.far_re
  93.5 3.1 %collective-permute-done.3.rest_1_.far_im = bf16[4,1,512,512]{3,2,1,0:T(8,128)(2,1)} collective-permute-done((bf16[4,1,512,512]{3,2,1,0:T(8,128)(2,1)}, bf16[4,1,512,512]{3,2,1,0:T(8,128)(2,1)}, u32[]{:S(2)}, u32[]{:S(2)}) %collective-permute-start.3) | collective-permute-done | bytes 2097184 | tf_op jit(solution)/shard_map/ppermute | solution.py:20
  96.6 0.0 copy-done.1
  96.6 9.6 %shard_map.68 = bf16[8,16,2,32,128]{4,3,2,1,0:T(8,128)(2,1)} custom-call(s32[4]{0:T(128)} %get-tuple-element.17.slot_ref, bf16[4,1,512,512]{3,2,1,0:T(8,128)(2,1)} %own_re.5, bf16[4,1,512,512]{3,2,1,0:T(8,128)(2,1)} %own_im.5, bf16[4,1,512,512]{3,2,1,0:T(8,128)(2,1)} %copy-done.1, bf16[4,1,512,512]{3,2,1,0:T(8,128)(2,1)} %collective-permute-done.1.far_im.rest_1_, ...), custom_call_target="tpu_custom_call" | custom-call | flops 4294967296 | bytes 9437184 | tf_op jit(solution)/shard_map/pallas_call | solution.py:83
  106.2 10.0 %all-to-all-start = ((bf16[128,2,32,128]{3,2,1,0:T(8,128)(2,1)}), bf16[128,2,32,128]{3,2,1,0:T(8,128)(2,1)S(1)}, u32[]{:S(2)}, u32[]{:S(2)}) async-start(bf16[128,2,32,128]{3,2,1,0:T(8,128)(2,1)} %bitcast.57), calls=%async_computation | async-start | bytes 4194304 | tf_op jit(solution)/shard_map/all_to_all | solution.py:159
  116.2 14.8 %shard_map.69.rest_2_ = bf16[8,16,6,32,128]{4,3,2,1,0:T(8,128)(2,1)} custom-call(s32[4]{0:T(128)} %get-tuple-element.16.slot_ref, bf16[4,1,512,512]{3,2,1,0:T(8,128)(2,1)} %own_re.5, bf16[4,1,512,512]{3,2,1,0:T(8,128)(2,1)} %own_im.5, bf16[4,1,512,512]{3,2,1,0:T(8,128)(2,1)} %collective-permute-done.2.rest_0_.far_re, ...), custom_call_target="tpu_custom_call" | custom-call | flops 8589934592 | bytes 15728640 | tf_op jit(solution)/shard_map/pallas_call | solution.py:83
  130.9 9.5 %shard_map.70 = bf16[8,16,6,32,128]{4,3,2,1,0:T(8,128)(2,1)} custom-call(s32[4]{0:T(128)} %get-tuple-element.17.slot_ref, bf16[4,1,512,512]{3,2,1,0:T(8,128)(2,1)} %own_re.5, bf16[4,1,512,512]{3,2,1,0:T(8,128)(2,1)} %own_im.5, bf16[4,1,512,512]{3,2,1,0:T(8,128)(2,1)} %copy-done.1, ...), custom_call_target="tpu_custom_call", output_to_operand_aliasing={{}: (10, {})} | custom-call | flops 4294967296 | bytes 9437184 | tf_op jit(solution)/shard_map/pallas_call | solution.py:83
  140.5 4.0 %all-to-all-done = bf16[128,2,32,128]{3,2,1,0:T(8,128)(2,1)S(1)} async-done(((bf16[128,2,32,128]{3,2,1,0:T(8,128)(2,1)}), bf16[128,2,32,128]{3,2,1,0:T(8,128)(2,1)S(1)}, u32[]{:S(2)}, u32[]{:S(2)}) %all-to-all-start) | async-done | bytes 2097184 | tf_op jit(solution)/shard_map/all_to_all | solution.py:159
  144.5 0.0 copy-start.2
  144.5 0.0 copy-start.3
  144.5 7.9 %all-to-all-start.1 = ((bf16[128,6,32,128]{3,2,1,0:T(8,128)(2,1)}), bf16[128,6,32,128]{3,2,1,0:T(8,128)(2,1)}, u32[]{:S(2)}, u32[]{:S(2)}) async-start(bf16[128,6,32,128]{3,2,1,0:T(8,128)(2,1)} %bitcast.56), calls=%async_computation.1 | async-start | bytes 12582912 | tf_op jit(solution)/shard_map/all_to_all | solution.py:159
  152.4 0.0 copy-done.2
  152.5 0.0 copy-done.3
  152.6 0.1 maximum_bitcast_fusion.2
  152.7 0.1 copy_bitcast_fusion
  152.9 6.5 %convolution_bitcast_fusion = f32[32,128,512]{2,1,0:T(8,128)} fusion(bf16[128,2,32,128]{3,2,1,0:T(8,128)(2,1)S(1)} %all-to-all-done, bf16[128,2,256]{2,0,1:T(8,128)(2,1)S(1)} %get-tuple-element.22, bf16[128,2,256]{2,0,1:T(8,128)(2,1)S(1)} %get-tuple-element.23), kind=kOutput, calls=%fused_computation.3 | convolution fusion | flops 1074266112 | bytes 10747904 | tf_op jit(solution)/shard_map/swrn,swx->rnx/dot_general | solution.py:166
  159.3 65.7 %all-to-all-done.1 = bf16[128,6,32,128]{3,2,1,0:T(8,128)(2,1)} async-done(((bf16[128,6,32,128]{3,2,1,0:T(8,128)(2,1)}), bf16[128,6,32,128]{3,2,1,0:T(8,128)(2,1)}, u32[]{:S(2)}, u32[]{:S(2)}) %all-to-all-start.1) | async-done | bytes 6291488 | tf_op jit(solution)/shard_map/all_to_all | solution.py:159
  225.0 0.0 copy-start
  225.0 7.4 %fusion.2 = f32[32,128,512]{2,1,0:T(8,128)S(1)} fusion(bf16[128,6,32,128]{3,2,1,0:T(8,128)(2,1)} %all-to-all-done.1, bf16[128,6,256]{2,0,1:T(8,128)(2,1)S(1)} %get-tuple-element.20, bf16[128,6,256]{2,0,1:T(8,128)(2,1)S(1)} %get-tuple-element.21), kind=kOutput, calls=%fused_computation.2 | convolution fusion | flops 3222798336 | bytes 15466496 | tf_op jit(solution)/shard_map/swrn,swx->rnx/dot_general | solution.py:166
  232.4 0.0 copy-done
  232.4 0.6 fusion.5
  233.0 1.6 fusion.26
  (9 shorter events, 0.2 us)
Async XLA Ops:
  0.6 48.8 %collective-permute-start = (bf16[4,1,512,512]{3,2,1,0:T(8,128)(2,1)}, bf16[4,1,512,512]{3,2,1,0:T(8,128)(2,1)S(1)}, u32[]{:S(2)}, u32[]{:S(2)}) collective-permute-start(bf16[4,1,512,512]{3,2,1,0:T(8,128)(2,1)} %own_re.5), channel_id=1, source_target_pairs={{0,32},{32,0},{16,48},{48,16},{64,96},{96,64},{80,112},{112,80},{1... | collective-permute-start | bytes 6291464 | tf_op jit(solution)/shard_map/ppermute | solution.py:20
  2.6 90.9 %collective-permute-start.1 = (bf16[4,1,512,512]{3,2,1,0:T(8,128)(2,1)}, bf16[4,1,512,512]{3,2,1,0:T(8,128)(2,1)}, u32[]{:S(2)}, u32[]{:S(2)}) collective-permute-start(bf16[4,1,512,512]{3,2,1,0:T(8,128)(2,1)} %own_im.5), channel_id=1, source_target_pairs={{0,32},{32,0},{16,48},{48,16},{64,96},{96,64},{80,112},{112,80},{1... | collective-permute-start | bytes 6291464 | tf_op jit(solution)/shard_map/ppermute | solution.py:20
  2.7 90.8 %collective-permute-start.2 = (bf16[4,1,512,512]{3,2,1,0:T(8,128)(2,1)}, bf16[4,1,512,512]{3,2,1,0:T(8,128)(2,1)}, u32[]{:S(2)}, u32[]{:S(2)}) collective-permute-start(bf16[4,1,512,512]{3,2,1,0:T(8,128)(2,1)} %own_re.5), channel_id=1, source_target_pairs={{0,16},{16,0},{32,48},{48,32},{64,80},{80,64},{96,112},{112,96},{1... | collective-permute-start | bytes 6291464 | tf_op jit(solution)/shard_map/ppermute | solution.py:20
  5.8 90.8 %collective-permute-start.3 = (bf16[4,1,512,512]{3,2,1,0:T(8,128)(2,1)}, bf16[4,1,512,512]{3,2,1,0:T(8,128)(2,1)}, u32[]{:S(2)}, u32[]{:S(2)}) collective-permute-start(bf16[4,1,512,512]{3,2,1,0:T(8,128)(2,1)} %own_im.5), channel_id=1, source_target_pairs={{0,16},{16,0},{32,48},{48,32},{64,80},{80,64},{96,112},{112,96},{1... | collective-permute-start | bytes 6291464 | tf_op jit(solution)/shard_map/ppermute | solution.py:20
  25.5 3.1 %copy-start.4 = (s32[2,4]{1,0:T(2,128)S(1)}, s32[2,4]{1,0:T(2,128)}, u32[]{:S(2)}) copy-start(s32[2,4]{1,0:T(2,128)} %param.7) | copy-start | bytes 100
  49.4 47.2 %copy-start.1 = (bf16[4,1,512,512]{3,2,1,0:T(8,128)(2,1)}, bf16[4,1,512,512]{3,2,1,0:T(8,128)(2,1)S(1)}, u32[]{:S(2)}) copy-start(bf16[4,1,512,512]{3,2,1,0:T(8,128)(2,1)S(1)} %collective-permute-done.far_re.rest_0_) | copy-start | bytes 6291460
  106.2 38.4 %all-to-all-start = ((bf16[128,2,32,128]{3,2,1,0:T(8,128)(2,1)}), bf16[128,2,32,128]{3,2,1,0:T(8,128)(2,1)S(1)}, u32[]{:S(2)}, u32[]{:S(2)}) async-start(bf16[128,2,32,128]{3,2,1,0:T(8,128)(2,1)} %bitcast.57), calls=%async_computation | async-start | bytes 4194304 | tf_op jit(solution)/shard_map/all_to_all | solution.py:159
  144.5 7.9 %copy-start.2 = (bf16[32,2,16,128]{3,2,1,0:T(8,128)(2,1)S(1)}, bf16[32,2,16,128]{3,2,1,0:T(8,128)(2,1)}, u32[]{:S(2)}) copy-start(bf16[32,2,16,128]{3,2,1,0:T(8,128)(2,1)} %param.9) | copy-start | bytes 786436
  144.5 7.9 %copy-start.3 = (bf16[32,2,16,128]{3,2,1,0:T(8,128)(2,1)S(1)}, bf16[32,2,16,128]{3,2,1,0:T(8,128)(2,1)}, u32[]{:S(2)}) copy-start(bf16[32,2,16,128]{3,2,1,0:T(8,128)(2,1)} %param.8) | copy-start | bytes 786436
  144.5 80.5 %all-to-all-start.1 = ((bf16[128,6,32,128]{3,2,1,0:T(8,128)(2,1)}), bf16[128,6,32,128]{3,2,1,0:T(8,128)(2,1)}, u32[]{:S(2)}, u32[]{:S(2)}) async-start(bf16[128,6,32,128]{3,2,1,0:T(8,128)(2,1)} %bitcast.56), calls=%async_computation.1 | async-start | bytes 12582912 | tf_op jit(solution)/shard_map/all_to_all | solution.py:159
  225.0 7.4 %copy-start = (f32[32,128,512]{2,1,0:T(8,128)S(1)}, f32[32,128,512]{2,1,0:T(8,128)}, u32[]{:S(2)}) copy-start(f32[32,128,512]{2,1,0:T(8,128)} %convolution_bitcast_fusion) | copy-start | bytes 25165828

commit v14 on v10

--- a/solution.py
+++ b/solution.py
@@ -58,8 +58,12 @@
     z_im = (a_im * b_re - a_re * b_im).astype(bf)
     z = jnp.concatenate([z_re, z_im], axis=1)
     y = jnp.dot(z, col_a[...], preferred_element_type=fp).astype(bf)
-    first = jnp.dot(row_re[...], y, preferred_element_type=fp)
-    second = jnp.dot(row_im[...], y, preferred_element_type=fp)
+    both = jnp.dot(
+        jnp.concatenate([row_re[...], row_im[...]], axis=0), y, preferred_element_type=fp
+    )
+    n = row_re.shape[0]
+    first = both[:n]
+    second = both[n:]
     blocks, groups, _, rows_per, lanes = out_ref.shape
     lane = lax.broadcasted_iota(jnp.int32, (first.shape[0], lanes), 1)
     for block in range(blocks):

time: 239 us -> 239 us (level)
  no operation moved by 1% of the time
where the time goes in v14:
time: 239 us; the launch traced here: 235 us
  waiting for transfers between devices  137 us (57%)
  Pallas kernels  33.9 us (14%)
  starting transfers between devices  23.5 us (10%)
  other arithmetic  19.5 us (8%)
  matrix products  13.8 us (6%)
  local copies, waits for them, and re-layouts  5.9 us (2%)
    all_to_all x2, waiting for transfers between devices, shards(): got = lax.all_to_all(send, ('wave', 'angle'), 0, 0, tiled=True)  69.8 us
    ppermute x4, waiting for transfers between devices, from_partner(): return lax.ppermute(block, axis, route)  67.4 us
    pallas_call x3, Pallas kernels, spectra(): pl.pallas_call(spectrum_kernel, out_shape=jax.ShapeDtypeStruct(shape, jnp...  33.9 us
    all_to_all x2, starting transfers between devices, shards(): got = lax.all_to_all(send, ('wave', 'angle'), 0, 0, tiled=True)  17.9 us
    dot_general x2, matrix products, shards(): t = jnp.einsum('swrn,swx->rnx', got, both, preferred_element_type=fp)  13.8 us
    convert_element_type x2, other arithmetic, dft_tables(): (-jnp.sin(phase) * factor).astype(jnp.bfloat16)  10.3 us
    ppermute x4, starting transfers between devices, from_partner(): return lax.ppermute(block, axis, route)  5.64 us
  transfers between devices with their start and end apart: 6, of which 5 were waited for; matrix products, arithmetic and copies ran while one was open for 13% of the time, Pallas kernels for 10%

profile of v14, /device:TPU:24, one launch (start us, length us, event | category | flops | bytes accessed | tf_op | source)
XLA Modules:
  0.0 234.6 jit_solution(3723594711723565620)
XLA Ops:
  0.6 2.0 collective-permute-start
  2.6 0.1 collective-permute-start.1
  2.7 3.0 %collective-permute-start.2 = (bf16[4,1,512,512]{3,2,1,0:T(8,128)(2,1)}, bf16[4,1,512,512]{3,2,1,0:T(8,128)(2,1)}, u32[]{:S(2)}, u32[]{:S(2)}) collective-permute-start(bf16[4,1,512,512]{3,2,1,0:T(8,128)(2,1)} %own_re.5), channel_id=1, source_target_pairs={{0,16},{16,0},{32,48},{48,32},{64,80},{80,64},{96,112},{112,96},{1... | collective-permute-start | bytes 6291464 | tf_op jit(solution)/shard_map/ppermute | solution.py:20
  5.8 0.5 collective-permute-start.3
  6.3 4.3 %fusion.23 = bf16[512,8,1,64]{0,3,2,1:T(8,128)(2,1)S(1)} fusion(s32[8,64]{1,0:T(8,128)S(1)} %multiply_add_fusion), kind=kLoop, calls=%fused_computation.46 | loop fusion | flops 5242880 | bytes 526336 | tf_op jit(solution)/shard_map/neg | solution.py:44
  10.6 4.9 %multiply_convert_fusion.2 = (bf16[512,8,1,64]{0,3,2,1:T(8,128)(2,1)S(1)}, bf16[512,8,1,64]{0,3,2,1:T(8,128)(2,1)S(1)}) fusion(s32[8,64]{1,0:T(8,128)S(1)} %multiply_add_fusion), kind=kLoop, calls=%fused_computation.27 | loop fusion | flops 4980736 | bytes 1050624 | tf_op jit(solution)/shard_map/convert_element_type | solution.py:30
  15.5 1.1 pad_maximum_fusion.1
  16.6 2.3 copy.15
  18.9 1.3 copy.16
  20.2 5.3 %multiply_convert_fusion = (bf16[512,512]{1,0:T(8,128)(2,1)}, bf16[512,512]{1,0:T(8,128)(2,1)}) fusion(), kind=kLoop, calls=%fused_computation.23 | loop fusion | flops 4980736 | bytes 1048576 | tf_op jit(solution)/shard_map/convert_element_type | solution.py:30
  25.5 0.0 copy-start.4
  25.5 3.1 %pad_maximum_fusion.col_a = bf16[1024,1024]{1,0:T(8,128)(2,1)} fusion(bf16[512,1024]{1,0:T(8,128)(2,1)} %copy.16, bf16[512,1024]{1,0:T(8,128)(2,1)} %copy.15), kind=kLoop, calls=%fused_computation.7 | loop fusion | flops 4194304 | bytes 4194304 | tf_op jit(solution)/shard_map/concatenate | solution.py:42
  28.6 0.0 copy-done.4
  28.6 0.5 slice_bitcast_fusion.4
  29.2 20.3 %collective-permute-done.far_re.rest_0_ = bf16[4,1,512,512]{3,2,1,0:T(8,128)(2,1)S(1)} collective-permute-done((bf16[4,1,512,512]{3,2,1,0:T(8,128)(2,1)}, bf16[4,1,512,512]{3,2,1,0:T(8,128)(2,1)S(1)}, u32[]{:S(2)}, u32[]{:S(2)}) %collective-permute-start) | collective-permute-done | bytes 2097184 | tf_op jit(solution)/shard_map/ppermute | solution.py:20
  49.4 0.0 copy-start.1
  49.4 44.1 %collective-permute-done.1.far_im.rest_1_ = bf16[4,1,512,512]{3,2,1,0:T(8,128)(2,1)} collective-permute-done((bf16[4,1,512,512]{3,2,1,0:T(8,128)(2,1)}, bf16[4,1,512,512]{3,2,1,0:T(8,128)(2,1)}, u32[]{:S(2)}, u32[]{:S(2)}) %collective-permute-start.1) | collective-permute-done | bytes 2097184 | tf_op jit(solution)/shard_map/ppermute | solution.py:20
  93.5 0.0 collective-permute-done.2.rest_0_.far_re
  93.5 3.1 %collective-permute-done.3.rest_1_.far_im = bf16[4,1,512,512]{3,2,1,0:T(8,128)(2,1)} collective-permute-done((bf16[4,1,512,512]{3,2,1,0:T(8,128)(2,1)}, bf16[4,1,512,512]{3,2,1,0:T(8,128)(2,1)}, u32[]{:S(2)}, u32[]{:S(2)}) %collective-permute-start.3) | collective-permute-done | bytes 2097184 | tf_op jit(solution)/shard_map/ppermute | solution.py:20
  96.6 0.0 copy-done.1
  96.6 9.6 %shard_map.68 = bf16[8,16,2,32,128]{4,3,2,1,0:T(8,128)(2,1)} custom-call(s32[4]{0:T(128)} %get-tuple-element.17.slot_ref, bf16[4,1,512,512]{3,2,1,0:T(8,128)(2,1)} %own_re.5, bf16[4,1,512,512]{3,2,1,0:T(8,128)(2,1)} %own_im.5, bf16[4,1,512,512]{3,2,1,0:T(8,128)(2,1)} %copy-done.1, bf16[4,1,512,512]{3,2,1,0:T(8,128)(2,1)} %collective-permute-done.1.far_im.rest_1_, ...), custom_call_target="tpu_custom_call" | custom-call | flops 4294967296 | bytes 9437184 | tf_op jit(solution)/shard_map/pallas_call | solution.py:87
  106.2 10.0 %all-to-all-start = ((bf16[128,2,32,128]{3,2,1,0:T(8,128)(2,1)}), bf16[128,2,32,128]{3,2,1,0:T(8,128)(2,1)S(1)}, u32[]{:S(2)}, u32[]{:S(2)}) async-start(bf16[128,2,32,128]{3,2,1,0:T(8,128)(2,1)} %bitcast.57), calls=%async_computation | async-start | bytes 4194304 | tf_op jit(solution)/shard_map/all_to_all | solution.py:163
  116.2 14.8 %shard_map.69.rest_2_ = bf16[8,16,6,32,128]{4,3,2,1,0:T(8,128)(2,1)} custom-call(s32[4]{0:T(128)} %get-tuple-element.16.slot_ref, bf16[4,1,512,512]{3,2,1,0:T(8,128)(2,1)} %own_re.5, bf16[4,1,512,512]{3,2,1,0:T(8,128)(2,1)} %own_im.5, bf16[4,1,512,512]{3,2,1,0:T(8,128)(2,1)} %collective-permute-done.2.rest_0_.far_re, ...), custom_call_target="tpu_custom_call" | custom-call | flops 8589934592 | bytes 15728640 | tf_op jit(solution)/shard_map/pallas_call | solution.py:87
  130.9 9.5 %shard_map.70 = bf16[8,16,6,32,128]{4,3,2,1,0:T(8,128)(2,1)} custom-call(s32[4]{0:T(128)} %get-tuple-element.17.slot_ref, bf16[4,1,512,512]{3,2,1,0:T(8,128)(2,1)} %own_re.5, bf16[4,1,512,512]{3,2,1,0:T(8,128)(2,1)} %own_im.5, bf16[4,1,512,512]{3,2,1,0:T(8,128)(2,1)} %copy-done.1, ...), custom_call_target="tpu_custom_call", output_to_operand_aliasing={{}: (10, {})} | custom-call | flops 4294967296 | bytes 9437184 | tf_op jit(solution)/shard_map/pallas_call | solution.py:87
  140.5 4.1 %all-to-all-done = bf16[128,2,32,128]{3,2,1,0:T(8,128)(2,1)S(1)} async-done(((bf16[128,2,32,128]{3,2,1,0:T(8,128)(2,1)}), bf16[128,2,32,128]{3,2,1,0:T(8,128)(2,1)S(1)}, u32[]{:S(2)}, u32[]{:S(2)}) %all-to-all-start) | async-done | bytes 2097184 | tf_op jit(solution)/shard_map/all_to_all | solution.py:163
  144.5 0.0 copy-start.2
  144.5 0.0 copy-start.3
  144.5 7.9 %all-to-all-start.1 = ((bf16[128,6,32,128]{3,2,1,0:T(8,128)(2,1)}), bf16[128,6,32,128]{3,2,1,0:T(8,128)(2,1)}, u32[]{:S(2)}, u32[]{:S(2)}) async-start(bf16[128,6,32,128]{3,2,1,0:T(8,128)(2,1)} %bitcast.56), calls=%async_computation.1 | async-start | bytes 12582912 | tf_op jit(solution)/shard_map/all_to_all | solution.py:163
  152.4 0.0 copy-done.2
  152.5 0.0 copy-done.3
  152.6 0.1 maximum_bitcast_fusion.2
  152.7 0.1 copy_bitcast_fusion
  152.9 6.5 %convolution_bitcast_fusion = f32[32,128,512]{2,1,0:T(8,128)} fusion(bf16[128,2,32,128]{3,2,1,0:T(8,128)(2,1)S(1)} %all-to-all-done, bf16[128,2,256]{2,0,1:T(8,128)(2,1)S(1)} %get-tuple-element.22, bf16[128,2,256]{2,0,1:T(8,128)(2,1)S(1)} %get-tuple-element.23), kind=kOutput, calls=%fused_computation.3 | convolution fusion | flops 1074266112 | bytes 10747904 | tf_op jit(solution)/shard_map/swrn,swx->rnx/dot_general | solution.py:170
  159.3 65.7 %all-to-all-done.1 = bf16[128,6,32,128]{3,2,1,0:T(8,128)(2,1)} async-done(((bf16[128,6,32,128]{3,2,1,0:T(8,128)(2,1)}), bf16[128,6,32,128]{3,2,1,0:T(8,128)(2,1)}, u32[]{:S(2)}, u32[]{:S(2)}) %all-to-all-start.1) | async-done | bytes 6291488 | tf_op jit(solution)/shard_map/all_to_all | solution.py:163
  225.0 0.0 copy-start
  225.0 7.4 %fusion.2 = f32[32,128,512]{2,1,0:T(8,128)S(1)} fusion(bf16[128,6,32,128]{3,2,1,0:T(8,128)(2,1)} %all-to-all-done.1, bf16[128,6,256]{2,0,1:T(8,128)(2,1)S(1)} %get-tuple-element.20, bf16[128,6,256]{2,0,1:T(8,128)(2,1)S(1)} %get-tuple-element.21), kind=kOutput, calls=%fused_computation.2 | convolution fusion | flops 3222798336 | bytes 15466496 | tf_op jit(solution)/shard_map/swrn,swx->rnx/dot_general | solution.py:170
  232.4 0.0 copy-done
  232.4 0.6 fusion.5
  233.0 1.6 fusion.26
  (9 shorter events, 0.2 us)
Async XLA Ops:
  0.6 48.8 %collective-permute-start = (bf16[4,1,512,512]{3,2,1,0:T(8,128)(2,1)}, bf16[4,1,512,512]{3,2,1,0:T(8,128)(2,1)S(1)}, u32[]{:S(2)}, u32[]{:S(2)}) collective-permute-start(bf16[4,1,512,512]{3,2,1,0:T(8,128)(2,1)} %own_re.5), channel_id=1, source_target_pairs={{0,32},{32,0},{16,48},{48,16},{64,96},{96,64},{80,112},{112,80},{1... | collective-permute-start | bytes 6291464 | tf_op jit(solution)/shard_map/ppermute | solution.py:20
  2.6 90.9 %collective-permute-start.1 = (bf16[4,1,512,512]{3,2,1,0:T(8,128)(2,1)}, bf16[4,1,512,512]{3,2,1,0:T(8,128)(2,1)}, u32[]{:S(2)}, u32[]{:S(2)}) collective-permute-start(bf16[4,1,512,512]{3,2,1,0:T(8,128)(2,1)} %own_im.5), channel_id=1, source_target_pairs={{0,32},{32,0},{16,48},{48,16},{64,96},{96,64},{80,112},{112,80},{1... | collective-permute-start | bytes 6291464 | tf_op jit(solution)/shard_map/ppermute | solution.py:20
  2.7 90.8 %collective-permute-start.2 = (bf16[4,1,512,512]{3,2,1,0:T(8,128)(2,1)}, bf16[4,1,512,512]{3,2,1,0:T(8,128)(2,1)}, u32[]{:S(2)}, u32[]{:S(2)}) collective-permute-start(bf16[4,1,512,512]{3,2,1,0:T(8,128)(2,1)} %own_re.5), channel_id=1, source_target_pairs={{0,16},{16,0},{32,48},{48,32},{64,80},{80,64},{96,112},{112,96},{1... | collective-permute-start | bytes 6291464 | tf_op jit(solution)/shard_map/ppermute | solution.py:20
  5.8 90.8 %collective-permute-start.3 = (bf16[4,1,512,512]{3,2,1,0:T(8,128)(2,1)}, bf16[4,1,512,512]{3,2,1,0:T(8,128)(2,1)}, u32[]{:S(2)}, u32[]{:S(2)}) collective-permute-start(bf16[4,1,512,512]{3,2,1,0:T(8,128)(2,1)} %own_im.5), channel_id=1, source_target_pairs={{0,16},{16,0},{32,48},{48,32},{64,80},{80,64},{96,112},{112,96},{1... | collective-permute-start | bytes 6291464 | tf_op jit(solution)/shard_map/ppermute | solution.py:20
  25.5 3.1 %copy-start.4 = (s32[2,4]{1,0:T(2,128)S(1)}, s32[2,4]{1,0:T(2,128)}, u32[]{:S(2)}) copy-start(s32[2,4]{1,0:T(2,128)} %param.7) | copy-start | bytes 100
  49.4 47.2 %copy-start.1 = (bf16[4,1,512,512]{3,2,1,0:T(8,128)(2,1)}, bf16[4,1,512,512]{3,2,1,0:T(8,128)(2,1)S(1)}, u32[]{:S(2)}) copy-start(bf16[4,1,512,512]{3,2,1,0:T(8,128)(2,1)S(1)} %collective-permute-done.far_re.rest_0_) | copy-start | bytes 6291460
  106.2 38.4 %all-to-all-start = ((bf16[128,2,32,128]{3,2,1,0:T(8,128)(2,1)}), bf16[128,2,32,128]{3,2,1,0:T(8,128)(2,1)S(1)}, u32[]{:S(2)}, u32[]{:S(2)}) async-start(bf16[128,2,32,128]{3,2,1,0:T(8,128)(2,1)} %bitcast.57), calls=%async_computation | async-start | bytes 4194304 | tf_op jit(solution)/shard_map/all_to_all | solution.py:163
  144.5 7.9 %copy-start.2 = (bf16[32,2,16,128]{3,2,1,0:T(8,128)(2,1)S(1)}, bf16[32,2,16,128]{3,2,1,0:T(8,128)(2,1)}, u32[]{:S(2)}) copy-start(bf16[32,2,16,128]{3,2,1,0:T(8,128)(2,1)} %param.9) | copy-start | bytes 786436
  144.5 7.9 %copy-start.3 = (bf16[32,2,16,128]{3,2,1,0:T(8,128)(2,1)S(1)}, bf16[32,2,16,128]{3,2,1,0:T(8,128)(2,1)}, u32[]{:S(2)}) copy-start(bf16[32,2,16,128]{3,2,1,0:T(8,128)(2,1)} %param.8) | copy-start | bytes 786436
  144.5 80.5 %all-to-all-start.1 = ((bf16[128,6,32,128]{3,2,1,0:T(8,128)(2,1)}), bf16[128,6,32,128]{3,2,1,0:T(8,128)(2,1)}, u32[]{:S(2)}, u32[]{:S(2)}) async-start(bf16[128,6,32,128]{3,2,1,0:T(8,128)(2,1)} %bitcast.56), calls=%async_computation.1 | async-start | bytes 12582912 | tf_op jit(solution)/shard_map/all_to_all | solution.py:163
  225.0 7.4 %copy-start = (f32[32,128,512]{2,1,0:T(8,128)S(1)}, f32[32,128,512]{2,1,0:T(8,128)}, u32[]{:S(2)}) copy-start(f32[32,128,512]{2,1,0:T(8,128)} %convolution_bitcast_fusion) | copy-start | bytes 25165828

commit v15 on v10

--- a/solution.py
+++ b/solution.py
@@ -140,7 +140,7 @@
             if lo >= hi:
                 continue
             got_real, got_imag = received[section_number]
-            after = [a for other, got in enumerate(received) if other != section_number for a in got]
+            after = [got[0] for other, got in enumerate(received) if other != section_number]
             send = spectra(
                 pair_slot[section_number],
                 hologram_real,

time: 239 us -> 237 us (level)
  waiting for transfers between devices: 137 us -> 142 us
  other arithmetic: 19.5 us -> 17 us
  local copies, waits for them, and re-layouts: 5.9 us -> 3.47 us
    ppermute x4, waiting for transfers between devices: 67.4 us -> 72.1 us  [from_partner(): return lax.ppermute(block, axis, route)]
  transfers between devices with their start and end apart: 6 -> 6, of which waited for: 5 -> 5; matrix products, arithmetic and copies ran while one was open for 13% -> 11% of each run, Pallas kernels for 10% -> 15%
where the time goes in v15:
time: 237 us; the launch traced here: 232 us
  waiting for transfers between devices  142 us (60%)
  Pallas kernels  33.8 us (14%)
  starting transfers between devices  21.7 us (9%)
  other arithmetic  17 us (7%)
  matrix products  13.9 us (6%)
  local copies, waits for them, and re-layouts  3.47 us (1%)
    ppermute x4, waiting for transfers between devices, from_partner(): return lax.ppermute(block, axis, route)  72.1 us
    all_to_all x2, waiting for transfers between devices, shards(): got = lax.all_to_all(send, ('wave', 'angle'), 0, 0, tiled=True)  69.8 us
    pallas_call x3, Pallas kernels, spectra(): pl.pallas_call(spectrum_kernel, out_shape=jax.ShapeDtypeStruct(shape, jnp...  33.8 us
    all_to_all x2, starting transfers between devices, shards(): got = lax.all_to_all(send, ('wave', 'angle'), 0, 0, tiled=True)  16.1 us
    dot_general x2, matrix products, shards(): t = jnp.einsum('swrn,swx->rnx', got, both, preferred_element_type=fp)  13.9 us
    convert_element_type x2, other arithmetic, dft_tables(): (-jnp.sin(phase) * factor).astype(jnp.bfloat16)  10.3 us
    ppermute x4, starting transfers between devices, from_partner(): return lax.ppermute(block, axis, route)  5.64 us
  transfers between devices with their start and end apart: 6, of which 5 were waited for; matrix products, arithmetic and copies ran while one was open for 11% of the time, Pallas kernels for 15%

profile of v15, /device:TPU:24, one launch (start us, length us, event | category | flops | bytes accessed | tf_op | source)
XLA Modules:
  0.0 232.5 jit_solution(3782089312588875279)
XLA Ops:
  0.6 3.1 %collective-permute-start.2 = (bf16[4,1,512,512]{3,2,1,0:T(8,128)(2,1)}, bf16[4,1,512,512]{3,2,1,0:T(8,128)(2,1)}, u32[]{:S(2)}, u32[]{:S(2)}) collective-permute-start(bf16[4,1,512,512]{3,2,1,0:T(8,128)(2,1)} %own_re.5), channel_id=1, source_target_pairs={{0,16},{16,0},{32,48},{48,32},{64,80},{80,64},{96,112},{112,96},{1... | collective-permute-start | bytes 6291464 | tf_op jit(solution)/shard_map/ppermute | solution.py:20
  3.7 1.9 collective-permute-start
  5.7 0.1 collective-permute-start.1
  5.8 0.5 collective-permute-start.3
  6.3 4.9 %multiply_convert_fusion.2 = (bf16[512,8,1,64]{0,3,2,1:T(8,128)(2,1)S(1)}, bf16[512,8,1,64]{0,3,2,1:T(8,128)(2,1)S(1)}) fusion(s32[8,64]{1,0:T(8,128)S(1)} %multiply_add_fusion), kind=kLoop, calls=%fused_computation.27 | loop fusion | flops 4980736 | bytes 1050624 | tf_op jit(solution)/shard_map/convert_element_type | solution.py:30
  11.2 4.3 %fusion.23 = bf16[512,8,1,64]{0,3,2,1:T(8,128)(2,1)S(1)} fusion(s32[8,64]{1,0:T(8,128)S(1)} %multiply_add_fusion), kind=kLoop, calls=%fused_computation.46 | loop fusion | flops 5242880 | bytes 526336 | tf_op jit(solution)/shard_map/neg | solution.py:44
  15.5 0.2 pad_maximum_fusion.1
  15.7 0.5 copy.15
  16.2 0.5 copy.16
  16.7 5.3 %multiply_convert_fusion = (bf16[512,512]{1,0:T(8,128)(2,1)}, bf16[512,512]{1,0:T(8,128)(2,1)}) fusion(), kind=kLoop, calls=%fused_computation.23 | loop fusion | flops 4980736 | bytes 1048576 | tf_op jit(solution)/shard_map/convert_element_type | solution.py:30
  22.1 0.0 copy-start.3
  22.1 1.5 pad_maximum_fusion.col_a
  23.6 0.0 copy-done.3
  23.6 0.6 slice_bitcast_fusion.4
  24.2 26.8 %collective-permute-done.2.rest_0_.far_re = bf16[4,1,512,512]{3,2,1,0:T(8,128)(2,1)} collective-permute-done((bf16[4,1,512,512]{3,2,1,0:T(8,128)(2,1)}, bf16[4,1,512,512]{3,2,1,0:T(8,128)(2,1)}, u32[]{:S(2)}, u32[]{:S(2)}) %collective-permute-start.2) | collective-permute-done | bytes 2097184 | tf_op jit(solution)/shard_map/ppermute | solution.py:20
  51.0 1.5 collective-permute-done.far_re.rest_0_
  52.6 43.7 %collective-permute-done.1.far_im = bf16[4,1,512,512]{3,2,1,0:T(8,128)(2,1)} collective-permute-done((bf16[4,1,512,512]{3,2,1,0:T(8,128)(2,1)}, bf16[4,1,512,512]{3,2,1,0:T(8,128)(2,1)}, u32[]{:S(2)}, u32[]{:S(2)}) %collective-permute-start.1) | collective-permute-done | bytes 2097184 | tf_op jit(solution)/shard_map/ppermute | solution.py:20
  96.3 9.5 %shard_map.68 = bf16[8,16,2,32,128]{4,3,2,1,0:T(8,128)(2,1)} custom-call(s32[4]{0:T(128)} %get-tuple-element.17.slot_ref, bf16[4,1,512,512]{3,2,1,0:T(8,128)(2,1)} %own_re.5, bf16[4,1,512,512]{3,2,1,0:T(8,128)(2,1)} %own_im.5, bf16[4,1,512,512]{3,2,1,0:T(8,128)(2,1)} %collective-permute-done.far_re.rest_0_, ...), custom_call_target="tpu_custom_call" | custom-call | flops 4294967296 | bytes 9437184 | tf_op jit(solution)/shard_map/pallas_call | solution.py:83
  105.8 8.2 %all-to-all-start = ((bf16[128,2,32,128]{3,2,1,0:T(8,128)(2,1)}), bf16[128,2,32,128]{3,2,1,0:T(8,128)(2,1)S(1)}, u32[]{:S(2)}, u32[]{:S(2)}) async-start(bf16[128,2,32,128]{3,2,1,0:T(8,128)(2,1)} %bitcast.59), calls=%async_computation | async-start | bytes 4194304 | tf_op jit(solution)/shard_map/all_to_all | solution.py:159
  114.0 0.0 collective-permute-done.3.far_im
  114.0 14.8 %shard_map.69.rest_1_ = bf16[8,16,6,32,128]{4,3,2,1,0:T(8,128)(2,1)} custom-call(s32[4]{0:T(128)} %get-tuple-element.16.slot_ref, bf16[4,1,512,512]{3,2,1,0:T(8,128)(2,1)} %own_re.5, bf16[4,1,512,512]{3,2,1,0:T(8,128)(2,1)} %own_im.5, bf16[4,1,512,512]{3,2,1,0:T(8,128)(2,1)} %collective-permute-done.2.rest_0_.far_re, ...), custom_call_target="tpu_custom_call" | custom-call | flops 8589934592 | bytes 15728640 | tf_op jit(solution)/shard_map/pallas_call | solution.py:83
  128.8 9.5 %shard_map.70 = bf16[8,16,6,32,128]{4,3,2,1,0:T(8,128)(2,1)} custom-call(s32[4]{0:T(128)} %get-tuple-element.17.slot_ref, bf16[4,1,512,512]{3,2,1,0:T(8,128)(2,1)} %own_re.5, bf16[4,1,512,512]{3,2,1,0:T(8,128)(2,1)} %own_im.5, bf16[4,1,512,512]{3,2,1,0:T(8,128)(2,1)} %collective-permute-done.far_re.rest_0_, ...), custom_call_target="tpu_custom_call", output_to_operand_aliasing={{}: (9, {})} | custom-call | flops 4294967296 | bytes 9437184 | tf_op jit(solution)/shard_map/pallas_call | solution.py:83
  138.3 4.1 %all-to-all-done = bf16[128,2,32,128]{3,2,1,0:T(8,128)(2,1)S(1)} async-done(((bf16[128,2,32,128]{3,2,1,0:T(8,128)(2,1)}), bf16[128,2,32,128]{3,2,1,0:T(8,128)(2,1)S(1)}, u32[]{:S(2)}, u32[]{:S(2)}) %all-to-all-start) | async-done | bytes 2097184 | tf_op jit(solution)/shard_map/all_to_all | solution.py:159
  142.3 0.0 copy-start.1
  142.3 0.0 copy-start.2
  142.3 7.9 %all-to-all-start.1 = ((bf16[128,6,32,128]{3,2,1,0:T(8,128)(2,1)}), bf16[128,6,32,128]{3,2,1,0:T(8,128)(2,1)}, u32[]{:S(2)}, u32[]{:S(2)}) async-start(bf16[128,6,32,128]{3,2,1,0:T(8,128)(2,1)} %bitcast.56), calls=%async_computation.1 | async-start | bytes 12582912 | tf_op jit(solution)/shard_map/all_to_all | solution.py:159
  150.2 0.0 copy-done.1
  150.3 0.0 copy-done.2
  150.5 0.1 maximum_bitcast_fusion.2
  150.6 0.1 copy_bitcast_fusion
  150.7 6.5 %convolution_bitcast_fusion = f32[32,128,512]{2,1,0:T(8,128)} fusion(bf16[128,2,32,128]{3,2,1,0:T(8,128)(2,1)S(1)} %all-to-all-done, bf16[128,2,256]{2,0,1:T(8,128)(2,1)S(1)} %get-tuple-element.22, bf16[128,2,256]{2,0,1:T(8,128)(2,1)S(1)} %get-tuple-element.23), kind=kOutput, calls=%fused_computation.3 | convolution fusion | flops 1074266112 | bytes 10747904 | tf_op jit(solution)/shard_map/swrn,swx->rnx/dot_general | solution.py:166
  157.1 65.7 %all-to-all-done.1 = bf16[128,6,32,128]{3,2,1,0:T(8,128)(2,1)} async-done(((bf16[128,6,32,128]{3,2,1,0:T(8,128)(2,1)}), bf16[128,6,32,128]{3,2,1,0:T(8,128)(2,1)}, u32[]{:S(2)}, u32[]{:S(2)}) %all-to-all-start.1) | async-done | bytes 6291488 | tf_op jit(solution)/shard_map/all_to_all | solution.py:159
  222.8 0.0 copy-start
  222.8 7.4 %fusion.2 = f32[32,128,512]{2,1,0:T(8,128)S(1)} fusion(bf16[128,6,32,128]{3,2,1,0:T(8,128)(2,1)} %all-to-all-done.1, bf16[128,6,256]{2,0,1:T(8,128)(2,1)S(1)} %get-tuple-element.20, bf16[128,6,256]{2,0,1:T(8,128)(2,1)S(1)} %get-tuple-element.21), kind=kOutput, calls=%fused_computation.2 | convolution fusion | flops 3222798336 | bytes 15466496 | tf_op jit(solution)/shard_map/swrn,swx->rnx/dot_general | solution.py:166
  230.3 0.0 copy-done
  230.3 0.6 fusion.5
  230.9 1.6 fusion.26
  (9 shorter events, 0.2 us)
Async XLA Ops:
  0.6 50.4 %collective-permute-start.2 = (bf16[4,1,512,512]{3,2,1,0:T(8,128)(2,1)}, bf16[4,1,512,512]{3,2,1,0:T(8,128)(2,1)}, u32[]{:S(2)}, u32[]{:S(2)}) collective-permute-start(bf16[4,1,512,512]{3,2,1,0:T(8,128)(2,1)} %own_re.5), channel_id=1, source_target_pairs={{0,16},{16,0},{32,48},{48,32},{64,80},{80,64},{96,112},{112,96},{1... | collective-permute-start | bytes 6291464 | tf_op jit(solution)/shard_map/ppermute | solution.py:20
  3.7 48.8 %collective-permute-start = (bf16[4,1,512,512]{3,2,1,0:T(8,128)(2,1)}, bf16[4,1,512,512]{3,2,1,0:T(8,128)(2,1)}, u32[]{:S(2)}, u32[]{:S(2)}) collective-permute-start(bf16[4,1,512,512]{3,2,1,0:T(8,128)(2,1)} %own_re.5), channel_id=1, source_target_pairs={{0,32},{32,0},{16,48},{48,16},{64,96},{96,64},{80,112},{112,80},{1... | collective-permute-start | bytes 6291464 | tf_op jit(solution)/shard_map/ppermute | solution.py:20
  5.7 90.6 %collective-permute-start.1 = (bf16[4,1,512,512]{3,2,1,0:T(8,128)(2,1)}, bf16[4,1,512,512]{3,2,1,0:T(8,128)(2,1)}, u32[]{:S(2)}, u32[]{:S(2)}) collective-permute-start(bf16[4,1,512,512]{3,2,1,0:T(8,128)(2,1)} %own_im.5), channel_id=1, source_target_pairs={{0,32},{32,0},{16,48},{48,16},{64,96},{96,64},{80,112},{112,80},{1... | collective-permute-start | bytes 6291464 | tf_op jit(solution)/shard_map/ppermute | solution.py:20
  5.8 108.2 %collective-permute-start.3 = (bf16[4,1,512,512]{3,2,1,0:T(8,128)(2,1)}, bf16[4,1,512,512]{3,2,1,0:T(8,128)(2,1)}, u32[]{:S(2)}, u32[]{:S(2)}) collective-permute-start(bf16[4,1,512,512]{3,2,1,0:T(8,128)(2,1)} %own_im.5), channel_id=1, source_target_pairs={{0,16},{16,0},{32,48},{48,32},{64,80},{80,64},{96,112},{112,96},{1... | collective-permute-start | bytes 6291464 | tf_op jit(solution)/shard_map/ppermute | solution.py:20
  22.1 1.5 copy-start.3
  105.8 36.5 %all-to-all-start = ((bf16[128,2,32,128]{3,2,1,0:T(8,128)(2,1)}), bf16[128,2,32,128]{3,2,1,0:T(8,128)(2,1)S(1)}, u32[]{:S(2)}, u32[]{:S(2)}) async-start(bf16[128,2,32,128]{3,2,1,0:T(8,128)(2,1)} %bitcast.59), calls=%async_computation | async-start | bytes 4194304 | tf_op jit(solution)/shard_map/all_to_all | solution.py:159
  142.3 7.9 %copy-start.1 = (bf16[32,2,16,128]{3,2,1,0:T(8,128)(2,1)S(1)}, bf16[32,2,16,128]{3,2,1,0:T(8,128)(2,1)}, u32[]{:S(2)}) copy-start(bf16[32,2,16,128]{3,2,1,0:T(8,128)(2,1)} %param.8) | copy-start | bytes 786436
  142.3 7.9 %copy-start.2 = (bf16[32,2,16,128]{3,2,1,0:T(8,128)(2,1)S(1)}, bf16[32,2,16,128]{3,2,1,0:T(8,128)(2,1)}, u32[]{:S(2)}) copy-start(bf16[32,2,16,128]{3,2,1,0:T(8,128)(2,1)} %param.9) | copy-start | bytes 786436
  142.3 80.5 %all-to-all-start.1 = ((bf16[128,6,32,128]{3,2,1,0:T(8,128)(2,1)}), bf16[128,6,32,128]{3,2,1,0:T(8,128)(2,1)}, u32[]{:S(2)}, u32[]{:S(2)}) async-start(bf16[128,6,32,128]{3,2,1,0:T(8,128)(2,1)} %bitcast.56), calls=%async_computation.1 | async-start | bytes 12582912 | tf_op jit(solution)/shard_map/all_to_all | solution.py:159
  222.8 7.4 %copy-start = (f32[32,128,512]{2,1,0:T(8,128)S(1)}, f32[32,128,512]{2,1,0:T(8,128)}, u32[]{:S(2)}) copy-start(f32[32,128,512]{2,1,0:T(8,128)} %convolution_bitcast_fusion) | copy-start | bytes 25165828

commit v16 on v15

--- a/solution.py
+++ b/solution.py
@@ -141,6 +141,7 @@
                 continue
             got_real, got_imag = received[section_number]
             after = [got[0] for other, got in enumerate(received) if other != section_number]
+            after = after if low == 0 else []
             send = spectra(
                 pair_slot[section_number],
                 hologram_real,

time: 237 us -> 236 us (level)
  waiting for transfers between devices: 142 us -> 139 us
    ppermute x4, waiting for transfers between devices: 72.1 us -> 69.3 us  [from_partner(): return lax.ppermute(block, axis, route)]
  transfers between devices with their start and end apart: 6 -> 6, of which waited for: 5 -> 4; matrix products, arithmetic and copies ran while one was open for 11% -> 11% of each run, Pallas kernels for 15% -> 15%
where the time goes in v16:
time: 236 us; the launch traced here: 232 us
  waiting for transfers between devices  139 us (59%)
  Pallas kernels  33.8 us (14%)
  starting transfers between devices  23.6 us (10%)
  other arithmetic  17 us (7%)
  matrix products  13.9 us (6%)
  local copies, waits for them, and re-layouts  3.47 us (1%)
    all_to_all x2, waiting for transfers between devices, shards(): got = lax.all_to_all(send, ('wave', 'angle'), 0, 0, tiled=True)  69.7 us
    ppermute x4, waiting for transfers between devices, from_partner(): return lax.ppermute(block, axis, route)  69.3 us
    pallas_call x3, Pallas kernels, spectra(): pl.pallas_call(spectrum_kernel, out_shape=jax.ShapeDtypeStruct(shape, jnp...  33.8 us
    all_to_all x2, starting transfers between devices, shards(): got = lax.all_to_all(send, ('wave', 'angle'), 0, 0, tiled=True)  18 us
    dot_general x2, matrix products, shards(): t = jnp.einsum('swrn,swx->rnx', got, both, preferred_element_type=fp)  13.9 us
    convert_element_type x2, other arithmetic, dft_tables(): (-jnp.sin(phase) * factor).astype(jnp.bfloat16)  10.3 us
    ppermute x4, starting transfers between devices, from_partner(): return lax.ppermute(block, axis, route)  5.64 us
  transfers between devices with their start and end apart: 6, of which 4 were waited for; matrix products, arithmetic and copies ran while one was open for 11% of the time, Pallas kernels for 15%

profile of v16, /device:TPU:24, one launch (start us, length us, event | category | flops | bytes accessed | tf_op | source)
XLA Modules:
  0.0 231.6 jit_solution(9673866209026930202)
XLA Ops:
  0.6 2.0 collective-permute-start
  2.6 0.1 collective-permute-start.1
  2.7 3.0 %collective-permute-start.2 = (bf16[4,1,512,512]{3,2,1,0:T(8,128)(2,1)}, bf16[4,1,512,512]{3,2,1,0:T(8,128)(2,1)}, u32[]{:S(2)}, u32[]{:S(2)}) collective-permute-start(bf16[4,1,512,512]{3,2,1,0:T(8,128)(2,1)} %own_re.5), channel_id=1, source_target_pairs={{0,16},{16,0},{32,48},{48,32},{64,80},{80,64},{96,112},{112,96},{1... | collective-permute-start | bytes 6291464 | tf_op jit(solution)/shard_map/ppermute | solution.py:20
  5.8 0.5 collective-permute-start.3
  6.3 4.9 %multiply_convert_fusion.2 = (bf16[512,8,1,64]{0,3,2,1:T(8,128)(2,1)S(1)}, bf16[512,8,1,64]{0,3,2,1:T(8,128)(2,1)S(1)}) fusion(s32[8,64]{1,0:T(8,128)S(1)} %multiply_add_fusion), kind=kLoop, calls=%fused_computation.27 | loop fusion | flops 4980736 | bytes 1050624 | tf_op jit(solution)/shard_map/convert_element_type | solution.py:30
  11.2 4.3 %fusion.23 = bf16[512,8,1,64]{0,3,2,1:T(8,128)(2,1)S(1)} fusion(s32[8,64]{1,0:T(8,128)S(1)} %multiply_add_fusion), kind=kLoop, calls=%fused_computation.46 | loop fusion | flops 5242880 | bytes 526336 | tf_op jit(solution)/shard_map/neg | solution.py:44
  15.5 0.2 pad_maximum_fusion.1
  15.7 0.5 copy.15
  16.2 0.5 copy.16
  16.7 5.3 %multiply_convert_fusion = (bf16[512,512]{1,0:T(8,128)(2,1)}, bf16[512,512]{1,0:T(8,128)(2,1)}) fusion(), kind=kLoop, calls=%fused_computation.23 | loop fusion | flops 4980736 | bytes 1048576 | tf_op jit(solution)/shard_map/convert_element_type | solution.py:30
  22.1 0.0 copy-start.3
  22.1 1.5 pad_maximum_fusion.col_a
  23.6 0.0 copy-done.3
  23.6 0.6 slice_bitcast_fusion.4
  24.2 25.3 %collective-permute-done.far_re.rest_0_ = bf16[4,1,512,512]{3,2,1,0:T(8,128)(2,1)} collective-permute-done((bf16[4,1,512,512]{3,2,1,0:T(8,128)(2,1)}, bf16[4,1,512,512]{3,2,1,0:T(8,128)(2,1)}, u32[]{:S(2)}, u32[]{:S(2)}) %collective-permute-start) | collective-permute-done | bytes 2097184 | tf_op jit(solution)/shard_map/ppermute | solution.py:20
  49.5 44.0 %collective-permute-done.1.far_im = bf16[4,1,512,512]{3,2,1,0:T(8,128)(2,1)} collective-permute-done((bf16[4,1,512,512]{3,2,1,0:T(8,128)(2,1)}, bf16[4,1,512,512]{3,2,1,0:T(8,128)(2,1)}, u32[]{:S(2)}, u32[]{:S(2)}) %collective-permute-start.1) | collective-permute-done | bytes 2097184 | tf_op jit(solution)/shard_map/ppermute | solution.py:20
  93.5 9.5 %shard_map.68 = bf16[8,16,2,32,128]{4,3,2,1,0:T(8,128)(2,1)} custom-call(s32[4]{0:T(128)} %get-tuple-element.17.slot_ref, bf16[4,1,512,512]{3,2,1,0:T(8,128)(2,1)} %own_re.5, bf16[4,1,512,512]{3,2,1,0:T(8,128)(2,1)} %own_im.5, bf16[4,1,512,512]{3,2,1,0:T(8,128)(2,1)} %collective-permute-done.far_re.rest_0_, ...), custom_call_target="tpu_custom_call" | custom-call | flops 4294967296 | bytes 9437184 | tf_op jit(solution)/shard_map/pallas_call | solution.py:83
  103.0 10.1 %all-to-all-start = ((bf16[128,2,32,128]{3,2,1,0:T(8,128)(2,1)}), bf16[128,2,32,128]{3,2,1,0:T(8,128)(2,1)S(1)}, u32[]{:S(2)}, u32[]{:S(2)}) async-start(bf16[128,2,32,128]{3,2,1,0:T(8,128)(2,1)} %bitcast.59), calls=%async_computation | async-start | bytes 4194304 | tf_op jit(solution)/shard_map/all_to_all | solution.py:160
  113.1 0.0 collective-permute-done.2.far_re.rest_0_
  113.1 0.0 collective-permute-done.3.far_im
  113.2 14.8 %shard_map.69.rest_1_ = bf16[8,16,6,32,128]{4,3,2,1,0:T(8,128)(2,1)} custom-call(s32[4]{0:T(128)} %get-tuple-element.16.slot_ref, bf16[4,1,512,512]{3,2,1,0:T(8,128)(2,1)} %own_re.5, bf16[4,1,512,512]{3,2,1,0:T(8,128)(2,1)} %own_im.5, bf16[4,1,512,512]{3,2,1,0:T(8,128)(2,1)} %collective-permute-done.2.far_re.rest_0_, ...), custom_call_target="tpu_custom_call" | custom-call | flops 8589934592 | bytes 15728640 | tf_op jit(solution)/shard_map/pallas_call | solution.py:83
  127.9 9.5 %shard_map.70 = bf16[8,16,6,32,128]{4,3,2,1,0:T(8,128)(2,1)} custom-call(s32[4]{0:T(128)} %get-tuple-element.17.slot_ref, bf16[4,1,512,512]{3,2,1,0:T(8,128)(2,1)} %own_re.5, bf16[4,1,512,512]{3,2,1,0:T(8,128)(2,1)} %own_im.5, bf16[4,1,512,512]{3,2,1,0:T(8,128)(2,1)} %collective-permute-done.far_re.rest_0_, ...), custom_call_target="tpu_custom_call", output_to_operand_aliasing={{}: (9, {})} | custom-call | flops 4294967296 | bytes 9437184 | tf_op jit(solution)/shard_map/pallas_call | solution.py:83
  137.4 4.0 %all-to-all-done = bf16[128,2,32,128]{3,2,1,0:T(8,128)(2,1)S(1)} async-done(((bf16[128,2,32,128]{3,2,1,0:T(8,128)(2,1)}), bf16[128,2,32,128]{3,2,1,0:T(8,128)(2,1)S(1)}, u32[]{:S(2)}, u32[]{:S(2)}) %all-to-all-start) | async-done | bytes 2097184 | tf_op jit(solution)/shard_map/all_to_all | solution.py:160
  141.5 0.0 copy-start.1
  141.5 0.0 copy-start.2
  141.5 7.9 %all-to-all-start.1 = ((bf16[128,6,32,128]{3,2,1,0:T(8,128)(2,1)}), bf16[128,6,32,128]{3,2,1,0:T(8,128)(2,1)}, u32[]{:S(2)}, u32[]{:S(2)}) async-start(bf16[128,6,32,128]{3,2,1,0:T(8,128)(2,1)} %bitcast.56), calls=%async_computation.1 | async-start | bytes 12582912 | tf_op jit(solution)/shard_map/all_to_all | solution.py:160
  149.4 0.0 copy-done.1
  149.4 0.0 copy-done.2
  149.6 0.1 maximum_bitcast_fusion.2
  149.7 0.1 copy_bitcast_fusion
  149.8 6.5 %convolution_bitcast_fusion = f32[32,128,512]{2,1,0:T(8,128)} fusion(bf16[128,2,32,128]{3,2,1,0:T(8,128)(2,1)S(1)} %all-to-all-done, bf16[128,2,256]{2,0,1:T(8,128)(2,1)S(1)} %get-tuple-element.22, bf16[128,2,256]{2,0,1:T(8,128)(2,1)S(1)} %get-tuple-element.23), kind=kOutput, calls=%fused_computation.3 | convolution fusion | flops 1074266112 | bytes 10747904 | tf_op jit(solution)/shard_map/swrn,swx->rnx/dot_general | solution.py:167
  156.3 65.7 %all-to-all-done.1 = bf16[128,6,32,128]{3,2,1,0:T(8,128)(2,1)} async-done(((bf16[128,6,32,128]{3,2,1,0:T(8,128)(2,1)}), bf16[128,6,32,128]{3,2,1,0:T(8,128)(2,1)}, u32[]{:S(2)}, u32[]{:S(2)}) %all-to-all-start.1) | async-done | bytes 6291488 | tf_op jit(solution)/shard_map/all_to_all | solution.py:160
  222.0 0.0 copy-start
  222.0 7.4 %fusion.2 = f32[32,128,512]{2,1,0:T(8,128)S(1)} fusion(bf16[128,6,32,128]{3,2,1,0:T(8,128)(2,1)} %all-to-all-done.1, bf16[128,6,256]{2,0,1:T(8,128)(2,1)S(1)} %get-tuple-element.20, bf16[128,6,256]{2,0,1:T(8,128)(2,1)S(1)} %get-tuple-element.21), kind=kOutput, calls=%fused_computation.2 | convolution fusion | flops 3222798336 | bytes 15466496 | tf_op jit(solution)/shard_map/swrn,swx->rnx/dot_general | solution.py:167
  229.4 0.0 copy-done
  229.4 0.6 fusion.5
  230.0 1.6 fusion.26
  (9 shorter events, 0.2 us)
Async XLA Ops:
  0.6 48.9 %collective-permute-start = (bf16[4,1,512,512]{3,2,1,0:T(8,128)(2,1)}, bf16[4,1,512,512]{3,2,1,0:T(8,128)(2,1)}, u32[]{:S(2)}, u32[]{:S(2)}) collective-permute-start(bf16[4,1,512,512]{3,2,1,0:T(8,128)(2,1)} %own_re.5), channel_id=1, source_target_pairs={{0,32},{32,0},{16,48},{48,16},{64,96},{96,64},{80,112},{112,80},{1... | collective-permute-start | bytes 6291464 | tf_op jit(solution)/shard_map/ppermute | solution.py:20
  2.6 90.9 %collective-permute-start.1 = (bf16[4,1,512,512]{3,2,1,0:T(8,128)(2,1)}, bf16[4,1,512,512]{3,2,1,0:T(8,128)(2,1)}, u32[]{:S(2)}, u32[]{:S(2)}) collective-permute-start(bf16[4,1,512,512]{3,2,1,0:T(8,128)(2,1)} %own_im.5), channel_id=1, source_target_pairs={{0,32},{32,0},{16,48},{48,16},{64,96},{96,64},{80,112},{112,80},{1... | collective-permute-start | bytes 6291464 | tf_op jit(solution)/shard_map/ppermute | solution.py:20
  2.7 110.4 %collective-permute-start.2 = (bf16[4,1,512,512]{3,2,1,0:T(8,128)(2,1)}, bf16[4,1,512,512]{3,2,1,0:T(8,128)(2,1)}, u32[]{:S(2)}, u32[]{:S(2)}) collective-permute-start(bf16[4,1,512,512]{3,2,1,0:T(8,128)(2,1)} %own_re.5), channel_id=1, source_target_pairs={{0,16},{16,0},{32,48},{48,32},{64,80},{80,64},{96,112},{112,96},{1... | collective-permute-start | bytes 6291464 | tf_op jit(solution)/shard_map/ppermute | solution.py:20
  5.8 107.4 %collective-permute-start.3 = (bf16[4,1,512,512]{3,2,1,0:T(8,128)(2,1)}, bf16[4,1,512,512]{3,2,1,0:T(8,128)(2,1)}, u32[]{:S(2)}, u32[]{:S(2)}) collective-permute-start(bf16[4,1,512,512]{3,2,1,0:T(8,128)(2,1)} %own_im.5), channel_id=1, source_target_pairs={{0,16},{16,0},{32,48},{48,32},{64,80},{80,64},{96,112},{112,96},{1... | collective-permute-start | bytes 6291464 | tf_op jit(solution)/shard_map/ppermute | solution.py:20
  22.1 1.5 copy-start.3
  103.0 38.4 %all-to-all-start = ((bf16[128,2,32,128]{3,2,1,0:T(8,128)(2,1)}), bf16[128,2,32,128]{3,2,1,0:T(8,128)(2,1)S(1)}, u32[]{:S(2)}, u32[]{:S(2)}) async-start(bf16[128,2,32,128]{3,2,1,0:T(8,128)(2,1)} %bitcast.59), calls=%async_computation | async-start | bytes 4194304 | tf_op jit(solution)/shard_map/all_to_all | solution.py:160
  141.5 7.9 %copy-start.1 = (bf16[32,2,16,128]{3,2,1,0:T(8,128)(2,1)S(1)}, bf16[32,2,16,128]{3,2,1,0:T(8,128)(2,1)}, u32[]{:S(2)}) copy-start(bf16[32,2,16,128]{3,2,1,0:T(8,128)(2,1)} %param.9) | copy-start | bytes 786436
  141.5 7.9 %copy-start.2 = (bf16[32,2,16,128]{3,2,1,0:T(8,128)(2,1)S(1)}, bf16[32,2,16,128]{3,2,1,0:T(8,128)(2,1)}, u32[]{:S(2)}) copy-start(bf16[32,2,16,128]{3,2,1,0:T(8,128)(2,1)} %param.8) | copy-start | bytes 786436
  141.5 80.5 %all-to-all-start.1 = ((bf16[128,6,32,128]{3,2,1,0:T(8,128)(2,1)}), bf16[128,6,32,128]{3,2,1,0:T(8,128)(2,1)}, u32[]{:S(2)}, u32[]{:S(2)}) async-start(bf16[128,6,32,128]{3,2,1,0:T(8,128)(2,1)} %bitcast.56), calls=%async_computation.1 | async-start | bytes 12582912 | tf_op jit(solution)/shard_map/all_to_all | solution.py:160
  222.0 7.4 %copy-start = (f32[32,128,512]{2,1,0:T(8,128)S(1)}, f32[32,128,512]{2,1,0:T(8,128)}, u32[]{:S(2)}) copy-start(f32[32,128,512]{2,1,0:T(8,128)} %convolution_bitcast_fusion) | copy-start | bytes 25165828
